TPU v7x, 512 devices: a whole 4x8x8 slice. The times are simulated.
512 devices in a mesh: grp: 4 (over x), gx: 16 (over z_hi, y), gy: 8 (over z_lo, core).
Axes of the slice: x: 4, y: 8, z: 8 (z_hi: 2, z_lo: 4; z = z_hi * 4 + z_lo), core: 2. Of those that a mesh axis runs over, the one named last changes fastest.
Arguments:
- fwd_now: float32 [3, 64, 64, 128], P(None, 'gx', 'gy'), may hold values from -6 to 6
- fwd_prev: float32 [3, 64, 64, 128], P(None, 'gx', 'gy'), may hold values from -6 to 6
- adj_now: float32 [16, 3, 64, 64, 128], P('grp', None, 'gx', 'gy'), may hold values from -6 to 6
- adj_prev: float32 [16, 3, 64, 64, 128], P('grp', None, 'gx', 'gy'), may hold values from -6 to 6
- lame_first: float32 [64, 64, 128], P('gx', 'gy'), may hold values from 0.5 to 2
- shear_mod: float32 [64, 64, 128], P('gx', 'gy'), may hold values from 0.3 to 1.2
- buoyancy: float32 [64, 64, 128], P('gx', 'gy'), may hold values from 0.5 to 1
- master_cell: int32 [1], replicated, may hold values from 0 to 524287
- master_lag: int32 [1], replicated, may hold values from 0 to 254
- master_trace: float32 [256, 3], replicated, may hold values from -96 to 96
- receiver_cell: int32 [16], P('grp'), may hold values from 0 to 524287
- receiver_lag: int32 [16], P('grp'), may hold values from 0 to 254
- receiver_trace: float32 [16, 256, 3], P('grp'), may hold values from -96 to 96
Outputs:
- adj_final: float32 [16, 3, 64, 64, 128], P('grp', None, 'gx', 'gy')
- kernels: float32 [2, 64, 64, 128], P(None, 'gx', 'gy', 'grp')
Inputs may be any that keep to these rules, and one draw needn't show every extreme that they name: `receiver_cell`: cell index in the whole grid, numbered (x * 64 + y) * 128 + z. `master_cell`: cell index in the whole grid, numbered (x * 64 + y) * 128 + z.
All inputs are finite; a program needn't handle non-finite values.
Results may differ from a plain program's by a relative error of at most 0.00011.
Values sent between devices are 32-bit elements; how exact they have to be, the bound alone decides.
No kernel may reach another device: no remote copies, remote signals or barrier semaphores. Data moves between devices by JAX's collectives and lax.ppermute only.
A program may use at most 64 MiB of HBM per device.

v0:
```python
import jax
import jax.numpy as jnp
from jax import lax
from jax.sharding import PartitionSpec as P

STEPS = 2


time_step_sq = 0.0625


def with_halo(cells, sides, width):
    for axis, dim in sides:
        count = lax.axis_size(axis)
        ends = count - 1
        head = lax.slice_in_dim(cells, 0, width, axis=dim)
        tail = lax.slice_in_dim(cells, cells.shape[dim] - width, cells.shape[dim], axis=dim)
        cells = jnp.concatenate(
            [
                lax.ppermute(tail, axis, [(i, (i + 1) % count) for i in range(ends)]),
                cells,
                lax.ppermute(head, axis, [((i + 1) % count, i) for i in range(ends)]),
            ],
            axis=dim,
        )
    return cells


def passed_along(value, axis, by):
    size = lax.axis_size(axis)
    pairs = [(i, i + by) for i in range(size) if 0 <= i + by < size]
    return lax.ppermute(value, axis, pairs)


def backward_diff(stress, axis):
    upper = stress[:, 1:, 1:, 1:]
    if axis == 1:
        lower = stress[:, :-1, 1:, 1:]
    elif axis == 2:
        lower = stress[:, 1:, :-1, 1:]
    else:
        lower = stress[:, 1:, 1:, :-1]
    return upper - lower


def stencil(padded, lame_pad, shear_pad):
    span_x = padded.shape[2] - 2
    span_y = padded.shape[3] - 2
    span_z = padded.shape[4] - 2
    anchor = padded[:, :, : span_x + 1, : span_y + 1, : span_z + 1]
    grad_x = padded[:, :, 1:, : span_y + 1, : span_z + 1] - anchor
    grad_y = padded[:, :, : span_x + 1, 1:, : span_z + 1] - anchor
    grad_z = padded[:, :, : span_x + 1, : span_y + 1, 1:] - anchor
    strain_xx = grad_x[:, 0]
    strain_yy = grad_y[:, 1]
    strain_zz = grad_z[:, 2]
    strain_xy = 0.5 * (grad_y[:, 0] + grad_x[:, 1])
    strain_xz = 0.5 * (grad_z[:, 0] + grad_x[:, 2])
    strain_yz = 0.5 * (grad_z[:, 1] + grad_y[:, 2])
    lame = lame_pad[: span_x + 1, : span_y + 1, : span_z + 1]
    shear = shear_pad[: span_x + 1, : span_y + 1, : span_z + 1]
    dilation = strain_xx + strain_yy + strain_zz
    stress_xx = lame * dilation + 2.0 * shear * strain_xx
    stress_yy = lame * dilation + 2.0 * shear * strain_yy
    stress_zz = lame * dilation + 2.0 * shear * strain_zz
    stress_xy = 2.0 * shear * strain_xy
    stress_xz = 2.0 * shear * strain_xz
    stress_yz = 2.0 * shear * strain_yz
    force_x = (
        backward_diff(stress_xx, 1) + backward_diff(stress_xy, 2) + backward_diff(stress_xz, 3)
    )
    force_y = (
        backward_diff(stress_xy, 1) + backward_diff(stress_yy, 2) + backward_diff(stress_yz, 3)
    )
    force_z = (
        backward_diff(stress_xz, 1) + backward_diff(stress_yz, 2) + backward_diff(stress_zz, 3)
    )
    force = jnp.stack([force_x, force_y, force_z], axis=1)
    strain = jnp.stack([strain_xx, strain_yy, strain_zz, strain_xy, strain_xz, strain_yz], axis=1)
    return (force, strain[:, :, 1:, 1:, 1:])


def faces(fields):
    count = fields.shape[0]
    flat = fields.reshape((count * 3,) + fields.shape[2:])
    grown = with_halo(flat, (("gx", 1), ("gy", 2)), 1)
    grown = jnp.pad(grown, ((0, 0), (0, 0), (0, 0), (1, 1)))
    return grown.reshape((count, 3) + grown.shape[1:])


def lower_rims(moduli):
    pairs, cells_x, cells_y, depth = moduli.shape
    from_x = passed_along(moduli[:, cells_x - 1 :], "gx", 1)
    from_y = passed_along(moduli[:, :, cells_y - 1 :], "gy", 1)
    corner = jnp.zeros((pairs, 1, 1, depth), jnp.float32)
    top_row = jnp.concatenate([corner, from_y], axis=1)
    rest = jnp.concatenate([from_x, moduli], axis=1)
    grown = jnp.concatenate([top_row, rest], axis=2)
    return jnp.pad(grown, ((0, 0), (0, 1), (0, 1), (1, 1)))


def locate(cells, start_x, start_y, start_z, width_y, depth, span_x, span_y, span_z):
    coord_x = cells // (width_y * depth) - start_x
    coord_y = cells // depth % width_y - start_y
    coord_z = cells % depth - start_z
    index_x = lax.broadcasted_iota(jnp.int32, (1, span_x, 1, 1), 1)
    index_y = lax.broadcasted_iota(jnp.int32, (1, 1, span_y, 1), 2)
    index_z = lax.broadcasted_iota(jnp.int32, (1, 1, 1, span_z), 3)
    found = (
        (index_x == coord_x[:, None, None, None])
        & (index_y == coord_y[:, None, None, None])
        & (index_z == coord_z[:, None, None, None])
    )
    return found.astype(jnp.float32)


def pick(trace, lags):
    positions = lax.broadcasted_iota(jnp.int32, (1, trace.shape[1]), 1)
    chosen = positions == lags[:, None]
    return jnp.sum(jnp.where(chosen[:, :, None], trace, 0.0), axis=1)


def advance(current, earlier, force, amplitudes, masks, buoyancy):
    source = amplitudes[:, :, None, None, None] * masks[:, None]
    return 2.0 * current - earlier + time_step_sq * buoyancy * (force + source)


def correlate(master, strains, totals):
    weights = jnp.array([1.0, 1.0, 1.0, 2.0, 2.0, 2.0], jnp.float32)[:, None, None, None]
    summed = jnp.sum(strains, axis=0)
    dilation_term = (master[0] + master[1] + master[2]) * (summed[0] + summed[1] + summed[2])
    shear_term = 2.0 * jnp.sum(weights * master * summed, axis=0)
    return totals + jnp.stack([dilation_term, shear_term])


def local(
    fwd_now,
    fwd_prev,
    adj_now,
    adj_prev,
    lame_first,
    shear_mod,
    buoyancy,
    master_cell,
    master_lag,
    master_trace,
    receiver_cell,
    receiver_lag,
    receiver_trace,
):
    cells_x, cells_y, depth = lame_first.shape
    groups = lax.axis_size("grp")
    receivers = adj_now.shape[0]
    width_y = cells_y * lax.axis_size("gy")
    start_x = lax.axis_index("gx") * cells_x
    start_y = lax.axis_index("gy") * cells_y
    moduli = lower_rims(jnp.stack([lame_first, shear_mod]))
    lame_pad = moduli[0]
    shear_pad = moduli[1]
    receiver_masks = locate(
        receiver_cell, start_x, start_y, 0, width_y, depth, cells_x, cells_y, depth
    )
    receiver_amps = [pick(receiver_trace, receiver_lag + instant) for instant in range(STEPS)]
    master_amps = [pick(master_trace[None], master_lag + instant) for instant in range(STEPS)]
    totals = jnp.zeros((2, cells_x, cells_y, depth), jnp.float32)
    share = depth // groups
    z_start = lax.axis_index("grp") * share
    master_now = lax.dynamic_slice_in_dim(fwd_now, z_start, share, 3)
    master_prev = lax.dynamic_slice_in_dim(fwd_prev, z_start, share, 3)
    lame_share = lax.dynamic_slice_in_dim(lame_pad, z_start, share + 2, 2)
    shear_share = lax.dynamic_slice_in_dim(shear_pad, z_start, share + 2, 2)
    buoyancy_share = lax.dynamic_slice_in_dim(buoyancy, z_start, share, 2)
    master_mask = locate(
        master_cell, start_x, start_y, z_start, width_y, depth, cells_x, cells_y, share
    )
    adjoint = adj_now
    adjoint_prev = adj_prev
    for instant in range(STEPS):
        grown = with_halo(master_now, (("grp", 3), ("gx", 1), ("gy", 2)), 1)
        master_force, master_strain = stencil(grown[None], lame_share, shear_share)
        master_whole = lax.all_gather(master_strain[0], "grp", axis=3, tiled=True)
        if instant + 1 < STEPS:
            master_next = advance(
                master_now[None],
                master_prev[None],
                master_force,
                master_amps[instant],
                master_mask,
                buoyancy_share,
            )[0]
            master_prev, master_now = (master_now, master_next)
        padded = faces(adjoint)
        force, strain = stencil(padded, lame_pad, shear_pad)
        totals = correlate(master_whole, strain, totals)
        adjoint_next = advance(
            adjoint, adjoint_prev, force, receiver_amps[instant], receiver_masks, buoyancy
        )
        adjoint_prev, adjoint = (adjoint, adjoint_next)
    scale_out = 1.0 / (STEPS * receivers * groups)
    kernels = lax.psum_scatter(totals * scale_out, "grp", scatter_dimension=3, tiled=True)
    return (adjoint, kernels)


def solution(mesh):
    in_specs = (
        P(None, "gx", "gy", None),
        P(None, "gx", "gy", None),
        P("grp", None, "gx", "gy", None),
        P("grp", None, "gx", "gy", None),
        P("gx", "gy", None),
        P("gx", "gy", None),
        P("gx", "gy", None),
        P(),
        P(),
        P(),
        P("grp"),
        P("grp"),
        P("grp", None, None),
    )
    out_specs = (P("grp", None, "gx", "gy", None), P(None, "gx", "gy", "grp"))
    return jax.shard_map(local, mesh=mesh, in_specs=in_specs, out_specs=out_specs, check_vma=False)
```

profile of v0, /device:TPU:8, one launch (start us, length us, event | category | flops | bytes accessed | tf_op | source)
XLA Modules:
  0.0 201.1 jit_solution(10094206814735372614)
XLA Ops:
  8.0 1.7 collective-permute-start
  9.7 3.5 %collective-permute-start.1 = (f32[2,1,8,128]{3,1,2,0:T(1,128)S(1)}, f32[2,1,8,128]{3,1,2,0:T(1,128)S(1)}, u32[]{:S(2)}, u32[]{:S(2)}) collective-permute-start(f32[2,1,8,128]{3,1,2,0:T(1,128)S(1)} %pad_maximum_fusion.14), channel_id=1, source_target_pairs={{0,8},{8,16},{16,24},{24,32},{32,40},{40,48},{48,56},{56,64},{64,7... | collective-permute-start | bytes 24584 | tf_op jit(solution)/shard_map/ppermute | solution.py:32
  14.2 3.4 %collective-permute-start.10 = (f32[3,4,8,1]{3,2,1,0:T(8,128)S(1)}, f32[3,4,8,1]{3,2,1,0:T(8,128)S(1)}, u32[]{:S(2)}, u32[]{:S(2)}) collective-permute-start(f32[3,4,8,1]{3,2,1,0:T(8,128)S(1)} %get-tuple-element.92), channel_id=1, source_target_pairs={{0,128},{128,256},{256,384},{1,129},{129,257},{257,385},{2,130},{1... | collective-permute-start | bytes 1160 | tf_op jit(solution)/shard_map/ppermute | solution.py:20
  17.6 1.3 collective-permute-start.11
  20.0 3.5 %collective-permute-start.2 = (f32[12,1,8,128]{3,1,2,0:T(1,128)S(1)}, f32[12,1,8,128]{3,1,2,0:T(1,128)S(1)}, u32[]{:S(2)}, u32[]{:S(2)}) collective-permute-start(f32[12,1,8,128]{3,1,2,0:T(1,128)S(1)} %get-tuple-element.66), channel_id=1, source_target_pairs={{0,8},{8,16},{16,24},{24,32},{32,40},{40,48},{48,56},{56,64},{64,7... | collective-permute-start | bytes 147464 | tf_op jit(solution)/shard_map/ppermute | solution.py:20
  30.8 4.7 %collective-permute-start.12 = (f32[3,1,8,34]{3,2,1,0:T(8,128)S(1)}, f32[3,1,8,34]{3,2,1,0:T(8,128)S(1)}, u32[]{:S(2)}, u32[]{:S(2)}) collective-permute-start(f32[3,1,8,34]{3,2,1,0:T(8,128)S(1)} %get-tuple-element.70), channel_id=1, source_target_pairs={{0,8},{8,16},{16,24},{24,32},{32,40},{40,48},{48,56},{56,64},{64,7... | collective-permute-start | bytes 9800 | tf_op jit(solution)/shard_map/ppermute | solution.py:20
  35.5 1.9 collective-permute-start.13
  37.4 3.6 %collective-permute-done.13 = f32[3,1,8,34]{3,2,1,0:T(8,128)S(1)} collective-permute-done((f32[3,1,8,34]{3,2,1,0:T(8,128)S(1)}, f32[3,1,8,34]{3,2,1,0:T(8,128)S(1)}, u32[]{:S(2)}, u32[]{:S(2)}) %collective-permute-start.13) | collective-permute-done | bytes 3296 | tf_op jit(solution)/shard_map/ppermute | solution.py:22
  41.2 2.4 %collective-permute-start.14 = (f32[3,6,1,34]{3,1,2,0:T(8,128)S(1)}, f32[3,6,1,34]{3,1,2,0:T(8,128)S(1)}, u32[]{:S(2)}, u32[]{:S(2)}) collective-permute-start(f32[3,6,1,34]{3,1,2,0:T(8,128)S(1)} %get-tuple-element.80), channel_id=1, source_target_pairs={{0,1},{1,2},{2,3},{3,4},{4,5},{5,6},{6,7},{8,9},{9,10},{10,11},{11... | collective-permute-start | bytes 7352 | tf_op jit(solution)/shard_map/ppermute | solution.py:20
  43.7 1.3 collective-permute-start.15
  45.1 2.2 %collective-permute-start.3 = (f32[12,1,8,128]{3,1,2,0:T(1,128)S(1)}, f32[12,1,8,128]{3,1,2,0:T(1,128)S(1)}, u32[]{:S(2)}, u32[]{:S(2)}) collective-permute-start(f32[12,1,8,128]{3,1,2,0:T(1,128)S(1)} %get-tuple-element.67), channel_id=1, source_target_pairs={{8,0},{16,8},{24,16},{32,24},{40,32},{48,40},{56,48},{64,56},{72,6... | collective-permute-start | bytes 147464 | tf_op jit(solution)/shard_map/ppermute | solution.py:22
  49.6 4.6 %collective-permute-start.16 = (f32[3,4,8,1]{3,2,1,0:T(8,128)S(1)}, f32[3,4,8,1]{3,2,1,0:T(8,128)S(1)}, u32[]{:S(2)}, u32[]{:S(2)}) collective-permute-start(f32[3,4,8,1]{3,2,1,0:T(8,128)S(1)} %get-tuple-element.90), channel_id=1, source_target_pairs={{0,128},{128,256},{256,384},{1,129},{129,257},{257,385},{2,130},{1... | collective-permute-start | bytes 1160 | tf_op jit(solution)/shard_map/ppermute | solution.py:20
  54.1 1.3 collective-permute-start.17
  55.9 4.3 %collective-permute-done.17 = f32[3,4,8,1]{3,2,1,0:T(8,128)S(1)} collective-permute-done((f32[3,4,8,1]{3,2,1,0:T(8,128)S(1)}, f32[3,4,8,1]{3,2,1,0:T(8,128)S(1)}, u32[]{:S(2)}, u32[]{:S(2)}) %collective-permute-start.17) | collective-permute-done | bytes 416 | tf_op jit(solution)/shard_map/ppermute | solution.py:22
  60.2 2.6 %collective-permute-start.18 = (f32[3,1,8,34]{3,2,1,0:T(8,128)S(1)}, f32[3,1,8,34]{3,2,1,0:T(8,128)S(1)}, u32[]{:S(2)}, u32[]{:S(2)}) collective-permute-start(f32[3,1,8,34]{3,2,1,0:T(8,128)S(1)} %get-tuple-element.68), channel_id=1, source_target_pairs={{0,8},{8,16},{16,24},{24,32},{32,40},{40,48},{48,56},{56,64},{64,7... | collective-permute-start | bytes 9800 | tf_op jit(solution)/shard_map/ppermute | solution.py:20
  62.8 3.3 %collective-permute-start.19 = (f32[3,1,8,34]{3,2,1,0:T(8,128)S(1)}, f32[3,1,8,34]{3,2,1,0:T(8,128)S(1)}, u32[]{:S(2)}, u32[]{:S(2)}) collective-permute-start(f32[3,1,8,34]{3,2,1,0:T(8,128)S(1)} %get-tuple-element.69), channel_id=1, source_target_pairs={{8,0},{16,8},{24,16},{32,24},{40,32},{48,40},{56,48},{64,56},{72,6... | collective-permute-start | bytes 9800 | tf_op jit(solution)/shard_map/ppermute | solution.py:22
  66.1 17.6 %all-gather = f32[1,6,4,8,128]{3,2,1,0,4:T(4,128)S(1)} all-gather(f32[1,6,4,8,32]{3,2,1,0,4:T(4,128)S(1)} %copy.434), channel_id=2, replica_groups=mesh['grp'=4,'gx'=16,'gy'=8] {'grp'}, dimensions={4}, use_global_device_ids=true | all-gather | bytes 122880 | tf_op jit(solution)/shard_map/all_gather | solution.py:181
  84.4 1.5 collective-permute-start.20
  85.9 1.3 collective-permute-start.21
  87.3 5.0 %collective-permute-done.21 = f32[3,6,1,34]{3,1,2,0:T(8,128)S(1)} collective-permute-done((f32[3,6,1,34]{3,1,2,0:T(8,128)S(1)}, f32[3,6,1,34]{3,1,2,0:T(8,128)S(1)}, u32[]{:S(2)}, u32[]{:S(2)}) %collective-permute-start.21) | collective-permute-done | bytes 2480 | tf_op jit(solution)/shard_map/ppermute | solution.py:22
  92.9 4.3 %collective-permute-start.4 = (f32[12,6,1,128]{3,1,2,0:T(8,128)S(1)}, f32[12,6,1,128]{3,1,2,0:T(8,128)S(1)}, u32[]{:S(2)}, u32[]{:S(2)}) collective-permute-start(f32[12,6,1,128]{3,1,2,0:T(8,128)S(1)} %get-tuple-element.59), channel_id=1, source_target_pairs={{0,1},{1,2},{2,3},{3,4},{4,5},{5,6},{6,7},{8,9},{9,10},{10,11},{11... | collective-permute-start | bytes 110600 | tf_op jit(solution)/shard_map/ppermute | solution.py:20
  97.3 1.3 collective-permute-start.5
  98.6 18.0 %all-gather.1 = f32[1,6,4,8,128]{3,2,1,0,4:T(4,128)S(1)} all-gather(f32[1,6,4,8,32]{3,2,1,0,4:T(4,128)S(1)} %copy.451), channel_id=3, replica_groups=mesh['grp'=4,'gx'=16,'gy'=8] {'grp'}, dimensions={4}, use_global_device_ids=true | all-gather | bytes 122880 | tf_op jit(solution)/shard_map/all_gather | solution.py:181
  116.6 1.2 copy.452
  120.7 3.5 %collective-permute-start.6 = (f32[12,1,8,128]{3,2,1,0:T(8,128)S(1)}, f32[12,1,8,128]{3,2,1,0:T(8,128)S(1)}, u32[]{:S(2)}, u32[]{:S(2)}) collective-permute-start(f32[12,1,8,128]{3,2,1,0:T(8,128)S(1)} %get-tuple-element.64), channel_id=1, source_target_pairs={{0,8},{8,16},{16,24},{24,32},{32,40},{40,48},{48,56},{56,64},{64,7... | collective-permute-start | bytes 147464 | tf_op jit(solution)/shard_map/ppermute | solution.py:20
  124.2 2.4 %collective-permute-start.7 = (f32[12,1,8,128]{3,2,1,0:T(8,128)S(1)}, f32[12,1,8,128]{3,2,1,0:T(8,128)S(1)}, u32[]{:S(2)}, u32[]{:S(2)}) collective-permute-start(f32[12,1,8,128]{3,2,1,0:T(8,128)S(1)} %get-tuple-element.65), channel_id=1, source_target_pairs={{8,0},{16,8},{24,16},{32,24},{40,32},{48,40},{56,48},{64,56},{72,6... | collective-permute-start | bytes 147464 | tf_op jit(solution)/shard_map/ppermute | solution.py:22
  127.2 4.8 %collective-permute-done.7 = f32[12,1,8,128]{3,2,1,0:T(8,128)S(1)} collective-permute-done((f32[12,1,8,128]{3,2,1,0:T(8,128)S(1)}, f32[12,1,8,128]{3,2,1,0:T(8,128)S(1)}, u32[]{:S(2)}, u32[]{:S(2)}) %collective-permute-start.7) | collective-permute-done | bytes 49184 | tf_op jit(solution)/shard_map/ppermute | solution.py:22
  132.0 1.3 collective-permute-start.8
  133.3 1.5 collective-permute-start.9
  134.8 3.6 %collective-permute-done.9 = f32[12,6,1,128]{3,2,1,0:T(1,128)S(1)} collective-permute-done((f32[12,6,1,128]{3,2,1,0:T(1,128)S(1)}, f32[12,6,1,128]{3,2,1,0:T(1,128)S(1)}, u32[]{:S(2)}, u32[]{:S(2)}) %collective-permute-start.9) | collective-permute-done | bytes 36896 | tf_op jit(solution)/shard_map/ppermute | solution.py:22
  139.7 2.0 %copy_subtract_fusion.1 = (f32[4,3,5,9,129]{4,2,3,0,1:T(8,128)S(1)}, f32[4,3,5,9,129]{4,2,3,0,1:T(8,128)S(1)}, f32[4,3,5,9,129]{4,2,3,0,1:T(8,128)S(1)}) fusion(f32[4,3,5,9,129]{4,3,2,1,0:T(8,128)S(1)} %get-tuple-element.34, f32[4,3,5,9,129]{4,3,2,1,0:T(8,128)S(1)} %get-tuple-element.35, f32[4,3,5,9,129]{4,3,2,1,0:T(8,128)S(1)} %get-tuple-element.37, ...), kind=kLoop, calls=%fused_computation.16 | loop fusion | flops 208980 | bytes 1950480 | tf_op jit(solution)/shard_map/sub | solution.py:52
  145.8 46.9 %reduce-scatter.4.cloned.1.call-done = f32[32,64]{1,0:T(8,128)} async-done(((f32[128,64]{1,0:T(8,128)}), f32[32,64]{1,0:T(8,128)}) %reduce-scatter.4.cloned.1.call-update) | async-done | bytes 8208
  (148 shorter events, 23.0 us)
Async XLA Ops:
  7.2 37.8 %copy-start.7 = (f32[256,3]{0,1:T(4,128)S(1)}, f32[256,3]{0,1:T(4,128)}, u32[]{:S(2)}) copy-start(f32[256,3]{0,1:T(4,128)} %param.24) | copy-start | bytes 9220
  7.2 185.5 %reduce-scatter.4.cloned.1.call-start = ((), (), s32[]{:S(2)}) async-start(), calls=%async_computation.1 | async-start | bytes 81920
  8.0 40.8 %collective-permute-start = (f32[2,4,1,128]{3,1,2,0:T(4,128)S(1)}, f32[2,4,1,128]{3,1,2,0:T(4,128)S(1)}, u32[]{:S(2)}, u32[]{:S(2)}) collective-permute-start(f32[2,4,1,128]{3,1,2,0:T(4,128)S(1)} %pad_maximum_fusion.15), channel_id=1, source_target_pairs={{0,1},{1,2},{2,3},{3,4},{4,5},{5,6},{6,7},{8,9},{9,10},{10,11},{11... | collective-permute-start | bytes 12296 | tf_op jit(solution)/shard_map/ppermute | solution.py:32
  9.7 39.0 %collective-permute-start.1 = (f32[2,1,8,128]{3,1,2,0:T(1,128)S(1)}, f32[2,1,8,128]{3,1,2,0:T(1,128)S(1)}, u32[]{:S(2)}, u32[]{:S(2)}) collective-permute-start(f32[2,1,8,128]{3,1,2,0:T(1,128)S(1)} %pad_maximum_fusion.14), channel_id=1, source_target_pairs={{0,8},{8,16},{16,24},{24,32},{32,40},{40,48},{48,56},{56,64},{64,7... | collective-permute-start | bytes 24584 | tf_op jit(solution)/shard_map/ppermute | solution.py:32
  14.2 16.5 %collective-permute-start.10 = (f32[3,4,8,1]{3,2,1,0:T(8,128)S(1)}, f32[3,4,8,1]{3,2,1,0:T(8,128)S(1)}, u32[]{:S(2)}, u32[]{:S(2)}) collective-permute-start(f32[3,4,8,1]{3,2,1,0:T(8,128)S(1)} %get-tuple-element.92), channel_id=1, source_target_pairs={{0,128},{128,256},{256,384},{1,129},{129,257},{257,385},{2,130},{1... | collective-permute-start | bytes 1160 | tf_op jit(solution)/shard_map/ppermute | solution.py:20
  17.6 13.1 %collective-permute-start.11 = (f32[3,4,8,1]{3,2,1,0:T(8,128)S(1)}, f32[3,4,8,1]{3,2,1,0:T(8,128)S(1)}, u32[]{:S(2)}, u32[]{:S(2)}) collective-permute-start(f32[3,4,8,1]{3,2,1,0:T(8,128)S(1)} %get-tuple-element.93), channel_id=1, source_target_pairs={{128,0},{256,128},{384,256},{129,1},{257,129},{385,257},{130,2},{2... | collective-permute-start | bytes 1160 | tf_op jit(solution)/shard_map/ppermute | solution.py:22
  20.0 72.9 %collective-permute-start.2 = (f32[12,1,8,128]{3,1,2,0:T(1,128)S(1)}, f32[12,1,8,128]{3,1,2,0:T(1,128)S(1)}, u32[]{:S(2)}, u32[]{:S(2)}) collective-permute-start(f32[12,1,8,128]{3,1,2,0:T(1,128)S(1)} %get-tuple-element.66), channel_id=1, source_target_pairs={{0,8},{8,16},{16,24},{24,32},{32,40},{40,48},{48,56},{56,64},{64,7... | collective-permute-start | bytes 147464 | tf_op jit(solution)/shard_map/ppermute | solution.py:20
  30.8 6.6 %collective-permute-start.12 = (f32[3,1,8,34]{3,2,1,0:T(8,128)S(1)}, f32[3,1,8,34]{3,2,1,0:T(8,128)S(1)}, u32[]{:S(2)}, u32[]{:S(2)}) collective-permute-start(f32[3,1,8,34]{3,2,1,0:T(8,128)S(1)} %get-tuple-element.70), channel_id=1, source_target_pairs={{0,8},{8,16},{16,24},{24,32},{32,40},{40,48},{48,56},{56,64},{64,7... | collective-permute-start | bytes 9800 | tf_op jit(solution)/shard_map/ppermute | solution.py:20
  35.5 5.6 %collective-permute-start.13 = (f32[3,1,8,34]{3,2,1,0:T(8,128)S(1)}, f32[3,1,8,34]{3,2,1,0:T(8,128)S(1)}, u32[]{:S(2)}, u32[]{:S(2)}) collective-permute-start(f32[3,1,8,34]{3,2,1,0:T(8,128)S(1)} %get-tuple-element.71), channel_id=1, source_target_pairs={{8,0},{16,8},{24,16},{32,24},{40,32},{48,40},{56,48},{64,56},{72,6... | collective-permute-start | bytes 9800 | tf_op jit(solution)/shard_map/ppermute | solution.py:22
  41.2 8.2 %copy-start.1 = (f32[3,4,8,128]{3,2,1,0:T(8,128)S(1)}, f32[3,4,8,128]{3,2,1,0:T(8,128)}, u32[]{:S(2)}) copy-start(f32[3,4,8,128]{3,2,1,0:T(8,128)} %param.15) | copy-start | bytes 147460
  41.2 8.2 %copy-start.6 = (f32[3,4,8,128]{3,2,1,0:T(8,128)S(1)}, f32[3,4,8,128]{3,2,1,0:T(8,128)}, u32[]{:S(2)}) copy-start(f32[3,4,8,128]{3,2,1,0:T(8,128)} %param.16) | copy-start | bytes 147460
  41.2 3.9 %collective-permute-start.14 = (f32[3,6,1,34]{3,1,2,0:T(8,128)S(1)}, f32[3,6,1,34]{3,1,2,0:T(8,128)S(1)}, u32[]{:S(2)}, u32[]{:S(2)}) collective-permute-start(f32[3,6,1,34]{3,1,2,0:T(8,128)S(1)} %get-tuple-element.80), channel_id=1, source_target_pairs={{0,1},{1,2},{2,3},{3,4},{4,5},{5,6},{6,7},{8,9},{9,10},{10,11},{11... | collective-permute-start | bytes 7352 | tf_op jit(solution)/shard_map/ppermute | solution.py:20
  43.7 4.9 %collective-permute-start.15 = (f32[3,6,1,34]{3,1,2,0:T(8,128)S(1)}, f32[3,6,1,34]{3,1,2,0:T(8,128)S(1)}, u32[]{:S(2)}, u32[]{:S(2)}) collective-permute-start(f32[3,6,1,34]{3,1,2,0:T(8,128)S(1)} %get-tuple-element.81), channel_id=1, source_target_pairs={{1,0},{2,1},{3,2},{4,3},{5,4},{6,5},{7,6},{9,8},{10,9},{11,10},{12... | collective-permute-start | bytes 7352 | tf_op jit(solution)/shard_map/ppermute | solution.py:22
  45.1 47.8 %collective-permute-start.3 = (f32[12,1,8,128]{3,1,2,0:T(1,128)S(1)}, f32[12,1,8,128]{3,1,2,0:T(1,128)S(1)}, u32[]{:S(2)}, u32[]{:S(2)}) collective-permute-start(f32[12,1,8,128]{3,1,2,0:T(1,128)S(1)} %get-tuple-element.67), channel_id=1, source_target_pairs={{8,0},{16,8},{24,16},{32,24},{40,32},{48,40},{56,48},{64,56},{72,6... | collective-permute-start | bytes 147464 | tf_op jit(solution)/shard_map/ppermute | solution.py:22
  49.6 6.3 %collective-permute-start.16 = (f32[3,4,8,1]{3,2,1,0:T(8,128)S(1)}, f32[3,4,8,1]{3,2,1,0:T(8,128)S(1)}, u32[]{:S(2)}, u32[]{:S(2)}) collective-permute-start(f32[3,4,8,1]{3,2,1,0:T(8,128)S(1)} %get-tuple-element.90), channel_id=1, source_target_pairs={{0,128},{128,256},{256,384},{1,129},{129,257},{257,385},{2,130},{1... | collective-permute-start | bytes 1160 | tf_op jit(solution)/shard_map/ppermute | solution.py:20
  54.1 6.0 %collective-permute-start.17 = (f32[3,4,8,1]{3,2,1,0:T(8,128)S(1)}, f32[3,4,8,1]{3,2,1,0:T(8,128)S(1)}, u32[]{:S(2)}, u32[]{:S(2)}) collective-permute-start(f32[3,4,8,1]{3,2,1,0:T(8,128)S(1)} %get-tuple-element.91), channel_id=1, source_target_pairs={{128,0},{256,128},{384,256},{129,1},{257,129},{385,257},{130,2},{2... | collective-permute-start | bytes 1160 | tf_op jit(solution)/shard_map/ppermute | solution.py:22
  60.2 24.1 %collective-permute-start.18 = (f32[3,1,8,34]{3,2,1,0:T(8,128)S(1)}, f32[3,1,8,34]{3,2,1,0:T(8,128)S(1)}, u32[]{:S(2)}, u32[]{:S(2)}) collective-permute-start(f32[3,1,8,34]{3,2,1,0:T(8,128)S(1)} %get-tuple-element.68), channel_id=1, source_target_pairs={{0,8},{8,16},{16,24},{24,32},{32,40},{40,48},{48,56},{56,64},{64,7... | collective-permute-start | bytes 9800 | tf_op jit(solution)/shard_map/ppermute | solution.py:20
  62.8 21.5 %collective-permute-start.19 = (f32[3,1,8,34]{3,2,1,0:T(8,128)S(1)}, f32[3,1,8,34]{3,2,1,0:T(8,128)S(1)}, u32[]{:S(2)}, u32[]{:S(2)}) collective-permute-start(f32[3,1,8,34]{3,2,1,0:T(8,128)S(1)} %get-tuple-element.69), channel_id=1, source_target_pairs={{8,0},{16,8},{24,16},{32,24},{40,32},{48,40},{56,48},{64,56},{72,6... | collective-permute-start | bytes 9800 | tf_op jit(solution)/shard_map/ppermute | solution.py:22
  84.3 50.5 %copy-start.2 = (f32[1,6,4,8,128]{4,2,3,1,0:T(4,128)}, f32[1,6,4,8,128]{4,2,3,1,0:T(4,128)S(1)}, u32[]{:S(2)}) copy-start(f32[1,6,4,8,128]{4,2,3,1,0:T(4,128)S(1)} %copy.435) | copy-start | bytes 294916
  84.4 2.8 %collective-permute-start.20 = (f32[3,6,1,34]{3,1,2,0:T(8,128)S(1)}, f32[3,6,1,34]{3,1,2,0:T(8,128)S(1)}, u32[]{:S(2)}, u32[]{:S(2)}) collective-permute-start(f32[3,6,1,34]{3,1,2,0:T(8,128)S(1)} %get-tuple-element.78), channel_id=1, source_target_pairs={{0,1},{1,2},{2,3},{3,4},{4,5},{5,6},{6,7},{8,9},{9,10},{10,11},{11... | collective-permute-start | bytes 7352 | tf_op jit(solution)/shard_map/ppermute | solution.py:20
  85.9 6.4 %collective-permute-start.21 = (f32[3,6,1,34]{3,1,2,0:T(8,128)S(1)}, f32[3,6,1,34]{3,1,2,0:T(8,128)S(1)}, u32[]{:S(2)}, u32[]{:S(2)}) collective-permute-start(f32[3,6,1,34]{3,1,2,0:T(8,128)S(1)} %get-tuple-element.79), channel_id=1, source_target_pairs={{1,0},{2,1},{3,2},{4,3},{5,4},{6,5},{7,6},{9,8},{10,9},{11,10},{12... | collective-permute-start | bytes 7352 | tf_op jit(solution)/shard_map/ppermute | solution.py:22
  92.9 24.9 %collective-permute-start.4 = (f32[12,6,1,128]{3,1,2,0:T(8,128)S(1)}, f32[12,6,1,128]{3,1,2,0:T(8,128)S(1)}, u32[]{:S(2)}, u32[]{:S(2)}) collective-permute-start(f32[12,6,1,128]{3,1,2,0:T(8,128)S(1)} %get-tuple-element.59), channel_id=1, source_target_pairs={{0,1},{1,2},{2,3},{3,4},{4,5},{5,6},{6,7},{8,9},{9,10},{10,11},{11... | collective-permute-start | bytes 110600 | tf_op jit(solution)/shard_map/ppermute | solution.py:20
  97.3 20.6 %collective-permute-start.5 = (f32[12,6,1,128]{3,1,2,0:T(8,128)S(1)}, f32[12,6,1,128]{3,1,2,0:T(8,128)S(1)}, u32[]{:S(2)}, u32[]{:S(2)}) collective-permute-start(f32[12,6,1,128]{3,1,2,0:T(8,128)S(1)} %get-tuple-element.60), channel_id=1, source_target_pairs={{1,0},{2,1},{3,2},{4,3},{5,4},{6,5},{7,6},{9,8},{10,9},{11,10},{12... | collective-permute-start | bytes 110600 | tf_op jit(solution)/shard_map/ppermute | solution.py:22
  119.5 0.9 copy-start
  119.5 1.0 copy-start.5
  120.7 6.5 %collective-permute-start.6 = (f32[12,1,8,128]{3,2,1,0:T(8,128)S(1)}, f32[12,1,8,128]{3,2,1,0:T(8,128)S(1)}, u32[]{:S(2)}, u32[]{:S(2)}) collective-permute-start(f32[12,1,8,128]{3,2,1,0:T(8,128)S(1)} %get-tuple-element.64), channel_id=1, source_target_pairs={{0,8},{8,16},{16,24},{24,32},{32,40},{40,48},{48,56},{56,64},{64,7... | collective-permute-start | bytes 147464 | tf_op jit(solution)/shard_map/ppermute | solution.py:20
  124.2 7.8 %collective-permute-start.7 = (f32[12,1,8,128]{3,2,1,0:T(8,128)S(1)}, f32[12,1,8,128]{3,2,1,0:T(8,128)S(1)}, u32[]{:S(2)}, u32[]{:S(2)}) collective-permute-start(f32[12,1,8,128]{3,2,1,0:T(8,128)S(1)} %get-tuple-element.65), channel_id=1, source_target_pairs={{8,0},{16,8},{24,16},{32,24},{40,32},{48,40},{56,48},{64,56},{72,6... | collective-permute-start | bytes 147464 | tf_op jit(solution)/shard_map/ppermute | solution.py:22
  132.0 2.8 %collective-permute-start.8 = (f32[12,6,1,128]{3,2,1,0:T(1,128)S(1)}, f32[12,6,1,128]{3,2,1,0:T(1,128)S(1)}, u32[]{:S(2)}, u32[]{:S(2)}) collective-permute-start(f32[12,6,1,128]{3,2,1,0:T(1,128)S(1)} %get-tuple-element.54), channel_id=1, source_target_pairs={{0,1},{1,2},{2,3},{3,4},{4,5},{5,6},{6,7},{8,9},{9,10},{10,11},{11... | collective-permute-start | bytes 110600 | tf_op jit(solution)/shard_map/ppermute | solution.py:20
  133.3 5.1 %collective-permute-start.9 = (f32[12,6,1,128]{3,2,1,0:T(1,128)S(1)}, f32[12,6,1,128]{3,2,1,0:T(1,128)S(1)}, u32[]{:S(2)}, u32[]{:S(2)}) collective-permute-start(f32[12,6,1,128]{3,2,1,0:T(1,128)S(1)} %get-tuple-element.55), channel_id=1, source_target_pairs={{1,0},{2,1},{3,2},{4,3},{5,4},{6,5},{7,6},{9,8},{10,9},{11,10},{12... | collective-permute-start | bytes 110600 | tf_op jit(solution)/shard_map/ppermute | solution.py:22
  142.0 0.9 copy-start.4
  142.1 0.9 copy-start.3
  142.1 0.9 copy-start.8
Sparse Core Ops, SparseCore 0:
  144.6 48.0 reduce-scatter.3
where the time goes:
time: 202 us; the launch traced here: 201 us
  waiting for transfers between devices  69.5 us (34%)
  starting transfers between devices  54.6 us (27%)
  blocking collectives  35.6 us (18%)
  between operations  16.4 us (8%)
  other arithmetic  13.2 us (7%)
  local copies, waits for them, and re-layouts  11.7 us (6%)
    unnamed x2, waiting for transfers between devices  46.9 us
    all_gather x2, blocking collectives, local(): master_whole = lax.all_gather(master_strain[0], 'grp', axis=3, tiled=True)  35.6 us
    ppermute x10, starting transfers between devices, with_halo(): lax.ppermute(tail, axis, [(i, (i + 1) % count) for i in range(ends)])  31.7 us
    ppermute x10, waiting for transfers between devices, with_halo(): lax.ppermute(head, axis, [((i + 1) % count, i) for i in range(ends)])  22.5 us
    ppermute x10, starting transfers between devices, with_halo(): lax.ppermute(head, axis, [((i + 1) % count, i) for i in range(ends)])  17.7 us
    unnamed x36, local copies, waits for them, and re-layouts  5.5 us
    ppermute x2, starting transfers between devices, passed_along(): return lax.ppermute(value, axis, pairs)  5.22 us
  transfers between devices with their start and end apart: 23, of which 8 were waited for; matrix products, arithmetic and copies ran while one was open for 7% of the time, Pallas kernels for 0%

commit v1 on v0

v1 whole, which is shorter than its diff:
```python
import jax
import jax.numpy as jnp
from jax import lax
from jax.sharding import PartitionSpec as P

STEPS = 2


time_step_sq = 0.0625


def with_halo(cells, sides, width):
    for axis, dim in sides:
        count = lax.axis_size(axis)
        ends = count - 1
        head = lax.slice_in_dim(cells, 0, width, axis=dim)
        tail = lax.slice_in_dim(cells, cells.shape[dim] - width, cells.shape[dim], axis=dim)
        cells = jnp.concatenate(
            [
                lax.ppermute(tail, axis, [(i, i + 1) for i in range(ends)]),
                cells,
                lax.ppermute(head, axis, [(i + 1, i) for i in range(ends)]),
            ],
            axis=dim,
        )
    return cells


def backward_diff(stress, axis):
    upper = stress[:, 1:, 1:, 1:]
    if axis == 1:
        lower = stress[:, :-1, 1:, 1:]
    elif axis == 2:
        lower = stress[:, 1:, :-1, 1:]
    else:
        lower = stress[:, 1:, 1:, :-1]
    return upper - lower


def strains_of(padded):
    span_x = padded.shape[2] - 2
    span_y = padded.shape[3] - 2
    span_z = padded.shape[4] - 2
    anchor = padded[:, :, : span_x + 1, : span_y + 1, : span_z + 1]
    grad_x = padded[:, :, 1:, : span_y + 1, : span_z + 1] - anchor
    grad_y = padded[:, :, : span_x + 1, 1:, : span_z + 1] - anchor
    grad_z = padded[:, :, : span_x + 1, : span_y + 1, 1:] - anchor
    strain_xx = grad_x[:, 0]
    strain_yy = grad_y[:, 1]
    strain_zz = grad_z[:, 2]
    strain_xy = 0.5 * (grad_y[:, 0] + grad_x[:, 1])
    strain_xz = 0.5 * (grad_z[:, 0] + grad_x[:, 2])
    strain_yz = 0.5 * (grad_z[:, 1] + grad_y[:, 2])
    return strain_xx, strain_yy, strain_zz, strain_xy, strain_xz, strain_yz


def stencil(padded, lame_pad, shear_pad):
    span_x = padded.shape[2] - 2
    span_y = padded.shape[3] - 2
    span_z = padded.shape[4] - 2
    strain_xx, strain_yy, strain_zz, strain_xy, strain_xz, strain_yz = strains_of(padded)
    lame = lame_pad[: span_x + 1, : span_y + 1, : span_z + 1]
    shear = shear_pad[: span_x + 1, : span_y + 1, : span_z + 1]
    dilation = strain_xx + strain_yy + strain_zz
    stress_xx = lame * dilation + 2.0 * shear * strain_xx
    stress_yy = lame * dilation + 2.0 * shear * strain_yy
    stress_zz = lame * dilation + 2.0 * shear * strain_zz
    stress_xy = 2.0 * shear * strain_xy
    stress_xz = 2.0 * shear * strain_xz
    stress_yz = 2.0 * shear * strain_yz
    force_x = (
        backward_diff(stress_xx, 1) + backward_diff(stress_xy, 2) + backward_diff(stress_xz, 3)
    )
    force_y = (
        backward_diff(stress_xy, 1) + backward_diff(stress_yy, 2) + backward_diff(stress_yz, 3)
    )
    force_z = (
        backward_diff(stress_xz, 1) + backward_diff(stress_yz, 2) + backward_diff(stress_zz, 3)
    )
    force = jnp.stack([force_x, force_y, force_z], axis=1)
    strain = jnp.stack([strain_xx, strain_yy, strain_zz, strain_xy, strain_xz, strain_yz], axis=1)
    return (force, strain[:, :, 1:, 1:, 1:])


def zpad(cells):
    widths = [(0, 0)] * (cells.ndim - 1) + [(1, 1)]
    return jnp.pad(cells, widths)


def locate(cells, start_x, start_y, width_y, depth, span_x, span_y):
    coord_x = cells // (width_y * depth) - start_x
    coord_y = cells // depth % width_y - start_y
    coord_z = cells % depth
    index_x = lax.broadcasted_iota(jnp.int32, (1, span_x, 1, 1), 1)
    index_y = lax.broadcasted_iota(jnp.int32, (1, 1, span_y, 1), 2)
    index_z = lax.broadcasted_iota(jnp.int32, (1, 1, 1, depth), 3)
    found = (
        (index_x == coord_x[:, None, None, None])
        & (index_y == coord_y[:, None, None, None])
        & (index_z == coord_z[:, None, None, None])
    )
    return found.astype(jnp.float32)


def pick(trace, lags):
    positions = lax.broadcasted_iota(jnp.int32, (1, trace.shape[1]), 1)
    chosen = positions == lags[:, None]
    return jnp.sum(jnp.where(chosen[:, :, None], trace, 0.0), axis=1)


def advance(current, earlier, force, amplitudes, masks, buoyancy):
    source = amplitudes[:, :, None, None, None] * masks[:, None]
    return 2.0 * current - earlier + time_step_sq * buoyancy * (force + source)


def local(
    fwd_now,
    fwd_prev,
    adj_now,
    adj_prev,
    lame_first,
    shear_mod,
    buoyancy,
    master_cell,
    master_lag,
    master_trace,
    receiver_cell,
    receiver_lag,
    receiver_trace,
):
    cells_x, cells_y, depth = lame_first.shape
    groups = lax.axis_size("grp")
    receivers = adj_now.shape[0]
    fields = receivers + 1
    width_y = cells_y * lax.axis_size("gy")
    start_x = lax.axis_index("gx") * cells_x
    start_y = lax.axis_index("gy") * cells_y
    grid = (cells_x, cells_y, depth)

    now = jnp.concatenate([fwd_now[None], adj_now]).reshape((fields * 3,) + grid)
    prev = jnp.concatenate([fwd_prev[None], adj_prev]).reshape((fields * 3,) + grid)
    moduli = jnp.stack([lame_first, shear_mod, buoyancy])
    stacked = jnp.concatenate([now, prev, moduli])
    grown = with_halo(stacked, (("gx", 1), ("gy", 2)), 2)
    now_grown = grown[: fields * 3].reshape((fields, 3) + grown.shape[1:])
    prev_grown = grown[fields * 3 : fields * 6].reshape((fields, 3) + grown.shape[1:])
    lame_grown = zpad(grown[fields * 6])
    shear_grown = zpad(grown[fields * 6 + 1])
    buoy_grown = grown[fields * 6 + 2]

    cells = jnp.concatenate([master_cell, receiver_cell])
    amps = [
        jnp.concatenate(
            [
                pick(master_trace[None], master_lag + instant),
                pick(receiver_trace, receiver_lag + instant),
            ]
        )
        for instant in range(STEPS)
    ]
    masks_wide = locate(
        cells, start_x - 1, start_y - 1, width_y, depth, cells_x + 2, cells_y + 2
    )
    masks = masks_wide[:, 1:-1, 1:-1]

    force0, strain0 = stencil(zpad(now_grown), lame_grown, shear_grown)
    now_wide = now_grown[:, :, 1:-1, 1:-1]
    next_wide = advance(
        now_wide,
        prev_grown[:, :, 1:-1, 1:-1],
        force0,
        amps[0],
        masks_wide,
        buoy_grown[1:-1, 1:-1],
    )
    strain0 = strain0[:, :, 1:-1, 1:-1]

    force1, strain1 = stencil(
        zpad(next_wide[1:]), lame_grown[1:-1, 1:-1], shear_grown[1:-1, 1:-1]
    )
    master1 = stencil(zpad(next_wide[:1]), lame_grown[1:-1, 1:-1], shear_grown[1:-1, 1:-1])[1]
    final = advance(
        next_wide[1:, :, 1:-1, 1:-1],
        now_wide[1:, :, 1:-1, 1:-1],
        force1,
        amps[1][1:],
        masks[1:],
        buoy_grown[2:-2, 2:-2],
    )

    weights = jnp.array([1.0, 1.0, 1.0, 2.0, 2.0, 2.0], jnp.float32)[:, None, None, None]
    totals = jnp.zeros((2,) + grid, jnp.float32)
    for master, strain in ((strain0[0], strain0[1:]), (master1[0], strain1)):
        summed = jnp.sum(strain, axis=0)
        dilation_term = (master[0] + master[1] + master[2]) * (summed[0] + summed[1] + summed[2])
        shear_term = 2.0 * jnp.sum(weights * master * summed, axis=0)
        totals = totals + jnp.stack([dilation_term, shear_term])
    totals = totals * (1.0 / (STEPS * receivers * groups))

    share = depth // groups
    me = lax.axis_index("grp")
    kernels = lax.dynamic_slice_in_dim(totals, me * share, share, 3)
    for shift in range(1, groups):
        part = lax.dynamic_slice_in_dim(totals, (me + shift) % groups * share, share, 3)
        kernels = kernels + lax.ppermute(
            part, "grp", [(i, (i + shift) % groups) for i in range(groups)]
        )
    return (final, kernels)


def solution(mesh):
    in_specs = (
        P(None, "gx", "gy", None),
        P(None, "gx", "gy", None),
        P("grp", None, "gx", "gy", None),
        P("grp", None, "gx", "gy", None),
        P("gx", "gy", None),
        P("gx", "gy", None),
        P("gx", "gy", None),
        P(),
        P(),
        P(),
        P("grp"),
        P("grp"),
        P("grp", None, None),
    )
    out_specs = (P("grp", None, "gx", "gy", None), P(None, "gx", "gy", "grp"))
    return jax.shard_map(local, mesh=mesh, in_specs=in_specs, out_specs=out_specs, check_vma=False)
```

time: 202 us -> 70.7 us (0.35)
  the two profiles are of different devices: /device:TPU:8 before, /device:TPU:121 now
where the time goes in v1:
time: 70.7 us; the launch traced here: 70.3 us
  starting transfers between devices  31.6 us (45%)
  waiting for transfers between devices  19.9 us (28%)
  other arithmetic  12.9 us (18%)
  local copies, waits for them, and re-layouts  3.27 us (5%)
  between operations  2.68 us (4%)
    ppermute x2, starting transfers between devices, with_halo(): lax.ppermute(tail, axis, [(i, i + 1) for i in range(ends)])  17.8 us
    ppermute x2, waiting for transfers between devices, with_halo(): lax.ppermute(head, axis, [(i + 1, i) for i in range(ends)])  15.5 us
    ppermute x3, starting transfers between devices, local(): lax.ppermute(part, 'grp', [(i, (i + shift) % groups) for i in range(group...  9.93 us
    ppermute x2, starting transfers between devices, with_halo(): lax.ppermute(head, axis, [(i + 1, i) for i in range(ends)])  3.84 us
    sub x3, other arithmetic, strains_of(): grad_y = padded[:, :, :span_x + 1, 1:, :span_z + 1] - anchor  3.66 us
    ppermute x2, waiting for transfers between devices, with_halo(): lax.ppermute(tail, axis, [(i, i + 1) for i in range(ends)])  2.76 us
    ppermute x3, waiting for transfers between devices, local(): lax.ppermute(part, 'grp', [(i, (i + shift) % groups) for i in range(group...  1.63 us
  transfers between devices with their start and end apart: 7, of which 5 were waited for; matrix products, arithmetic and copies ran while one was open for 3% of the time, Pallas kernels for 0%

profile of v1, /device:TPU:121, one launch (start us, length us, event | category | flops | bytes accessed | tf_op | source)
XLA Modules:
  0.0 70.3 jit_solution(9980593830380954980)
XLA Ops:
  0.7 1.0 %pad_maximum_fusion.4 = f32[5,3,4,8,128]{4,3,2,1,0:T(8,128)S(1)} fusion(f32[4,3,4,8,128]{4,3,2,1,0:T(8,128)} %param.16, f32[1,3,4,8,128]{4,3,2,1,0:T(8,128)} %bitcast.190), kind=kLoop, calls=%fused_computation.94 | loop fusion | flops 61440 | bytes 491520 | tf_op jit(solution)/shard_map/concatenate | solution.py:140
  1.7 1.0 %pad_maximum_fusion.5 = f32[5,3,4,8,128]{4,3,2,1,0:T(8,128)S(1)} fusion(f32[4,3,4,8,128]{4,3,2,1,0:T(8,128)} %param.17, f32[1,3,4,8,128]{4,3,2,1,0:T(8,128)} %bitcast.191), kind=kLoop, calls=%fused_computation.95 | loop fusion | flops 61440 | bytes 491520 | tf_op jit(solution)/shard_map/concatenate | solution.py:141
  2.9 0.2 fusion.68
  3.2 8.9 %collective-permute-start = (f32[33,2,8,128]{3,1,2,0:T(2,128)S(1)}, f32[33,2,8,128]{3,1,2,0:T(2,128)S(1)}, u32[]{:S(2)}, u32[]{:S(2)}) collective-permute-start(f32[33,2,8,128]{3,1,2,0:T(2,128)S(1)} %get-tuple-element.40), channel_id=1, source_target_pairs={{0,8},{8,16},{16,24},{24,32},{32,40},{40,48},{48,56},{56,64},{64,7... | collective-permute-start | bytes 811016 | tf_op jit(solution)/shard_map/ppermute | solution.py:20
  12.1 1.9 %collective-permute-start.1 = (f32[33,2,8,128]{3,1,2,0:T(2,128)S(1)}, f32[33,2,8,128]{3,1,2,0:T(2,128)S(1)}, u32[]{:S(2)}, u32[]{:S(2)}) collective-permute-start(f32[33,2,8,128]{3,1,2,0:T(2,128)S(1)} %get-tuple-element.41), channel_id=1, source_target_pairs={{8,0},{16,8},{24,16},{32,24},{40,32},{48,40},{56,48},{64,56},{72,6... | collective-permute-start | bytes 811016 | tf_op jit(solution)/shard_map/ppermute | solution.py:22
  16.3 1.6 %collective-permute-done = f32[33,2,8,128]{3,1,2,0:T(2,128)S(1)} collective-permute-done((f32[33,2,8,128]{3,1,2,0:T(2,128)S(1)}, f32[33,2,8,128]{3,1,2,0:T(2,128)S(1)}, u32[]{:S(2)}, u32[]{:S(2)}) %collective-permute-start) | collective-permute-done | bytes 270368 | tf_op jit(solution)/shard_map/ppermute | solution.py:20
  17.8 11.1 %collective-permute-done.1 = f32[33,2,8,128]{3,1,2,0:T(2,128)S(1)} collective-permute-done((f32[33,2,8,128]{3,1,2,0:T(2,128)S(1)}, f32[33,2,8,128]{3,1,2,0:T(2,128)S(1)}, u32[]{:S(2)}, u32[]{:S(2)}) %collective-permute-start.1) | collective-permute-done | bytes 270368 | tf_op jit(solution)/shard_map/ppermute | solution.py:22
  28.9 0.2 pad_maximum_fusion.3
  29.1 8.9 %collective-permute-start.2 = (f32[33,8,2,128]{3,1,2,0:T(8,128)S(1)}, f32[33,8,2,128]{3,1,2,0:T(8,128)S(1)}, u32[]{:S(2)}, u32[]{:S(2)}) collective-permute-start(f32[33,8,2,128]{3,1,2,0:T(8,128)S(1)} %get-tuple-element.27), channel_id=1, source_target_pairs={{0,1},{1,2},{2,3},{3,4},{4,5},{5,6},{6,7},{8,9},{9,10},{10,11},{11... | collective-permute-start | bytes 811016 | tf_op jit(solution)/shard_map/ppermute | solution.py:20
  38.0 1.9 %collective-permute-start.3 = (f32[33,8,2,128]{3,1,2,0:T(8,128)S(1)}, f32[33,8,2,128]{3,1,2,0:T(8,128)S(1)}, u32[]{:S(2)}, u32[]{:S(2)}) collective-permute-start(f32[33,8,2,128]{3,1,2,0:T(8,128)S(1)} %get-tuple-element.28), channel_id=1, source_target_pairs={{1,0},{2,1},{3,2},{4,3},{5,4},{6,5},{7,6},{9,8},{10,9},{11,10},{12... | collective-permute-start | bytes 811016 | tf_op jit(solution)/shard_map/ppermute | solution.py:22
  40.1 1.2 %collective-permute-done.2 = f32[33,8,2,128]{3,1,2,0:T(8,128)S(1)} collective-permute-done((f32[33,8,2,128]{3,1,2,0:T(8,128)S(1)}, f32[33,8,2,128]{3,1,2,0:T(8,128)S(1)}, u32[]{:S(2)}, u32[]{:S(2)}) %collective-permute-start.2) | collective-permute-done | bytes 270368 | tf_op jit(solution)/shard_map/ppermute | solution.py:20
  41.4 4.4 %collective-permute-done.3 = f32[33,8,2,128]{3,1,2,0:T(8,128)S(1)} collective-permute-done((f32[33,8,2,128]{3,1,2,0:T(8,128)S(1)}, f32[33,8,2,128]{3,1,2,0:T(8,128)S(1)}, u32[]{:S(2)}, u32[]{:S(2)}) %collective-permute-start.3) | collective-permute-done | bytes 270368 | tf_op jit(solution)/shard_map/ppermute | solution.py:22
  46.1 0.4 pad_maximum_fusion
  47.0 2.3 %fusion.1 = (f32[5,3,7,11,129]{4,3,2,0,1:T(8,128)S(1)}, f32[5,3,7,11,129]{4,3,2,0,1:T(8,128)S(1)}, f32[5,3,7,11,129]{4,3,2,0,1:T(8,128)S(1)}) fusion(f32[5,3,8,12,128]{4,3,2,0,1:T(8,128)S(1)} %copy.112), kind=kLoop, calls=%fused_computation.9 | loop fusion | flops 446985 | bytes 2525220 | tf_op jit(solution)/shard_map/sub | solution.py:46
  49.3 0.7 fusion.14
  50.0 0.2 fusion.13
  50.2 0.9 %fusion.27 = (f32[5,1,6,10,128]{4,3,2,0,1:T(8,128)S(1)}, f32[5,1,6,10,128]{4,3,2,0,1:T(8,128)S(1)}, f32[5,1,6,10,128]{4,3,2,0,1:T(8,128)S(1)}) fusion(f32[5,7,11,129]{3,2,1,0:T(8,128)S(1)} %get-tuple-element.17, f32[5,7,11,129]{3,2,1,0:T(8,128)S(1)} %get-tuple-element.16, f32[5,7,11,129]{3,2,1,0:T(8,128)S(1)} %get-tuple-element.14, ...), kind=kLoop, calls=%fused_computation.90 | loop fusion | flops 576000 | bytes 2764800 | tf_op jit(solution)/shard_map/stack | solution.py:80
  51.1 0.3 fusion.7
  51.6 0.6 copy-done
  52.5 0.8 %slice-done = f32[4,3,6,10,128]{4,3,2,0,1:T(8,128)S(1)} async-done(((f32[5,3,6,10,128]{4,3,2,0,1:T(8,128)}), f32[4,3,6,10,128]{4,3,2,0,1:T(8,128)S(1)}, s32[]{:S(2)}) %slice-start) | async-done | bytes 368664 | tf_op jit(solution)/shard_map/slice | solution.py:179
  53.4 1.3 %fusion.4 = (f32[4,3,5,9,129]{4,3,2,0,1:T(8,128)S(1)}, f32[4,3,5,9,129]{4,3,2,0,1:T(8,128)S(1)}, f32[4,3,5,9,129]{4,3,2,0,1:T(8,128)S(1)}) fusion(f32[4,3,6,10,128]{4,3,2,0,1:T(8,128)S(1)} %slice-done), kind=kLoop, calls=%fused_computation.13 | loop fusion | flops 208980 | bytes 1204560 | tf_op jit(solution)/shard_map/sub | solution.py:46
  54.7 0.4 fusion.18
  55.5 0.2 slice_reduce_fusion
  56.2 0.2 slice_reduce_fusion.1
  56.5 0.2 copy-done.7
  56.9 3.1 %collective-permute-start.4 = (f32[2,4,8,32]{3,2,1,0:T(8,128)S(1)}, f32[2,4,8,32]{3,2,1,0:T(8,128)S(1)}, u32[]{:S(2)}, u32[]{:S(2)}) collective-permute-start(f32[2,4,8,32]{3,2,1,0:T(8,128)S(1)} %get-tuple-element.53), channel_id=1, source_target_pairs={{0,128},{128,256},{256,384},{384,0},{1,129},{129,257},{257,385},{3... | collective-permute-start | bytes 24584 | tf_op jit(solution)/shard_map/ppermute | solution.py:205
  60.1 3.4 %collective-permute-start.6 = (f32[2,4,8,32]{3,2,1,0:T(8,128)S(1)}, f32[2,4,8,32]{3,2,1,0:T(8,128)S(1)}, u32[]{:S(2)}, u32[]{:S(2)}) collective-permute-start(f32[2,4,8,32]{3,2,1,0:T(8,128)S(1)} %get-tuple-element.54), channel_id=1, source_target_pairs={{0,384},{128,0},{256,128},{384,256},{1,385},{129,1},{257,129},{385... | collective-permute-start | bytes 24584 | tf_op jit(solution)/shard_map/ppermute | solution.py:205
  63.5 3.4 %collective-permute-start.5 = (f32[2,4,8,32]{3,2,1,0:T(8,128)S(1)}, f32[2,4,8,32]{3,2,1,0:T(8,128)S(1)}, u32[]{:S(2)}, u32[]{:S(2)}) collective-permute-start(f32[2,4,8,32]{3,2,1,0:T(8,128)S(1)} %get-tuple-element.55), channel_id=1, source_target_pairs={{0,256},{128,384},{256,0},{384,128},{1,257},{129,385},{257,1},{385... | collective-permute-start | bytes 24584 | tf_op jit(solution)/shard_map/ppermute | solution.py:205
  66.9 0.3 fusion.55
  67.2 0.8 %fusion.30 = f32[4,3,4,8,128]{4,3,2,1,0:T(8,128)} fusion(f32[4,1,4,8,128]{4,3,2,1,0:T(8,128)S(1)} %get-tuple-element.46, f32[4,1,4,8,128]{4,3,2,1,0:T(8,128)S(1)} %get-tuple-element.45, f32[4,1,4,8,128]{4,3,2,1,0:T(8,128)S(1)} %get-tuple-element.44, f32[4,3,4,8,128]{4,2,3,1,0:T(4,128)S(1)} %slice.502, f32[4,4,8,128]{3,2,1,0:T(8,128)S(1)} %slice.529, ...), kind=kLoop, calls=%fused_computation.99 | loop fusion | flops 393216 | bytes 870400 | tf_op jit(solution)/shard_map/add | solution.py:113
  68.0 1.6 %collective-permute-done.5 = f32[2,4,8,32]{3,2,1,0:T(8,128)S(1)} collective-permute-done((f32[2,4,8,32]{3,2,1,0:T(8,128)S(1)}, f32[2,4,8,32]{3,2,1,0:T(8,128)S(1)}, u32[]{:S(2)}, u32[]{:S(2)}) %collective-permute-start.5) | collective-permute-done | bytes 8224 | tf_op jit(solution)/shard_map/ppermute | solution.py:205
  69.6 0.7 add_add_fusion
  (90 shorter events, 3.6 us)
Async XLA Ops:
  0.6 2.2 %copy-start.2 = (f32[4,8,128]{2,1,0:T(8,128)S(1)}, f32[4,8,128]{2,1,0:T(8,128)}, u32[]{:S(2)}) copy-start(f32[4,8,128]{2,1,0:T(8,128)} %param.18) | copy-start | bytes 49156
  0.6 2.2 %copy-start.3 = (f32[4,8,128]{2,1,0:T(8,128)S(1)}, f32[4,8,128]{2,1,0:T(8,128)}, u32[]{:S(2)}) copy-start(f32[4,8,128]{2,1,0:T(8,128)} %param.19) | copy-start | bytes 49156
  0.7 2.3 %copy-start.4 = (f32[4,8,128]{2,1,0:T(8,128)S(1)}, f32[4,8,128]{2,1,0:T(8,128)}, u32[]{:S(2)}) copy-start(f32[4,8,128]{2,1,0:T(8,128)} %param.20) | copy-start | bytes 49156
  1.6 13.7 %copy-start.8 = (s32[4]{0:T(128)S(1)}, s32[4]{0:T(128)}, u32[]{:S(2)}) copy-start(s32[4]{0:T(128)} %param.24) | copy-start | bytes 52
  1.6 13.9 %copy-start.9 = (s32[4]{0:T(128)S(1)}, s32[4]{0:T(128)}, u32[]{:S(2)}) copy-start(s32[4]{0:T(128)} %param.25) | copy-start | bytes 52
  1.7 14.0 %copy-start.5 = (f32[4,256,3]{1,0,2:T(4,128)S(1)}, f32[4,256,3]{1,0,2:T(4,128)}, u32[]{:S(2)}) copy-start(f32[4,256,3]{1,0,2:T(4,128)} %param.26) | copy-start | bytes 36868
  1.7 14.1 %copy-start.6 = (f32[256,3]{0,1:T(4,128)S(1)}, f32[256,3]{0,1:T(4,128)}, u32[]{:S(2)}) copy-start(f32[256,3]{0,1:T(4,128)} %param.23) | copy-start | bytes 9220
  3.2 14.7 %collective-permute-start = (f32[33,2,8,128]{3,1,2,0:T(2,128)S(1)}, f32[33,2,8,128]{3,1,2,0:T(2,128)S(1)}, u32[]{:S(2)}, u32[]{:S(2)}) collective-permute-start(f32[33,2,8,128]{3,1,2,0:T(2,128)S(1)} %get-tuple-element.40), channel_id=1, source_target_pairs={{0,8},{8,16},{16,24},{24,32},{32,40},{40,48},{48,56},{56,64},{64,7... | collective-permute-start | bytes 811016 | tf_op jit(solution)/shard_map/ppermute | solution.py:20
  12.1 16.8 %collective-permute-start.1 = (f32[33,2,8,128]{3,1,2,0:T(2,128)S(1)}, f32[33,2,8,128]{3,1,2,0:T(2,128)S(1)}, u32[]{:S(2)}, u32[]{:S(2)}) collective-permute-start(f32[33,2,8,128]{3,1,2,0:T(2,128)S(1)} %get-tuple-element.41), channel_id=1, source_target_pairs={{8,0},{16,8},{24,16},{32,24},{40,32},{48,40},{56,48},{64,56},{72,6... | collective-permute-start | bytes 811016 | tf_op jit(solution)/shard_map/ppermute | solution.py:22
  29.1 12.3 %collective-permute-start.2 = (f32[33,8,2,128]{3,1,2,0:T(8,128)S(1)}, f32[33,8,2,128]{3,1,2,0:T(8,128)S(1)}, u32[]{:S(2)}, u32[]{:S(2)}) collective-permute-start(f32[33,8,2,128]{3,1,2,0:T(8,128)S(1)} %get-tuple-element.27), channel_id=1, source_target_pairs={{0,1},{1,2},{2,3},{3,4},{4,5},{5,6},{6,7},{8,9},{9,10},{10,11},{11... | collective-permute-start | bytes 811016 | tf_op jit(solution)/shard_map/ppermute | solution.py:20
  38.0 7.8 %collective-permute-start.3 = (f32[33,8,2,128]{3,1,2,0:T(8,128)S(1)}, f32[33,8,2,128]{3,1,2,0:T(8,128)S(1)}, u32[]{:S(2)}, u32[]{:S(2)}) collective-permute-start(f32[33,8,2,128]{3,1,2,0:T(8,128)S(1)} %get-tuple-element.28), channel_id=1, source_target_pairs={{1,0},{2,1},{3,2},{4,3},{5,4},{6,5},{7,6},{9,8},{10,9},{11,10},{12... | collective-permute-start | bytes 811016 | tf_op jit(solution)/shard_map/ppermute | solution.py:22
  51.4 0.9 %copy-start = (f32[5,3,6,10,128]{4,3,2,0,1:T(8,128)}, f32[5,3,6,10,128]{4,3,2,0,1:T(8,128)S(1)}, u32[]{:S(2)}) copy-start(f32[5,3,6,10,128]{4,3,2,0,1:T(8,128)S(1)} %fusion.7) | copy-start | bytes 1382404
  52.3 1.1 %slice-start = ((f32[5,3,6,10,128]{4,3,2,0,1:T(8,128)}), f32[4,3,6,10,128]{4,3,2,0,1:T(8,128)S(1)}, s32[]{:S(2)}) async-start(f32[5,3,6,10,128]{4,3,2,0,1:T(8,128)} %copy-done), calls=%async_computation | async-start | bytes 1179648 | tf_op jit(solution)/shard_map/slice | solution.py:179
  56.0 0.7 copy-start.7
  56.2 11.0 %copy-start.1 = (f32[5,3,6,10,128]{4,3,2,0,1:T(8,128)S(1)}, f32[5,3,6,10,128]{4,3,2,0,1:T(8,128)}, u32[]{:S(2)}) copy-start(f32[5,3,6,10,128]{4,3,2,0,1:T(8,128)} %copy-done) | copy-start | bytes 1382404
  56.9 11.0 %collective-permute-start.4 = (f32[2,4,8,32]{3,2,1,0:T(8,128)S(1)}, f32[2,4,8,32]{3,2,1,0:T(8,128)S(1)}, u32[]{:S(2)}, u32[]{:S(2)}) collective-permute-start(f32[2,4,8,32]{3,2,1,0:T(8,128)S(1)} %get-tuple-element.53), channel_id=1, source_target_pairs={{0,128},{128,256},{256,384},{384,0},{1,129},{129,257},{257,385},{3... | collective-permute-start | bytes 24584 | tf_op jit(solution)/shard_map/ppermute | solution.py:205
  60.1 7.9 %collective-permute-start.6 = (f32[2,4,8,32]{3,2,1,0:T(8,128)S(1)}, f32[2,4,8,32]{3,2,1,0:T(8,128)S(1)}, u32[]{:S(2)}, u32[]{:S(2)}) collective-permute-start(f32[2,4,8,32]{3,2,1,0:T(8,128)S(1)} %get-tuple-element.54), channel_id=1, source_target_pairs={{0,384},{128,0},{256,128},{384,256},{1,385},{129,1},{257,129},{385... | collective-permute-start | bytes 24584 | tf_op jit(solution)/shard_map/ppermute | solution.py:205
  63.5 6.2 %collective-permute-start.5 = (f32[2,4,8,32]{3,2,1,0:T(8,128)S(1)}, f32[2,4,8,32]{3,2,1,0:T(8,128)S(1)}, u32[]{:S(2)}, u32[]{:S(2)}) collective-permute-start(f32[2,4,8,32]{3,2,1,0:T(8,128)S(1)} %get-tuple-element.55), channel_id=1, source_target_pairs={{0,256},{128,384},{256,0},{384,128},{1,257},{129,385},{257,1},{385... | collective-permute-start | bytes 24584 | tf_op jit(solution)/shard_map/ppermute | solution.py:205

commit v2 on v1

--- a/solution.py
+++ b/solution.py
@@ -111,6 +111,54 @@
 def advance(current, earlier, force, amplitudes, masks, buoyancy):
     source = amplitudes[:, :, None, None, None] * masks[:, None]
     return 2.0 * current - earlier + time_step_sq * buoyancy * (force + source)
+
+
+def shifted(value, by_x, by_y):
+    count_x = lax.axis_size("gx")
+    count_y = lax.axis_size("gy")
+    pairs = [
+        (i * count_y + j, (i + by_x) * count_y + j + by_y)
+        for i in range(count_x)
+        for j in range(count_y)
+        if 0 <= i + by_x < count_x and 0 <= j + by_y < count_y
+    ]
+    return lax.ppermute(value, ("gx", "gy"), pairs)
+
+
+def exchange(stacked, pairs_lo, pairs_hi):
+    channels, cells_x, cells_y, depth = stacked.shape
+    plane = (cells_y, depth)
+    wide_lo = stacked[:pairs_lo, cells_x - 2 :].reshape((-1,) + plane)
+    thin_lo = stacked[pairs_lo:, cells_x - 1 :].reshape((-1,) + plane)
+    wide_hi = stacked[:pairs_hi, :2].reshape((-1,) + plane)
+    thin_hi = stacked[pairs_hi:, :1].reshape((-1,) + plane)
+    from_lo = shifted(jnp.concatenate([wide_lo, thin_lo]), 1, 0)
+    from_hi = shifted(jnp.concatenate([wide_hi, thin_hi]), -1, 0)
+    from_y_lo = shifted(stacked[:, :, cells_y - 2 :], 0, 1)
+    from_y_hi = shifted(stacked[:, :, :2], 0, -1)
+    corner_ll = shifted(stacked[:, cells_x - 2 :, cells_y - 2 :], 1, 1)
+    corner_lh = shifted(stacked[:, cells_x - 2 :, :2], 1, -1)
+    corner_hl = shifted(stacked[:, :2, cells_y - 2 :], -1, 1)
+    corner_hh = shifted(stacked[:, :2, :2], -1, -1)
+
+    blank = jnp.zeros((channels - pairs_lo, 1) + plane, jnp.float32)
+    rows_lo = jnp.concatenate(
+        [
+            from_lo[: pairs_lo * 2].reshape((pairs_lo, 2) + plane),
+            jnp.concatenate([blank, from_lo[pairs_lo * 2 :].reshape((-1, 1) + plane)], axis=1),
+        ]
+    )
+    blank = jnp.zeros((channels - pairs_hi, 1) + plane, jnp.float32)
+    rows_hi = jnp.concatenate(
+        [
+            from_hi[: pairs_hi * 2].reshape((pairs_hi, 2) + plane),
+            jnp.concatenate([from_hi[pairs_hi * 2 :].reshape((-1, 1) + plane), blank], axis=1),
+        ]
+    )
+    band_lo = jnp.concatenate([corner_ll, rows_lo, corner_lh], axis=2)
+    band_mid = jnp.concatenate([from_y_lo, stacked, from_y_hi], axis=2)
+    band_hi = jnp.concatenate([corner_hl, rows_hi, corner_hh], axis=2)
+    return jnp.concatenate([band_lo, band_mid, band_hi], axis=1)
 
 
 def local(
@@ -136,17 +184,17 @@
     start_x = lax.axis_index("gx") * cells_x
     start_y = lax.axis_index("gy") * cells_y
     grid = (cells_x, cells_y, depth)
-
-    now = jnp.concatenate([fwd_now[None], adj_now]).reshape((fields * 3,) + grid)
-    prev = jnp.concatenate([fwd_prev[None], adj_prev]).reshape((fields * 3,) + grid)
-    moduli = jnp.stack([lame_first, shear_mod, buoyancy])
-    stacked = jnp.concatenate([now, prev, moduli])
-    grown = with_halo(stacked, (("gx", 1), ("gy", 2)), 2)
-    now_grown = grown[: fields * 3].reshape((fields, 3) + grown.shape[1:])
-    prev_grown = grown[fields * 3 : fields * 6].reshape((fields, 3) + grown.shape[1:])
-    lame_grown = zpad(grown[fields * 6])
-    shear_grown = zpad(grown[fields * 6 + 1])
-    buoy_grown = grown[fields * 6 + 2]
+    comps = fields * 3
+
+    now = jnp.concatenate([fwd_now[None], adj_now]).reshape((comps,) + grid)
+    prev = jnp.concatenate([fwd_prev[None], adj_prev]).reshape((comps,) + grid)
+    stacked = jnp.concatenate([now, lame_first[None], shear_mod[None], prev, buoyancy[None]])
+    grown = exchange(stacked, comps + 2, comps)
+    now_grown = grown[:comps].reshape((fields, 3) + grown.shape[1:])
+    lame_grown = zpad(grown[comps])
+    shear_grown = zpad(grown[comps + 1])
+    prev_grown = grown[comps + 2 : 2 * comps + 2].reshape((fields, 3) + grown.shape[1:])
+    buoy_grown = grown[2 * comps + 2]
 
     cells = jnp.concatenate([master_cell, receiver_cell])
     amps = [
@@ -198,13 +246,8 @@
     totals = totals * (1.0 / (STEPS * receivers * groups))
 
     share = depth // groups
-    me = lax.axis_index("grp")
-    kernels = lax.dynamic_slice_in_dim(totals, me * share, share, 3)
-    for shift in range(1, groups):
-        part = lax.dynamic_slice_in_dim(totals, (me + shift) % groups * share, share, 3)
-        kernels = kernels + lax.ppermute(
-            part, "grp", [(i, (i + shift) % groups) for i in range(groups)]
-        )
+    parts = jnp.moveaxis(totals.reshape((2, cells_x, cells_y, groups, share)), 3, 0)
+    kernels = jnp.sum(lax.all_to_all(parts, "grp", 0, 0, tiled=False), axis=0)
     return (final, kernels)
 
 

time: 70.7 us -> 88.2 us (1.25)
  the two profiles are of different devices: /device:TPU:121 before, /device:TPU:448 now
where the time goes in v2:
time: 88.2 us; the launch traced here: 87.5 us
  starting transfers between devices  30.1 us (34%)
  other arithmetic  27.5 us (31%)
  waiting for transfers between devices  14 us (16%)
  local copies, waits for them, and re-layouts  13.2 us (15%)
  between operations  2.73 us (3%)
    ppermute x8, starting transfers between devices, shifted(): return lax.ppermute(value, ('gx', 'gy'), pairs)  25.8 us
    ppermute x8, waiting for transfers between devices, shifted(): return lax.ppermute(value, ('gx', 'gy'), pairs)  12.7 us
    unnamed x43, local copies, waits for them, and re-layouts  7.6 us
    all_to_all x1, starting transfers between devices, local(): kernels = jnp.sum(lax.all_to_all(parts, 'grp', 0, 0, tiled=False), axis=0)  4.29 us
    sub x3, other arithmetic, strains_of(): grad_y = padded[:, :, :span_x + 1, 1:, :span_z + 1] - anchor  3.8 us
    unnamed x6, other arithmetic  3.25 us
    another operation x2, other arithmetic, stencil(): force = jnp.stack([force_x, force_y, force_z], axis=1)  3.04 us
    add x2, other arithmetic, advance(): return 2.0 * current - earlier + time_step_sq * buoyancy * (force + source)  2.28 us
  transfers between devices with their start and end apart: 9, of which 4 were waited for; matrix products, arithmetic and copies ran while one was open for 8% of the time, Pallas kernels for 0%

profile of v2, /device:TPU:448, one launch (start us, length us, event | category | flops | bytes accessed | tf_op | source)
XLA Modules:
  0.0 87.5 jit_solution(11906121091210716609)
XLA Ops:
  1.4 0.9 %pad_maximum_fusion = f32[5,3,4,8,128]{4,3,2,1,0:T(8,128)S(1)} fusion(f32[4,3,4,8,128]{4,3,2,1,0:T(8,128)} %param.16, f32[1,3,4,8,128]{4,3,2,1,0:T(8,128)} %bitcast.243), kind=kLoop, calls=%fused_computation.111 | loop fusion | flops 61440 | bytes 491520 | tf_op jit(solution)/shard_map/concatenate | solution.py:189
  2.5 0.9 %pad_maximum_fusion.1 = f32[5,3,4,8,128]{4,3,2,1,0:T(8,128)S(1)} fusion(f32[4,3,4,8,128]{4,3,2,1,0:T(8,128)} %param.17, f32[1,3,4,8,128]{4,3,2,1,0:T(8,128)} %bitcast.244), kind=kLoop, calls=%fused_computation.112 | loop fusion | flops 61440 | bytes 491520 | tf_op jit(solution)/shard_map/concatenate | solution.py:190
  3.7 4.4 %collective-permute-start.6 = (f32[48,8,128]{2,1,0:T(8,128)S(1)}, f32[48,8,128]{2,1,0:T(8,128)S(1)}, u32[]{:S(2)}, u32[]{:S(2)}) collective-permute-start(f32[48,8,128]{2,1,0:T(8,128)S(1)} %pad_maximum_fusion.3), channel_id=1, source_target_pairs={{8,0},{9,1},{10,2},{11,3},{12,4},{13,5},{14,6},{15,7},{16,8},{17,9... | collective-permute-start | bytes 589832 | tf_op jit(solution)/shard_map/ppermute | solution.py:125
  8.4 1.9 %collective-permute-start.1 = (f32[50,8,128]{2,1,0:T(8,128)S(1)}, f32[50,8,128]{2,1,0:T(8,128)S(1)}, u32[]{:S(2)}, u32[]{:S(2)}) collective-permute-start(f32[50,8,128]{2,1,0:T(8,128)S(1)} %pad_maximum_fusion.2), channel_id=1, source_target_pairs={{0,8},{1,9},{2,10},{3,11},{4,12},{5,13},{6,14},{7,15},{8,16},{9,17... | collective-permute-start | bytes 614408 | tf_op jit(solution)/shard_map/ppermute | solution.py:125
  10.6 1.9 %collective-permute-start = (f32[33,2,2,128]{3,1,2,0:T(2,128)S(1)}, f32[33,2,2,128]{3,1,2,0:T(2,128)S(1)}, u32[]{:S(2)}, u32[]{:S(2)}) collective-permute-start(f32[33,2,2,128]{3,1,2,0:T(2,128)S(1)} %get-tuple-element.45), channel_id=1, source_target_pairs={{0,9},{1,10},{2,11},{3,12},{4,13},{5,14},{6,15},{8,17},{9,18},{10,... | collective-permute-start | bytes 202760 | tf_op jit(solution)/shard_map/ppermute | solution.py:125
  12.5 1.9 %collective-permute-start.3 = (f32[33,4,2,128]{3,1,2,0:T(4,128)S(1)}, f32[33,4,2,128]{3,1,2,0:T(4,128)S(1)}, u32[]{:S(2)}, u32[]{:S(2)}) collective-permute-start(f32[33,4,2,128]{3,1,2,0:T(4,128)S(1)} %get-tuple-element.49), channel_id=1, source_target_pairs={{0,1},{1,2},{2,3},{3,4},{4,5},{5,6},{6,7},{8,9},{9,10},{10,11},{11... | collective-permute-start | bytes 405512 | tf_op jit(solution)/shard_map/ppermute | solution.py:125
  14.4 4.1 %collective-permute-start.4 = (f32[33,4,2,128]{3,1,2,0:T(4,128)S(1)}, f32[33,4,2,128]{3,1,2,0:T(4,128)S(1)}, u32[]{:S(2)}, u32[]{:S(2)}) collective-permute-start(f32[33,4,2,128]{3,1,2,0:T(4,128)S(1)} %get-tuple-element.50), channel_id=1, source_target_pairs={{1,0},{2,1},{3,2},{4,3},{5,4},{6,5},{7,6},{9,8},{10,9},{11,10},{12... | collective-permute-start | bytes 405512 | tf_op jit(solution)/shard_map/ppermute | solution.py:125
  22.1 3.0 %collective-permute-done = f32[33,2,2,128]{3,1,2,0:T(2,128)S(1)} collective-permute-done((f32[33,2,2,128]{3,1,2,0:T(2,128)S(1)}, f32[33,2,2,128]{3,1,2,0:T(2,128)S(1)}, u32[]{:S(2)}, u32[]{:S(2)}) %collective-permute-start) | collective-permute-done | bytes 67616 | tf_op jit(solution)/shard_map/ppermute | solution.py:125
  25.1 5.0 %collective-permute-start.7 = (f32[33,2,2,128]{3,1,2,0:T(2,128)S(1)}, f32[33,2,2,128]{3,1,2,0:T(2,128)S(1)}, u32[]{:S(2)}, u32[]{:S(2)}) collective-permute-start(f32[33,2,2,128]{3,1,2,0:T(2,128)S(1)} %get-tuple-element.46), channel_id=1, source_target_pairs={{9,0},{10,1},{11,2},{12,3},{13,4},{14,5},{15,6},{17,8},{18,9},{19,... | collective-permute-start | bytes 202760 | tf_op jit(solution)/shard_map/ppermute | solution.py:125
  30.1 4.5 %collective-permute-start.5 = (f32[33,2,2,128]{3,1,2,0:T(2,128)S(1)}, f32[33,2,2,128]{3,1,2,0:T(2,128)S(1)}, u32[]{:S(2)}, u32[]{:S(2)}) collective-permute-start(f32[33,2,2,128]{3,1,2,0:T(2,128)S(1)} %get-tuple-element.47), channel_id=1, source_target_pairs={{8,1},{9,2},{10,3},{11,4},{12,5},{13,6},{14,7},{16,9},{17,10},{18,... | collective-permute-start | bytes 202760 | tf_op jit(solution)/shard_map/ppermute | solution.py:125
  34.7 1.9 %collective-permute-start.2 = (f32[33,2,2,128]{3,1,2,0:T(2,128)S(1)}, f32[33,2,2,128]{3,1,2,0:T(2,128)S(1)}, u32[]{:S(2)}, u32[]{:S(2)}) collective-permute-start(f32[33,2,2,128]{3,1,2,0:T(2,128)S(1)} %get-tuple-element.48), channel_id=1, source_target_pairs={{1,8},{2,9},{3,10},{4,11},{5,12},{6,13},{7,14},{9,16},{10,17},{11,... | collective-permute-start | bytes 202760 | tf_op jit(solution)/shard_map/ppermute | solution.py:125
  37.3 9.4 %collective-permute-done.2 = f32[33,2,2,128]{3,1,2,0:T(2,128)S(1)} collective-permute-done((f32[33,2,2,128]{3,1,2,0:T(2,128)S(1)}, f32[33,2,2,128]{3,1,2,0:T(2,128)S(1)}, u32[]{:S(2)}, u32[]{:S(2)}) %collective-permute-start.2) | collective-permute-done | bytes 67616 | tf_op jit(solution)/shard_map/ppermute | solution.py:125
  46.6 1.7 %fusion.8 = f32[33,8,12,128]{3,1,2,0:T(8,128)S(1)} fusion(f32[18,1,8,128]{3,1,2,0:T(1,128)S(1)} %bitcast.237, f32[16,1,8,128]{3,1,2,0:T(1,128)S(1)} %bitcast.240, f32[33,2,2,128]{3,1,2,0:T(2,128)S(1)} %collective-permute-done.7, f32[15,2,8,128]{3,1,2,0:T(2,128)S(1)} %copy.302, f32[33,2,2,128]{3,1,2,0:T(2,128)S(1)} %collective-permute-done.5, ...), kind=kLoop, calls=%fused_computation.20 | loop fusion | flops 11354112 | bytes 3104768 | tf_op jit(solution)/shard_map/concatenate | solution.py:161
  50.0 2.4 %fusion.5 = (f32[5,3,7,11,129]{4,3,2,0,1:T(8,128)S(1)}, f32[5,3,7,11,129]{4,3,2,0,1:T(8,128)S(1)}, f32[5,3,7,11,129]{4,3,2,0,1:T(8,128)S(1)}, f32[5,3,7,11,129]{4,3,2,0,1:T(8,128)S(1)}) fusion(f32[5,3,8,12,128]{4,3,2,0,1:T(8,128)S(1)} %copy.303), kind=kLoop, calls=%fused_computation.15 | loop fusion | flops 297990 | bytes 3121200 | tf_op jit(solution)/shard_map/sub | solution.py:46
  53.8 0.9 %fusion.39 = (f32[5,1,6,10,128]{4,3,2,0,1:T(8,128)S(1)}, f32[5,1,6,10,128]{4,3,2,0,1:T(8,128)S(1)}, f32[5,1,6,10,128]{4,3,2,0,1:T(8,128)S(1)}) fusion(f32[5,7,11,129]{3,2,1,0:T(8,128)S(1)} %get-tuple-element.23, f32[5,7,11,129]{3,2,1,0:T(8,128)S(1)} %get-tuple-element.22, f32[5,7,11,129]{3,2,1,0:T(8,128)S(1)} %get-tuple-element.20, ...), kind=kLoop, calls=%fused_computation.107 | loop fusion | flops 576000 | bytes 2764800 | tf_op jit(solution)/shard_map/stack | solution.py:80
  55.9 0.9 %bitcast_dynamic-update-slice_fusion.1 = f32[5,6,7,11,129]{4,3,2,1,0:T(8,128)} fusion(f32[5,3,7,11,129]{4,3,2,0,1:T(8,128)S(1)} %get-tuple-element.36), kind=kLoop, calls=%fused_computation.53 | loop fusion | bytes 772100
  61.3 1.3 %fusion.15 = (f32[4,3,5,9,129]{4,3,2,0,1:T(8,128)S(1)}, f32[4,3,5,9,129]{4,3,2,0,1:T(8,128)S(1)}, f32[4,3,5,9,129]{4,3,2,0,1:T(8,128)S(1)}) fusion(f32[4,3,6,10,128]{4,3,2,0,1:T(8,128)S(1)} %slice-done), kind=kLoop, calls=%fused_computation.32 | loop fusion | flops 208980 | bytes 1204560 | tf_op jit(solution)/shard_map/sub | solution.py:46
  62.7 1.3 %fusion.30 = (f32[4,5,9,129]{3,2,1,0:T(8,128)}, f32[4,5,9,129]{3,2,1,0:T(8,128)S(1)}, f32[4,5,9,129]{3,2,1,0:T(8,128)}, f32[4,5,9,129]{3,2,1,0:T(8,128)}, f32[4,5,9,129]{3,2,1,0:T(8,128)}) fusion(f32[4,3,5,9,129]{4,3,2,0,1:T(8,128)S(1)} %get-tuple-element.41, f32[5,9,129]{2,1,0:T(8,128)S(1)} %copy.322, f32[4,3,5,9,129]{4,3,2,0,1:T(8,128)S(1)} %get-tuple-element.40, ...), kind=kLoop, calls=%fused_computation.83 | loop fusion | flops 255420 | bytes 1369980 | tf_op jit(solution)/shard_map/add | solution.py:65
  64.0 1.0 %fusion.29 = (f32[4,5,9,129]{3,2,1,0:T(8,128)}, f32[4,5,9,129]{3,2,1,0:T(8,128)}) fusion(f32[4,5,9,129]{3,2,1,0:T(8,128)S(1)} %get-tuple-element.19, f32[4,3,5,9,129]{4,3,2,0,1:T(8,128)S(1)} %get-tuple-element.39, f32[5,9,129]{2,1,0:T(8,128)S(1)} %copy.322, f32[4,3,5,9,129]{4,3,2,0,1:T(8,128)S(1)} %get-tuple-element.40), kind=kLoop, calls=%fused_computation.81 | loop fusion | flops 92880 | bytes 487620 | tf_op jit(solution)/shard_map/add | solution.py:66
  66.2 0.9 bitcast_dynamic-update-slice_fusion
  67.1 0.9 slice_dynamic-update-slice_fusion
  67.9 0.9 %multiply_dynamic-update-slice_fusion.1 = f32[5,6,7,11,129]{4,3,2,1,0:T(8,128)} fusion(f32[5,6,7,11,129]{4,3,2,1,0:T(8,128)} %slice_dynamic-update-slice_fusion, f32[5,3,7,11,129]{4,3,2,0,1:T(8,128)S(1)} %copy-done.1, f32[5,3,7,11,129]{4,3,2,0,1:T(8,128)S(1)} %get-tuple-element.33), kind=kLoop, calls=%fused_computation.63 | loop fusion | flops 99330 | bytes 970760
  68.9 0.9 %fusion.24 = f32[5,6,7,11,129]{4,3,2,1,0:T(8,128)} fusion(f32[5,6,7,11,129]{4,3,2,1,0:T(8,128)} %multiply_dynamic-update-slice_fusion.1, f32[5,3,7,11,129]{4,3,2,0,1:T(8,128)S(1)} %copy-done.1, f32[5,3,7,11,129]{4,3,2,1,0:T(8,128)S(1)} %copy_subtract_fusion), kind=kLoop, calls=%fused_computation.51 | loop fusion | flops 99330 | bytes 970760
  69.8 0.9 %multiply_dynamic-update-slice_fusion = f32[5,6,7,11,129]{4,3,2,1,0:T(8,128)} fusion(f32[5,6,7,11,129]{4,3,2,1,0:T(8,128)} %fusion.24, f32[5,3,7,11,129]{4,3,2,0,1:T(8,128)S(1)} %get-tuple-element.33, f32[5,3,7,11,129]{4,3,2,1,0:T(8,128)S(1)} %copy_subtract_fusion), kind=kLoop, calls=%fused_computation.62 | loop fusion | flops 99330 | bytes 970760 | tf_op jit(solution)/shard_map/stack | solution.py:81
  70.7 1.6 %slice_reduce_fusion.1 = f32[6,4,8,128]{3,2,1,0:T(8,128)S(1)} fusion(f32[5,6,7,11,129]{4,3,2,1,0:T(8,128)} %multiply_dynamic-update-slice_fusion), kind=kLoop, calls=%fused_computation.66 | loop fusion | flops 73728 | bytes 491520 | tf_op jit(solution)/shard_map/reduce_sum | solution.py:242
  72.4 1.3 %fusion.47 = (f32[4,8,128]{2,1,0:T(8,128)S(1)}, f32[4,8,128]{2,1,0:T(8,128)S(1)}) fusion(f32[6,4,8,128]{3,2,1,0:T(8,128)S(1)} %slice_reduce_fusion, f32[1,6,5,9,129]{4,3,2,0,1:T(8,128)} %fusion.53, f32[6]{0:T(128)S(1)} %copy-done.10, f32[6,4,8,128]{3,2,1,0:T(8,128)S(1)} %slice_reduce_fusion.1, f32[5,6,7,11,129]{4,3,2,1,0:T(8,128)} %multiply_dynamic-update-slice_fusion), kind=kLoop, calls=%fused_computation.133 | loop fusion | flops 139264 | bytes 426008 | tf_op jit(solution)/shard_map/reduce_sum | solution.py:244
  74.0 0.9 %fusion.44 = f32[4,2,4,8,32]{4,0,3,2,1:T(4,128)S(1)} fusion(f32[1,4,8,4,32]{4,3,2,1,0:T(4,128)S(1)} %mul.355, f32[1,4,8,4,32]{4,3,2,1,0:T(4,128)S(1)} %stack.65, f32[1,4,8,4,32]{4,3,2,1,0:T(4,128)S(1)} %mul.366, f32[1,4,8,4,32]{4,3,2,1,0:T(4,128)} %stack.68), kind=kLoop, calls=%fused_computation.125 | loop fusion | flops 32768 | bytes 98304 | tf_op jit(solution)/shard_map/transpose | solution.py:249
  75.0 0.8 reshape.482
  75.8 4.3 %all-to-all-start = ((f32[4,1,2048]{2,1,0:T(1,128)}), f32[4,1,2048]{2,1,0:T(1,128)S(1)}, u32[]{:S(2)}, u32[]{:S(2)}) async-start(f32[4,1,2048]{2,1,0:T(1,128)} %reshape.482), calls=%async_computation | async-start | bytes 65536 | tf_op jit(solution)/shard_map/all_to_all | solution.py:250
  80.0 2.1 %fusion.69 = (f32[4,1,4,8,128]{4,3,2,1,0:T(8,128)S(1)}, f32[4,1,4,8,128]{4,3,2,1,0:T(8,128)S(1)}, f32[4,1,4,8,128]{4,3,2,1,0:T(8,128)S(1)}) fusion(f32[4,5,9,129]{3,2,1,0:T(8,128)} %get-tuple-element.26, f32[4,5,9,129]{3,2,1,0:T(8,128)} %get-tuple-element.25, f32[4,5,9,129]{3,2,1,0:T(8,128)} %get-tuple-element.18, f32[4,5,9,129]{3,2,1,0:T(8,128)} %get-tuple-element.27, ...), kind=kLoop, calls=%fused_computation.172 | loop fusion | flops 245760 | bytes 1179648 | tf_op jit(solution)/shard_map/stack | solution.py:80
  82.2 2.0 %fusion.42 = f32[4,3,4,8,128]{4,3,2,1,0:T(8,128)} fusion(f32[4,1,4,8,128]{4,3,2,1,0:T(8,128)S(1)} %get-tuple-element.55, f32[4,1,4,8,128]{4,3,2,1,0:T(8,128)S(1)} %get-tuple-element.54, f32[4,1,4,8,128]{4,3,2,1,0:T(8,128)S(1)} %get-tuple-element.53, f32[4,3,4,8,128]{4,2,3,1,0:T(4,128)} %slice.557, f32[4,4,8,128]{3,2,1,0:T(8,128)} %slice.584, ...), kind=kLoop, calls=%fused_computation.118 | loop fusion | flops 393216 | bytes 870400 | tf_op jit(solution)/shard_map/add | solution.py:113
  84.2 1.3 %all-to-all-done = f32[4,1,2048]{2,1,0:T(1,128)S(1)} async-done(((f32[4,1,2048]{2,1,0:T(1,128)}), f32[4,1,2048]{2,1,0:T(1,128)S(1)}, u32[]{:S(2)}, u32[]{:S(2)}) %all-to-all-start) | async-done | bytes 32800 | tf_op jit(solution)/shard_map/all_to_all | solution.py:250
  (128 shorter events, 16.5 us)
Async XLA Ops:
  0.6 2.9 %copy-start.7 = (f32[4,8,128]{2,1,0:T(8,128)S(1)}, f32[4,8,128]{2,1,0:T(8,128)}, u32[]{:S(2)}) copy-start(f32[4,8,128]{2,1,0:T(8,128)} %param.19) | copy-start | bytes 49156
  0.6 2.9 %copy-start.6 = (f32[4,8,128]{2,1,0:T(8,128)S(1)}, f32[4,8,128]{2,1,0:T(8,128)}, u32[]{:S(2)}) copy-start(f32[4,8,128]{2,1,0:T(8,128)} %param.18) | copy-start | bytes 49156
  3.5 6.9 %copy-start.5 = (f32[4,8,128]{2,1,0:T(8,128)S(1)}, f32[4,8,128]{2,1,0:T(8,128)}, u32[]{:S(2)}) copy-start(f32[4,8,128]{2,1,0:T(8,128)} %param.20) | copy-start | bytes 49156
  3.7 16.2 %copy-start.11 = (s32[4]{0:T(128)S(1)}, s32[4]{0:T(128)}, u32[]{:S(2)}) copy-start(s32[4]{0:T(128)} %param.24) | copy-start | bytes 52
  3.7 16.4 %copy-start.12 = (s32[4]{0:T(128)S(1)}, s32[4]{0:T(128)}, u32[]{:S(2)}) copy-start(s32[4]{0:T(128)} %param.25) | copy-start | bytes 52
  3.7 26.4 %collective-permute-start.6 = (f32[48,8,128]{2,1,0:T(8,128)S(1)}, f32[48,8,128]{2,1,0:T(8,128)S(1)}, u32[]{:S(2)}, u32[]{:S(2)}) collective-permute-start(f32[48,8,128]{2,1,0:T(8,128)S(1)} %pad_maximum_fusion.3), channel_id=1, source_target_pairs={{8,0},{9,1},{10,2},{11,3},{12,4},{13,5},{14,6},{15,7},{16,8},{17,9... | collective-permute-start | bytes 589832 | tf_op jit(solution)/shard_map/ppermute | solution.py:125
  8.2 12.3 %copy-start.8 = (f32[4,256,3]{1,0,2:T(4,128)S(1)}, f32[4,256,3]{1,0,2:T(4,128)}, u32[]{:S(2)}) copy-start(f32[4,256,3]{1,0,2:T(4,128)} %param.26) | copy-start | bytes 36868
  8.2 12.4 %copy-start.9 = (f32[256,3]{0,1:T(4,128)S(1)}, f32[256,3]{0,1:T(4,128)}, u32[]{:S(2)}) copy-start(f32[256,3]{0,1:T(4,128)} %param.23) | copy-start | bytes 9220
  8.4 26.3 %collective-permute-start.1 = (f32[50,8,128]{2,1,0:T(8,128)S(1)}, f32[50,8,128]{2,1,0:T(8,128)S(1)}, u32[]{:S(2)}, u32[]{:S(2)}) collective-permute-start(f32[50,8,128]{2,1,0:T(8,128)S(1)} %pad_maximum_fusion.2), channel_id=1, source_target_pairs={{0,8},{1,9},{2,10},{3,11},{4,12},{5,13},{6,14},{7,15},{8,16},{9,17... | collective-permute-start | bytes 614408 | tf_op jit(solution)/shard_map/ppermute | solution.py:125
  10.6 14.5 %collective-permute-start = (f32[33,2,2,128]{3,1,2,0:T(2,128)S(1)}, f32[33,2,2,128]{3,1,2,0:T(2,128)S(1)}, u32[]{:S(2)}, u32[]{:S(2)}) collective-permute-start(f32[33,2,2,128]{3,1,2,0:T(2,128)S(1)} %get-tuple-element.45), channel_id=1, source_target_pairs={{0,9},{1,10},{2,11},{3,12},{4,13},{5,14},{6,15},{8,17},{9,18},{10,... | collective-permute-start | bytes 202760 | tf_op jit(solution)/shard_map/ppermute | solution.py:125
  12.5 34.1 %collective-permute-start.3 = (f32[33,4,2,128]{3,1,2,0:T(4,128)S(1)}, f32[33,4,2,128]{3,1,2,0:T(4,128)S(1)}, u32[]{:S(2)}, u32[]{:S(2)}) collective-permute-start(f32[33,4,2,128]{3,1,2,0:T(4,128)S(1)} %get-tuple-element.49), channel_id=1, source_target_pairs={{0,1},{1,2},{2,3},{3,4},{4,5},{5,6},{6,7},{8,9},{9,10},{10,11},{11... | collective-permute-start | bytes 405512 | tf_op jit(solution)/shard_map/ppermute | solution.py:125
  14.4 32.2 %collective-permute-start.4 = (f32[33,4,2,128]{3,1,2,0:T(4,128)S(1)}, f32[33,4,2,128]{3,1,2,0:T(4,128)S(1)}, u32[]{:S(2)}, u32[]{:S(2)}) collective-permute-start(f32[33,4,2,128]{3,1,2,0:T(4,128)S(1)} %get-tuple-element.50), channel_id=1, source_target_pairs={{1,0},{2,1},{3,2},{4,3},{5,4},{6,5},{7,6},{9,8},{10,9},{11,10},{12... | collective-permute-start | bytes 405512 | tf_op jit(solution)/shard_map/ppermute | solution.py:125
  20.5 27.9 %copy-start.3 = (f32[5,6,10,128]{3,2,1,0:T(8,128)}, f32[5,6,10,128]{3,2,1,0:T(8,128)S(1)}, u32[]{:S(2)}) copy-start(f32[5,6,10,128]{3,2,1,0:T(8,128)S(1)} %and_convert_fusion) | copy-start | bytes 460804
  25.1 11.8 %collective-permute-start.7 = (f32[33,2,2,128]{3,1,2,0:T(2,128)S(1)}, f32[33,2,2,128]{3,1,2,0:T(2,128)S(1)}, u32[]{:S(2)}, u32[]{:S(2)}) collective-permute-start(f32[33,2,2,128]{3,1,2,0:T(2,128)S(1)} %get-tuple-element.46), channel_id=1, source_target_pairs={{9,0},{10,1},{11,2},{12,3},{13,4},{14,5},{15,6},{17,8},{18,9},{19,... | collective-permute-start | bytes 202760 | tf_op jit(solution)/shard_map/ppermute | solution.py:125
  30.1 7.2 %collective-permute-start.5 = (f32[33,2,2,128]{3,1,2,0:T(2,128)S(1)}, f32[33,2,2,128]{3,1,2,0:T(2,128)S(1)}, u32[]{:S(2)}, u32[]{:S(2)}) collective-permute-start(f32[33,2,2,128]{3,1,2,0:T(2,128)S(1)} %get-tuple-element.47), channel_id=1, source_target_pairs={{8,1},{9,2},{10,3},{11,4},{12,5},{13,6},{14,7},{16,9},{17,10},{18,... | collective-permute-start | bytes 202760 | tf_op jit(solution)/shard_map/ppermute | solution.py:125
  34.7 12.0 %collective-permute-start.2 = (f32[33,2,2,128]{3,1,2,0:T(2,128)S(1)}, f32[33,2,2,128]{3,1,2,0:T(2,128)S(1)}, u32[]{:S(2)}, u32[]{:S(2)}) collective-permute-start(f32[33,2,2,128]{3,1,2,0:T(2,128)S(1)} %get-tuple-element.48), channel_id=1, source_target_pairs={{1,8},{2,9},{3,10},{4,11},{5,12},{6,13},{7,14},{9,16},{10,17},{11,... | collective-permute-start | bytes 202760 | tf_op jit(solution)/shard_map/ppermute | solution.py:125
  52.5 2.8 %copy-start = (f32[5,3,7,11,129]{4,3,2,0,1:T(8,128)}, f32[5,3,7,11,129]{4,3,2,0,1:T(8,128)S(1)}, u32[]{:S(2)}) copy-start(f32[5,3,7,11,129]{4,3,2,0,1:T(8,128)S(1)} %get-tuple-element.36) | copy-start | bytes 1787944
  53.8 0.9 %copy-start.4 = (f32[5,6,10,128]{3,2,1,0:T(8,128)S(1)}, f32[5,6,10,128]{3,2,1,0:T(8,128)}, u32[]{:S(2)}) copy-start(f32[5,6,10,128]{3,2,1,0:T(8,128)} %copy-done.3) | copy-start | bytes 460804
  55.0 0.9 %copy-start.2 = (f32[5,3,6,10,128]{4,3,2,0,1:T(8,128)}, f32[5,3,6,10,128]{4,3,2,0,1:T(8,128)S(1)}, u32[]{:S(2)}) copy-start(f32[5,3,6,10,128]{4,3,2,0,1:T(8,128)S(1)} %fusion.18) | copy-start | bytes 1382404
  56.8 4.5 %slice-start = ((f32[5,3,6,10,128]{4,3,2,0,1:T(8,128)}), f32[4,3,6,10,128]{4,3,2,0,1:T(8,128)S(1)}, s32[]{:S(2)}) async-start(f32[5,3,6,10,128]{4,3,2,0,1:T(8,128)} %copy-done.2), calls=%async_computation.1 | async-start | bytes 1179648 | tf_op jit(solution)/shard_map/slice | solution.py:227
  66.2 1.7 %copy-start.1 = (f32[5,3,7,11,129]{4,3,2,0,1:T(8,128)S(1)}, f32[5,3,7,11,129]{4,3,2,0,1:T(8,128)}, u32[]{:S(2)}) copy-start(f32[5,3,7,11,129]{4,3,2,0,1:T(8,128)} %copy-done) | copy-start | bytes 1787944
  68.9 3.5 %copy-start.10 = (f32[6]{0:T(128)S(1)}, f32[6]{0:T(128)}, u32[]{:S(2)}) copy-start(f32[6]{0:T(128)} %constant.97.clone) | copy-start | bytes 76
  75.8 9.7 %all-to-all-start = ((f32[4,1,2048]{2,1,0:T(1,128)}), f32[4,1,2048]{2,1,0:T(1,128)S(1)}, u32[]{:S(2)}, u32[]{:S(2)}) async-start(f32[4,1,2048]{2,1,0:T(1,128)} %reshape.482), calls=%async_computation | async-start | bytes 65536 | tf_op jit(solution)/shard_map/all_to_all | solution.py:250

commit v3 on v1

--- a/solution.py
+++ b/solution.py
@@ -198,13 +198,8 @@
     totals = totals * (1.0 / (STEPS * receivers * groups))
 
     share = depth // groups
-    me = lax.axis_index("grp")
-    kernels = lax.dynamic_slice_in_dim(totals, me * share, share, 3)
-    for shift in range(1, groups):
-        part = lax.dynamic_slice_in_dim(totals, (me + shift) % groups * share, share, 3)
-        kernels = kernels + lax.ppermute(
-            part, "grp", [(i, (i + shift) % groups) for i in range(groups)]
-        )
+    parts = jnp.moveaxis(totals.reshape((2, cells_x, cells_y, groups, share)), 3, 0)
+    kernels = jnp.sum(lax.all_to_all(parts, "grp", 0, 0, tiled=False), axis=0)
     return (final, kernels)
 
 

time: 70.7 us -> 84.4 us (1.19)
  the two profiles are of different devices: /device:TPU:121 before, /device:TPU:123 now
where the time goes in v3:
time: 84.4 us; the launch traced here: 83.9 us
  other arithmetic  26.3 us (31%)
  starting transfers between devices  25.9 us (31%)
  waiting for transfers between devices  17.1 us (20%)
  local copies, waits for them, and re-layouts  12.2 us (14%)
  between operations  2.51 us (3%)
    ppermute x2, starting transfers between devices, with_halo(): lax.ppermute(tail, axis, [(i, i + 1) for i in range(ends)])  17.8 us
    ppermute x2, waiting for transfers between devices, with_halo(): lax.ppermute(head, axis, [(i + 1, i) for i in range(ends)])  15.5 us
    unnamed x38, local copies, waits for them, and re-layouts  6.85 us
    all_to_all x1, starting transfers between devices, local(): kernels = jnp.sum(lax.all_to_all(parts, 'grp', 0, 0, tiled=False), axis=0)  4.26 us
    ppermute x2, starting transfers between devices, with_halo(): lax.ppermute(head, axis, [(i + 1, i) for i in range(ends)])  3.84 us
    sub x3, other arithmetic, strains_of(): grad_y = padded[:, :, :span_x + 1, 1:, :span_z + 1] - anchor  3.8 us
    unnamed x6, other arithmetic  3.23 us
    another operation x2, other arithmetic, stencil(): force = jnp.stack([force_x, force_y, force_z], axis=1)  3.15 us
  transfers between devices with their start and end apart: 5, of which 4 were waited for; matrix products, arithmetic and copies ran while one was open for 8% of the time, Pallas kernels for 0%

profile of v3, /device:TPU:123, one launch (start us, length us, event | category | flops | bytes accessed | tf_op | source)
XLA Modules:
  0.0 83.9 jit_solution(4891707681816713136)
XLA Ops:
  0.7 1.0 %pad_maximum_fusion.4 = f32[5,3,4,8,128]{4,3,2,1,0:T(8,128)S(1)} fusion(f32[4,3,4,8,128]{4,3,2,1,0:T(8,128)} %param.16, f32[1,3,4,8,128]{4,3,2,1,0:T(8,128)} %bitcast.214), kind=kLoop, calls=%fused_computation.95 | loop fusion | flops 61440 | bytes 491520 | tf_op jit(solution)/shard_map/concatenate | solution.py:140
  1.7 1.0 %pad_maximum_fusion.5 = f32[5,3,4,8,128]{4,3,2,1,0:T(8,128)S(1)} fusion(f32[4,3,4,8,128]{4,3,2,1,0:T(8,128)} %param.17, f32[1,3,4,8,128]{4,3,2,1,0:T(8,128)} %bitcast.215), kind=kLoop, calls=%fused_computation.96 | loop fusion | flops 61440 | bytes 491520 | tf_op jit(solution)/shard_map/concatenate | solution.py:141
  3.2 8.9 %collective-permute-start = (f32[33,2,8,128]{3,1,2,0:T(2,128)S(1)}, f32[33,2,8,128]{3,1,2,0:T(2,128)S(1)}, u32[]{:S(2)}, u32[]{:S(2)}) collective-permute-start(f32[33,2,8,128]{3,1,2,0:T(2,128)S(1)} %get-tuple-element.45), channel_id=1, source_target_pairs={{0,8},{8,16},{16,24},{24,32},{32,40},{40,48},{48,56},{56,64},{64,7... | collective-permute-start | bytes 811016 | tf_op jit(solution)/shard_map/ppermute | solution.py:20
  12.1 1.9 %collective-permute-start.1 = (f32[33,2,8,128]{3,1,2,0:T(2,128)S(1)}, f32[33,2,8,128]{3,1,2,0:T(2,128)S(1)}, u32[]{:S(2)}, u32[]{:S(2)}) collective-permute-start(f32[33,2,8,128]{3,1,2,0:T(2,128)S(1)} %get-tuple-element.46), channel_id=1, source_target_pairs={{8,0},{16,8},{24,16},{32,24},{40,32},{48,40},{56,48},{64,56},{72,6... | collective-permute-start | bytes 811016 | tf_op jit(solution)/shard_map/ppermute | solution.py:22
  16.1 0.7 copy.239
  16.8 1.0 %collective-permute-done = f32[33,2,8,128]{3,1,2,0:T(2,128)S(1)} collective-permute-done((f32[33,2,8,128]{3,1,2,0:T(2,128)S(1)}, f32[33,2,8,128]{3,1,2,0:T(2,128)S(1)}, u32[]{:S(2)}, u32[]{:S(2)}) %collective-permute-start) | collective-permute-done | bytes 270368 | tf_op jit(solution)/shard_map/ppermute | solution.py:20
  17.8 11.1 %collective-permute-done.1 = f32[33,2,8,128]{3,1,2,0:T(2,128)S(1)} collective-permute-done((f32[33,2,8,128]{3,1,2,0:T(2,128)S(1)}, f32[33,2,8,128]{3,1,2,0:T(2,128)S(1)}, u32[]{:S(2)}, u32[]{:S(2)}) %collective-permute-start.1) | collective-permute-done | bytes 270368 | tf_op jit(solution)/shard_map/ppermute | solution.py:22
  29.1 8.9 %collective-permute-start.2 = (f32[33,8,2,128]{3,1,2,0:T(8,128)S(1)}, f32[33,8,2,128]{3,1,2,0:T(8,128)S(1)}, u32[]{:S(2)}, u32[]{:S(2)}) collective-permute-start(f32[33,8,2,128]{3,1,2,0:T(8,128)S(1)} %get-tuple-element.31), channel_id=1, source_target_pairs={{0,1},{1,2},{2,3},{3,4},{4,5},{5,6},{6,7},{8,9},{9,10},{10,11},{11... | collective-permute-start | bytes 811016 | tf_op jit(solution)/shard_map/ppermute | solution.py:20
  38.0 1.9 %collective-permute-start.3 = (f32[33,8,2,128]{3,1,2,0:T(8,128)S(1)}, f32[33,8,2,128]{3,1,2,0:T(8,128)S(1)}, u32[]{:S(2)}, u32[]{:S(2)}) collective-permute-start(f32[33,8,2,128]{3,1,2,0:T(8,128)S(1)} %get-tuple-element.32), channel_id=1, source_target_pairs={{1,0},{2,1},{3,2},{4,3},{5,4},{6,5},{7,6},{9,8},{10,9},{11,10},{12... | collective-permute-start | bytes 811016 | tf_op jit(solution)/shard_map/ppermute | solution.py:22
  41.4 4.4 %collective-permute-done.3 = f32[33,8,2,128]{3,1,2,0:T(8,128)S(1)} collective-permute-done((f32[33,8,2,128]{3,1,2,0:T(8,128)S(1)}, f32[33,8,2,128]{3,1,2,0:T(8,128)S(1)}, u32[]{:S(2)}, u32[]{:S(2)}) %collective-permute-start.3) | collective-permute-done | bytes 270368 | tf_op jit(solution)/shard_map/ppermute | solution.py:22
  46.6 0.8 slice.502
  47.7 2.4 %fusion.1 = (f32[5,3,7,11,129]{4,3,2,0,1:T(8,128)S(1)}, f32[5,3,7,11,129]{4,3,2,0,1:T(8,128)S(1)}, f32[5,3,7,11,129]{4,3,2,0,1:T(8,128)S(1)}, f32[5,3,7,11,129]{4,3,2,0,1:T(8,128)S(1)}) fusion(f32[5,3,8,12,128]{4,3,2,0,1:T(8,128)S(1)} %copy.216), kind=kLoop, calls=%fused_computation.9 | loop fusion | flops 297990 | bytes 3121200 | tf_op jit(solution)/shard_map/sub | solution.py:46
  50.5 0.7 fusion.14
  51.4 0.9 %fusion.27 = (f32[5,1,6,10,128]{4,3,2,0,1:T(8,128)S(1)}, f32[5,1,6,10,128]{4,3,2,0,1:T(8,128)S(1)}, f32[5,1,6,10,128]{4,3,2,0,1:T(8,128)S(1)}) fusion(f32[5,7,11,129]{3,2,1,0:T(8,128)S(1)} %get-tuple-element.21, f32[5,7,11,129]{3,2,1,0:T(8,128)S(1)} %get-tuple-element.20, f32[5,7,11,129]{3,2,1,0:T(8,128)S(1)} %get-tuple-element.18, ...), kind=kLoop, calls=%fused_computation.91 | loop fusion | flops 576000 | bytes 2764800 | tf_op jit(solution)/shard_map/stack | solution.py:80
  53.6 0.9 %bitcast_dynamic-update-slice_fusion.1 = f32[5,6,7,11,129]{4,3,2,1,0:T(8,128)} fusion(f32[5,3,7,11,129]{4,3,2,0,1:T(8,128)S(1)} %get-tuple-element.36), kind=kLoop, calls=%fused_computation.34 | loop fusion | bytes 772100
  58.9 1.3 %fusion.3 = (f32[4,3,5,9,129]{4,3,2,0,1:T(8,128)S(1)}, f32[4,3,5,9,129]{4,3,2,0,1:T(8,128)S(1)}, f32[4,3,5,9,129]{4,3,2,0,1:T(8,128)S(1)}) fusion(f32[4,3,6,10,128]{4,3,2,0,1:T(8,128)S(1)} %slice-done), kind=kLoop, calls=%fused_computation.13 | loop fusion | flops 208980 | bytes 1204560 | tf_op jit(solution)/shard_map/sub | solution.py:46
  60.3 1.3 %fusion.18 = (f32[4,5,9,129]{3,2,1,0:T(8,128)}, f32[4,5,9,129]{3,2,1,0:T(8,128)S(1)}, f32[4,5,9,129]{3,2,1,0:T(8,128)}, f32[4,5,9,129]{3,2,1,0:T(8,128)}, f32[4,5,9,129]{3,2,1,0:T(8,128)}) fusion(f32[4,3,5,9,129]{4,3,2,0,1:T(8,128)S(1)} %get-tuple-element.41, f32[5,9,129]{2,1,0:T(8,128)S(1)} %copy.235, f32[4,3,5,9,129]{4,3,2,0,1:T(8,128)S(1)} %get-tuple-element.40, ...), kind=kLoop, calls=%fused_computation.64 | loop fusion | flops 255420 | bytes 1369980 | tf_op jit(solution)/shard_map/add | solution.py:65
  61.6 1.0 %fusion.17 = (f32[4,5,9,129]{3,2,1,0:T(8,128)}, f32[4,5,9,129]{3,2,1,0:T(8,128)}) fusion(f32[4,5,9,129]{3,2,1,0:T(8,128)S(1)} %get-tuple-element.17, f32[4,3,5,9,129]{4,3,2,0,1:T(8,128)S(1)} %get-tuple-element.39, f32[5,9,129]{2,1,0:T(8,128)S(1)} %copy.235, f32[4,3,5,9,129]{4,3,2,0,1:T(8,128)S(1)} %get-tuple-element.40), kind=kLoop, calls=%fused_computation.62 | loop fusion | flops 92880 | bytes 487620 | tf_op jit(solution)/shard_map/add | solution.py:66
  63.1 0.7 stack.80
  63.8 0.9 %bitcast_dynamic-update-slice_fusion = f32[5,6,7,11,129]{4,3,2,1,0:T(8,128)} fusion(f32[5,6,7,11,129]{4,3,2,1,0:T(8,128)} %bitcast_dynamic-update-slice_fusion.1, f32[5,3,7,11,129]{4,3,2,0,1:T(8,128)S(1)} %get-tuple-element.33), kind=kLoop, calls=%fused_computation.33 | loop fusion | bytes 772100
  64.7 0.9 %slice_dynamic-update-slice_fusion = f32[5,6,7,11,129]{4,3,2,1,0:T(8,128)} fusion(f32[5,6,7,11,129]{4,3,2,1,0:T(8,128)} %bitcast_dynamic-update-slice_fusion, f32[5,3,7,11,129]{4,3,2,1,0:T(8,128)S(1)} %copy_subtract_fusion), kind=kLoop, calls=%fused_computation.45 | loop fusion | bytes 772100
  65.6 0.9 %multiply_dynamic-update-slice_fusion.1 = f32[5,6,7,11,129]{4,3,2,1,0:T(8,128)} fusion(f32[5,6,7,11,129]{4,3,2,1,0:T(8,128)} %slice_dynamic-update-slice_fusion, f32[5,3,7,11,129]{4,3,2,0,1:T(8,128)S(1)} %copy-done.1, f32[5,3,7,11,129]{4,3,2,0,1:T(8,128)S(1)} %get-tuple-element.33), kind=kLoop, calls=%fused_computation.44 | loop fusion | flops 99330 | bytes 970760
  66.5 0.9 %fusion.12 = f32[5,6,7,11,129]{4,3,2,1,0:T(8,128)} fusion(f32[5,6,7,11,129]{4,3,2,1,0:T(8,128)} %multiply_dynamic-update-slice_fusion.1, f32[5,3,7,11,129]{4,3,2,0,1:T(8,128)S(1)} %copy-done.1, f32[5,3,7,11,129]{4,3,2,1,0:T(8,128)S(1)} %copy_subtract_fusion), kind=kLoop, calls=%fused_computation.32 | loop fusion | flops 99330 | bytes 970760
  67.4 0.9 %multiply_dynamic-update-slice_fusion = f32[5,6,7,11,129]{4,3,2,1,0:T(8,128)} fusion(f32[5,6,7,11,129]{4,3,2,1,0:T(8,128)} %fusion.12, f32[5,3,7,11,129]{4,3,2,0,1:T(8,128)S(1)} %get-tuple-element.33, f32[5,3,7,11,129]{4,3,2,1,0:T(8,128)S(1)} %copy_subtract_fusion), kind=kLoop, calls=%fused_computation.43 | loop fusion | flops 99330 | bytes 970760 | tf_op jit(solution)/shard_map/stack | solution.py:81
  68.4 1.6 %slice_reduce_fusion.1 = f32[6,4,8,128]{3,2,1,0:T(8,128)S(1)} fusion(f32[5,6,7,11,129]{4,3,2,1,0:T(8,128)} %multiply_dynamic-update-slice_fusion), kind=kLoop, calls=%fused_computation.47 | loop fusion | flops 73728 | bytes 491520 | tf_op jit(solution)/shard_map/reduce_sum | solution.py:194
  70.0 1.3 %fusion.35 = (f32[4,8,128]{2,1,0:T(8,128)S(1)}, f32[4,8,128]{2,1,0:T(8,128)S(1)}) fusion(f32[6,4,8,128]{3,2,1,0:T(8,128)S(1)} %slice_reduce_fusion, f32[1,6,5,9,129]{4,3,2,0,1:T(8,128)} %fusion.41, f32[6]{0:T(128)S(1)} %copy-done.8, f32[6,4,8,128]{3,2,1,0:T(8,128)S(1)} %slice_reduce_fusion.1, f32[5,6,7,11,129]{4,3,2,1,0:T(8,128)} %multiply_dynamic-update-slice_fusion), kind=kLoop, calls=%fused_computation.113 | loop fusion | flops 139264 | bytes 426008 | tf_op jit(solution)/shard_map/reduce_sum | solution.py:196
  71.6 0.9 %fusion.32 = f32[4,2,4,8,32]{4,0,3,2,1:T(4,128)S(1)} fusion(f32[1,4,8,4,32]{4,3,2,1,0:T(4,128)S(1)} %mul.355, f32[1,4,8,4,32]{4,3,2,1,0:T(4,128)S(1)} %stack.77, f32[1,4,8,4,32]{4,3,2,1,0:T(4,128)S(1)} %mul.366, f32[1,4,8,4,32]{4,3,2,1,0:T(4,128)} %stack.80), kind=kLoop, calls=%fused_computation.105 | loop fusion | flops 32768 | bytes 98304 | tf_op jit(solution)/shard_map/transpose | solution.py:201
  72.6 0.8 reshape.450
  73.4 4.3 %all-to-all-start = ((f32[4,1,2048]{2,1,0:T(1,128)}), f32[4,1,2048]{2,1,0:T(1,128)S(1)}, u32[]{:S(2)}, u32[]{:S(2)}) async-start(f32[4,1,2048]{2,1,0:T(1,128)} %reshape.450), calls=%async_computation | async-start | bytes 65536 | tf_op jit(solution)/shard_map/all_to_all | solution.py:202
  77.7 2.3 %fusion.57 = (f32[4,1,4,8,128]{4,3,2,1,0:T(8,128)S(1)}, f32[4,1,4,8,128]{4,3,2,1,0:T(8,128)S(1)}, f32[4,1,4,8,128]{4,3,2,1,0:T(8,128)S(1)}) fusion(f32[4,5,9,129]{3,2,1,0:T(8,128)} %get-tuple-element.24, f32[4,5,9,129]{3,2,1,0:T(8,128)} %get-tuple-element.23, f32[4,5,9,129]{3,2,1,0:T(8,128)} %get-tuple-element.16, f32[4,5,9,129]{3,2,1,0:T(8,128)} %get-tuple-element.25, ...), kind=kLoop, calls=%fused_computation.149 | loop fusion | flops 245760 | bytes 1179648 | tf_op jit(solution)/shard_map/stack | solution.py:80
  79.9 2.0 %fusion.30 = f32[4,3,4,8,128]{4,3,2,1,0:T(8,128)} fusion(f32[4,1,4,8,128]{4,3,2,1,0:T(8,128)S(1)} %get-tuple-element.51, f32[4,1,4,8,128]{4,3,2,1,0:T(8,128)S(1)} %get-tuple-element.50, f32[4,1,4,8,128]{4,3,2,1,0:T(8,128)S(1)} %get-tuple-element.49, f32[4,3,4,8,128]{4,2,3,1,0:T(4,128)} %slice.502, f32[4,4,8,128]{3,2,1,0:T(8,128)} %slice.529, ...), kind=kLoop, calls=%fused_computation.100 | loop fusion | flops 393216 | bytes 870400 | tf_op jit(solution)/shard_map/add | solution.py:113
  82.4 0.7 reduce.2
  (98 shorter events, 12.5 us)
Async XLA Ops:
  0.6 2.2 %copy-start.3 = (f32[4,8,128]{2,1,0:T(8,128)S(1)}, f32[4,8,128]{2,1,0:T(8,128)}, u32[]{:S(2)}) copy-start(f32[4,8,128]{2,1,0:T(8,128)} %param.18) | copy-start | bytes 49156
  0.6 2.2 %copy-start.4 = (f32[4,8,128]{2,1,0:T(8,128)S(1)}, f32[4,8,128]{2,1,0:T(8,128)}, u32[]{:S(2)}) copy-start(f32[4,8,128]{2,1,0:T(8,128)} %param.19) | copy-start | bytes 49156
  0.7 2.3 %copy-start.5 = (f32[4,8,128]{2,1,0:T(8,128)S(1)}, f32[4,8,128]{2,1,0:T(8,128)}, u32[]{:S(2)}) copy-start(f32[4,8,128]{2,1,0:T(8,128)} %param.20) | copy-start | bytes 49156
  1.6 13.7 %copy-start.9 = (s32[4]{0:T(128)S(1)}, s32[4]{0:T(128)}, u32[]{:S(2)}) copy-start(s32[4]{0:T(128)} %param.24) | copy-start | bytes 52
  1.6 13.9 %copy-start.10 = (s32[4]{0:T(128)S(1)}, s32[4]{0:T(128)}, u32[]{:S(2)}) copy-start(s32[4]{0:T(128)} %param.25) | copy-start | bytes 52
  1.7 14.0 %copy-start.6 = (f32[4,256,3]{1,0,2:T(4,128)S(1)}, f32[4,256,3]{1,0,2:T(4,128)}, u32[]{:S(2)}) copy-start(f32[4,256,3]{1,0,2:T(4,128)} %param.26) | copy-start | bytes 36868
  1.7 14.1 %copy-start.7 = (f32[256,3]{0,1:T(4,128)S(1)}, f32[256,3]{0,1:T(4,128)}, u32[]{:S(2)}) copy-start(f32[256,3]{0,1:T(4,128)} %param.23) | copy-start | bytes 9220
  3.2 14.7 %collective-permute-start = (f32[33,2,8,128]{3,1,2,0:T(2,128)S(1)}, f32[33,2,8,128]{3,1,2,0:T(2,128)S(1)}, u32[]{:S(2)}, u32[]{:S(2)}) collective-permute-start(f32[33,2,8,128]{3,1,2,0:T(2,128)S(1)} %get-tuple-element.45), channel_id=1, source_target_pairs={{0,8},{8,16},{16,24},{24,32},{32,40},{40,48},{48,56},{56,64},{64,7... | collective-permute-start | bytes 811016 | tf_op jit(solution)/shard_map/ppermute | solution.py:20
  12.1 16.8 %collective-permute-start.1 = (f32[33,2,8,128]{3,1,2,0:T(2,128)S(1)}, f32[33,2,8,128]{3,1,2,0:T(2,128)S(1)}, u32[]{:S(2)}, u32[]{:S(2)}) collective-permute-start(f32[33,2,8,128]{3,1,2,0:T(2,128)S(1)} %get-tuple-element.46), channel_id=1, source_target_pairs={{8,0},{16,8},{24,16},{32,24},{40,32},{48,40},{56,48},{64,56},{72,6... | collective-permute-start | bytes 811016 | tf_op jit(solution)/shard_map/ppermute | solution.py:22
  29.1 12.3 %collective-permute-start.2 = (f32[33,8,2,128]{3,1,2,0:T(8,128)S(1)}, f32[33,8,2,128]{3,1,2,0:T(8,128)S(1)}, u32[]{:S(2)}, u32[]{:S(2)}) collective-permute-start(f32[33,8,2,128]{3,1,2,0:T(8,128)S(1)} %get-tuple-element.31), channel_id=1, source_target_pairs={{0,1},{1,2},{2,3},{3,4},{4,5},{5,6},{6,7},{8,9},{9,10},{10,11},{11... | collective-permute-start | bytes 811016 | tf_op jit(solution)/shard_map/ppermute | solution.py:20
  38.0 7.8 %collective-permute-start.3 = (f32[33,8,2,128]{3,1,2,0:T(8,128)S(1)}, f32[33,8,2,128]{3,1,2,0:T(8,128)S(1)}, u32[]{:S(2)}, u32[]{:S(2)}) collective-permute-start(f32[33,8,2,128]{3,1,2,0:T(8,128)S(1)} %get-tuple-element.32), channel_id=1, source_target_pairs={{1,0},{2,1},{3,2},{4,3},{5,4},{6,5},{7,6},{9,8},{10,9},{11,10},{12... | collective-permute-start | bytes 811016 | tf_op jit(solution)/shard_map/ppermute | solution.py:22
  50.1 2.8 %copy-start = (f32[5,3,7,11,129]{4,3,2,0,1:T(8,128)}, f32[5,3,7,11,129]{4,3,2,0,1:T(8,128)S(1)}, u32[]{:S(2)}) copy-start(f32[5,3,7,11,129]{4,3,2,0,1:T(8,128)S(1)} %get-tuple-element.36) | copy-start | bytes 1787944
  52.7 0.9 %copy-start.2 = (f32[5,3,6,10,128]{4,3,2,0,1:T(8,128)}, f32[5,3,6,10,128]{4,3,2,0,1:T(8,128)S(1)}, u32[]{:S(2)}) copy-start(f32[5,3,6,10,128]{4,3,2,0,1:T(8,128)S(1)} %fusion.6) | copy-start | bytes 1382404
  54.4 4.5 %slice-start = ((f32[5,3,6,10,128]{4,3,2,0,1:T(8,128)}), f32[4,3,6,10,128]{4,3,2,0,1:T(8,128)S(1)}, s32[]{:S(2)}) async-start(f32[5,3,6,10,128]{4,3,2,0,1:T(8,128)} %copy-done.2), calls=%async_computation.1 | async-start | bytes 1179648 | tf_op jit(solution)/shard_map/slice | solution.py:179
  63.8 1.7 %copy-start.1 = (f32[5,3,7,11,129]{4,3,2,0,1:T(8,128)S(1)}, f32[5,3,7,11,129]{4,3,2,0,1:T(8,128)}, u32[]{:S(2)}) copy-start(f32[5,3,7,11,129]{4,3,2,0,1:T(8,128)} %copy-done) | copy-start | bytes 1787944
  66.5 3.5 %copy-start.8 = (f32[6]{0:T(128)S(1)}, f32[6]{0:T(128)}, u32[]{:S(2)}) copy-start(f32[6]{0:T(128)} %constant.95.clone) | copy-start | bytes 76
  73.4 8.5 %all-to-all-start = ((f32[4,1,2048]{2,1,0:T(1,128)}), f32[4,1,2048]{2,1,0:T(1,128)S(1)}, u32[]{:S(2)}, u32[]{:S(2)}) async-start(f32[4,1,2048]{2,1,0:T(1,128)} %reshape.450), calls=%async_computation | async-start | bytes 65536 | tf_op jit(solution)/shard_map/all_to_all | solution.py:202

commit v4 on v3

--- a/solution.py
+++ b/solution.py
@@ -198,8 +198,8 @@
     totals = totals * (1.0 / (STEPS * receivers * groups))
 
     share = depth // groups
-    parts = jnp.moveaxis(totals.reshape((2, cells_x, cells_y, groups, share)), 3, 0)
-    kernels = jnp.sum(lax.all_to_all(parts, "grp", 0, 0, tiled=False), axis=0)
+    gathered = lax.all_to_all(totals, "grp", 3, 0, tiled=True)
+    kernels = jnp.sum(gathered.reshape((groups, 2, cells_x, cells_y, share)), axis=0)
     return (final, kernels)
 
 

time: 84.4 us -> 69.7 us (0.83)
  the two profiles are of different devices: /device:TPU:123 before, /device:TPU:121 now
where the time goes in v4:
time: 69.7 us; the launch traced here: 69.3 us
  starting transfers between devices  25.7 us (37%)
  waiting for transfers between devices  21.5 us (31%)
  other arithmetic  13 us (19%)
  local copies, waits for them, and re-layouts  6.45 us (9%)
  between operations  2.62 us (4%)
    ppermute x2, starting transfers between devices, with_halo(): lax.ppermute(tail, axis, [(i, i + 1) for i in range(ends)])  17.8 us
    ppermute x2, waiting for transfers between devices, with_halo(): lax.ppermute(head, axis, [(i + 1, i) for i in range(ends)])  15.5 us
    all_to_all x1, starting transfers between devices, local(): gathered = lax.all_to_all(totals, 'grp', 3, 0, tiled=True)  4.01 us
    ppermute x2, starting transfers between devices, with_halo(): lax.ppermute(head, axis, [(i + 1, i) for i in range(ends)])  3.84 us
    sub x3, other arithmetic, strains_of(): grad_y = padded[:, :, :span_x + 1, 1:, :span_z + 1] - anchor  3.66 us
    unnamed x36, local copies, waits for them, and re-layouts  3.63 us
    all_to_all x1, waiting for transfers between devices, local(): gathered = lax.all_to_all(totals, 'grp', 3, 0, tiled=True)  3.23 us
    ppermute x2, waiting for transfers between devices, with_halo(): lax.ppermute(tail, axis, [(i, i + 1) for i in range(ends)])  2.82 us
  transfers between devices with their start and end apart: 5, of which 5 were waited for; matrix products, arithmetic and copies ran while one was open for 3% of the time, Pallas kernels for 0%

profile of v4, /device:TPU:121, one launch (start us, length us, event | category | flops | bytes accessed | tf_op | source)
XLA Modules:
  0.0 69.3 jit_solution(17184540720163065921)
XLA Ops:
  0.7 1.0 %pad_maximum_fusion.4 = f32[5,3,4,8,128]{4,3,2,1,0:T(8,128)S(1)} fusion(f32[4,3,4,8,128]{4,3,2,1,0:T(8,128)} %param.16, f32[1,3,4,8,128]{4,3,2,1,0:T(8,128)} %bitcast.195), kind=kLoop, calls=%fused_computation.94 | loop fusion | flops 61440 | bytes 491520 | tf_op jit(solution)/shard_map/concatenate | solution.py:140
  1.7 1.0 %pad_maximum_fusion.5 = f32[5,3,4,8,128]{4,3,2,1,0:T(8,128)S(1)} fusion(f32[4,3,4,8,128]{4,3,2,1,0:T(8,128)} %param.17, f32[1,3,4,8,128]{4,3,2,1,0:T(8,128)} %bitcast.196), kind=kLoop, calls=%fused_computation.95 | loop fusion | flops 61440 | bytes 491520 | tf_op jit(solution)/shard_map/concatenate | solution.py:141
  2.9 0.2 fusion.68
  3.2 8.9 %collective-permute-start = (f32[33,2,8,128]{3,1,2,0:T(2,128)S(1)}, f32[33,2,8,128]{3,1,2,0:T(2,128)S(1)}, u32[]{:S(2)}, u32[]{:S(2)}) collective-permute-start(f32[33,2,8,128]{3,1,2,0:T(2,128)S(1)} %get-tuple-element.42), channel_id=1, source_target_pairs={{0,8},{8,16},{16,24},{24,32},{32,40},{40,48},{48,56},{56,64},{64,7... | collective-permute-start | bytes 811016 | tf_op jit(solution)/shard_map/ppermute | solution.py:20
  12.1 1.9 %collective-permute-start.1 = (f32[33,2,8,128]{3,1,2,0:T(2,128)S(1)}, f32[33,2,8,128]{3,1,2,0:T(2,128)S(1)}, u32[]{:S(2)}, u32[]{:S(2)}) collective-permute-start(f32[33,2,8,128]{3,1,2,0:T(2,128)S(1)} %get-tuple-element.43), channel_id=1, source_target_pairs={{8,0},{16,8},{24,16},{32,24},{40,32},{48,40},{56,48},{64,56},{72,6... | collective-permute-start | bytes 811016 | tf_op jit(solution)/shard_map/ppermute | solution.py:22
  16.2 1.6 %collective-permute-done = f32[33,2,8,128]{3,1,2,0:T(2,128)S(1)} collective-permute-done((f32[33,2,8,128]{3,1,2,0:T(2,128)S(1)}, f32[33,2,8,128]{3,1,2,0:T(2,128)S(1)}, u32[]{:S(2)}, u32[]{:S(2)}) %collective-permute-start) | collective-permute-done | bytes 270368 | tf_op jit(solution)/shard_map/ppermute | solution.py:20
  17.8 11.1 %collective-permute-done.1 = f32[33,2,8,128]{3,1,2,0:T(2,128)S(1)} collective-permute-done((f32[33,2,8,128]{3,1,2,0:T(2,128)S(1)}, f32[33,2,8,128]{3,1,2,0:T(2,128)S(1)}, u32[]{:S(2)}, u32[]{:S(2)}) %collective-permute-start.1) | collective-permute-done | bytes 270368 | tf_op jit(solution)/shard_map/ppermute | solution.py:22
  28.9 0.2 pad_maximum_fusion.3
  29.1 8.9 %collective-permute-start.2 = (f32[33,8,2,128]{3,1,2,0:T(8,128)S(1)}, f32[33,8,2,128]{3,1,2,0:T(8,128)S(1)}, u32[]{:S(2)}, u32[]{:S(2)}) collective-permute-start(f32[33,8,2,128]{3,1,2,0:T(8,128)S(1)} %get-tuple-element.29), channel_id=1, source_target_pairs={{0,1},{1,2},{2,3},{3,4},{4,5},{5,6},{6,7},{8,9},{9,10},{10,11},{11... | collective-permute-start | bytes 811016 | tf_op jit(solution)/shard_map/ppermute | solution.py:20
  38.0 1.9 %collective-permute-start.3 = (f32[33,8,2,128]{3,1,2,0:T(8,128)S(1)}, f32[33,8,2,128]{3,1,2,0:T(8,128)S(1)}, u32[]{:S(2)}, u32[]{:S(2)}) collective-permute-start(f32[33,8,2,128]{3,1,2,0:T(8,128)S(1)} %get-tuple-element.30), channel_id=1, source_target_pairs={{1,0},{2,1},{3,2},{4,3},{5,4},{6,5},{7,6},{9,8},{10,9},{11,10},{12... | collective-permute-start | bytes 811016 | tf_op jit(solution)/shard_map/ppermute | solution.py:22
  40.1 1.2 %collective-permute-done.2 = f32[33,8,2,128]{3,1,2,0:T(8,128)S(1)} collective-permute-done((f32[33,8,2,128]{3,1,2,0:T(8,128)S(1)}, f32[33,8,2,128]{3,1,2,0:T(8,128)S(1)}, u32[]{:S(2)}, u32[]{:S(2)}) %collective-permute-start.2) | collective-permute-done | bytes 270368 | tf_op jit(solution)/shard_map/ppermute | solution.py:20
  41.4 4.4 %collective-permute-done.3 = f32[33,8,2,128]{3,1,2,0:T(8,128)S(1)} collective-permute-done((f32[33,8,2,128]{3,1,2,0:T(8,128)S(1)}, f32[33,8,2,128]{3,1,2,0:T(8,128)S(1)}, u32[]{:S(2)}, u32[]{:S(2)}) %collective-permute-start.3) | collective-permute-done | bytes 270368 | tf_op jit(solution)/shard_map/ppermute | solution.py:22
  46.1 0.4 pad_maximum_fusion
  47.0 2.3 %fusion.1 = (f32[5,3,7,11,129]{4,3,2,0,1:T(8,128)S(1)}, f32[5,3,7,11,129]{4,3,2,0,1:T(8,128)S(1)}, f32[5,3,7,11,129]{4,3,2,0,1:T(8,128)S(1)}) fusion(f32[5,3,8,12,128]{4,3,2,0,1:T(8,128)S(1)} %copy.152), kind=kLoop, calls=%fused_computation.9 | loop fusion | flops 446985 | bytes 2525220 | tf_op jit(solution)/shard_map/sub | solution.py:46
  49.3 0.7 fusion.14
  50.0 0.2 fusion.13
  50.2 0.9 %fusion.27 = (f32[5,1,6,10,128]{4,3,2,0,1:T(8,128)S(1)}, f32[5,1,6,10,128]{4,3,2,0,1:T(8,128)S(1)}, f32[5,1,6,10,128]{4,3,2,0,1:T(8,128)S(1)}) fusion(f32[5,7,11,129]{3,2,1,0:T(8,128)S(1)} %get-tuple-element.19, f32[5,7,11,129]{3,2,1,0:T(8,128)S(1)} %get-tuple-element.18, f32[5,7,11,129]{3,2,1,0:T(8,128)S(1)} %get-tuple-element.16, ...), kind=kLoop, calls=%fused_computation.90 | loop fusion | flops 576000 | bytes 2764800 | tf_op jit(solution)/shard_map/stack | solution.py:80
  51.1 0.3 fusion.7
  51.6 0.6 copy-done
  52.5 0.8 %slice-done = f32[4,3,6,10,128]{4,3,2,0,1:T(8,128)S(1)} async-done(((f32[5,3,6,10,128]{4,3,2,0,1:T(8,128)}), f32[4,3,6,10,128]{4,3,2,0,1:T(8,128)S(1)}, s32[]{:S(2)}) %slice-start) | async-done | bytes 368664 | tf_op jit(solution)/shard_map/slice | solution.py:179
  53.4 1.3 %fusion.4 = (f32[4,3,5,9,129]{4,3,2,0,1:T(8,128)S(1)}, f32[4,3,5,9,129]{4,3,2,0,1:T(8,128)S(1)}, f32[4,3,5,9,129]{4,3,2,0,1:T(8,128)S(1)}) fusion(f32[4,3,6,10,128]{4,3,2,0,1:T(8,128)S(1)} %slice-done), kind=kLoop, calls=%fused_computation.13 | loop fusion | flops 208980 | bytes 1204560 | tf_op jit(solution)/shard_map/sub | solution.py:46
  54.7 0.4 fusion.18
  56.8 0.3 copy.189
  57.0 1.2 %reshape.441 = f32[4,1,2048]{2,1,0:T(1,128)} reshape(f32[128,2,4,8]{3,2,1,0:T(4,128)S(1)} %bitcast.190) | data formatting | bytes 65536
  58.2 4.0 %all-to-all-start = ((f32[4,1,2048]{2,1,0:T(1,128)}), f32[4,1,2048]{2,1,0:T(1,128)S(1)}, u32[]{:S(2)}, u32[]{:S(2)}) async-start(f32[4,1,2048]{2,1,0:T(1,128)} %reshape.441), calls=%async_computation | async-start | bytes 65536 | tf_op jit(solution)/shard_map/all_to_all | solution.py:201
  62.2 0.3 fusion.55
  62.5 0.8 %fusion.30 = f32[4,3,4,8,128]{4,3,2,1,0:T(8,128)} fusion(f32[4,1,4,8,128]{4,3,2,1,0:T(8,128)S(1)} %get-tuple-element.48, f32[4,1,4,8,128]{4,3,2,1,0:T(8,128)S(1)} %get-tuple-element.47, f32[4,1,4,8,128]{4,3,2,1,0:T(8,128)S(1)} %get-tuple-element.46, f32[4,3,4,8,128]{4,2,3,1,0:T(4,128)S(1)} %slice.502, f32[4,4,8,128]{3,2,1,0:T(8,128)S(1)} %slice.529, ...), kind=kLoop, calls=%fused_computation.99 | loop fusion | flops 393216 | bytes 870400 | tf_op jit(solution)/shard_map/add | solution.py:113
  63.3 3.2 %all-to-all-done = f32[4,1,2048]{2,1,0:T(1,128)S(1)} async-done(((f32[4,1,2048]{2,1,0:T(1,128)}), f32[4,1,2048]{2,1,0:T(1,128)S(1)}, u32[]{:S(2)}, u32[]{:S(2)}) %all-to-all-start) | async-done | bytes 32800 | tf_op jit(solution)/shard_map/all_to_all | solution.py:201
  66.5 0.5 broadcast.365
  67.0 0.7 %reduce.4 = f32[4,2048]{1,0:T(4,128)S(1)} reduce(f32[4,1,2048]{2,1,0:T(1,128)S(1)} %all-to-all-done, f32[]{:T(128)} %broadcast.365), dimensions={1}, to_apply=%all_to_all.4.reduce_sub_computation | reduce | bytes 65540 | tf_op jit(solution)/shard_map/all_to_all | solution.py:201
  67.8 0.6 reshape.442
  68.6 0.7 %copy.191 = f32[2,4,8,32]{3,2,1,0:T(8,128)} copy(f32[2,4,8,32]{2,1,0,3:T(4,128)S(1)} %reduce_sum.82) | data formatting | bytes 16384
  (91 shorter events, 4.2 us)
Async XLA Ops:
  0.6 2.2 %copy-start.2 = (f32[4,8,128]{2,1,0:T(8,128)S(1)}, f32[4,8,128]{2,1,0:T(8,128)}, u32[]{:S(2)}) copy-start(f32[4,8,128]{2,1,0:T(8,128)} %param.18) | copy-start | bytes 49156
  0.6 2.2 %copy-start.3 = (f32[4,8,128]{2,1,0:T(8,128)S(1)}, f32[4,8,128]{2,1,0:T(8,128)}, u32[]{:S(2)}) copy-start(f32[4,8,128]{2,1,0:T(8,128)} %param.19) | copy-start | bytes 49156
  0.7 2.3 %copy-start.4 = (f32[4,8,128]{2,1,0:T(8,128)S(1)}, f32[4,8,128]{2,1,0:T(8,128)}, u32[]{:S(2)}) copy-start(f32[4,8,128]{2,1,0:T(8,128)} %param.20) | copy-start | bytes 49156
  1.6 13.7 %copy-start.8 = (s32[4]{0:T(128)S(1)}, s32[4]{0:T(128)}, u32[]{:S(2)}) copy-start(s32[4]{0:T(128)} %param.24) | copy-start | bytes 52
  1.6 13.9 %copy-start.9 = (s32[4]{0:T(128)S(1)}, s32[4]{0:T(128)}, u32[]{:S(2)}) copy-start(s32[4]{0:T(128)} %param.25) | copy-start | bytes 52
  1.7 14.0 %copy-start.5 = (f32[4,256,3]{1,0,2:T(4,128)S(1)}, f32[4,256,3]{1,0,2:T(4,128)}, u32[]{:S(2)}) copy-start(f32[4,256,3]{1,0,2:T(4,128)} %param.26) | copy-start | bytes 36868
  1.7 14.1 %copy-start.6 = (f32[256,3]{0,1:T(4,128)S(1)}, f32[256,3]{0,1:T(4,128)}, u32[]{:S(2)}) copy-start(f32[256,3]{0,1:T(4,128)} %param.23) | copy-start | bytes 9220
  3.2 14.7 %collective-permute-start = (f32[33,2,8,128]{3,1,2,0:T(2,128)S(1)}, f32[33,2,8,128]{3,1,2,0:T(2,128)S(1)}, u32[]{:S(2)}, u32[]{:S(2)}) collective-permute-start(f32[33,2,8,128]{3,1,2,0:T(2,128)S(1)} %get-tuple-element.42), channel_id=1, source_target_pairs={{0,8},{8,16},{16,24},{24,32},{32,40},{40,48},{48,56},{56,64},{64,7... | collective-permute-start | bytes 811016 | tf_op jit(solution)/shard_map/ppermute | solution.py:20
  12.1 16.8 %collective-permute-start.1 = (f32[33,2,8,128]{3,1,2,0:T(2,128)S(1)}, f32[33,2,8,128]{3,1,2,0:T(2,128)S(1)}, u32[]{:S(2)}, u32[]{:S(2)}) collective-permute-start(f32[33,2,8,128]{3,1,2,0:T(2,128)S(1)} %get-tuple-element.43), channel_id=1, source_target_pairs={{8,0},{16,8},{24,16},{32,24},{40,32},{48,40},{56,48},{64,56},{72,6... | collective-permute-start | bytes 811016 | tf_op jit(solution)/shard_map/ppermute | solution.py:22
  29.1 12.3 %collective-permute-start.2 = (f32[33,8,2,128]{3,1,2,0:T(8,128)S(1)}, f32[33,8,2,128]{3,1,2,0:T(8,128)S(1)}, u32[]{:S(2)}, u32[]{:S(2)}) collective-permute-start(f32[33,8,2,128]{3,1,2,0:T(8,128)S(1)} %get-tuple-element.29), channel_id=1, source_target_pairs={{0,1},{1,2},{2,3},{3,4},{4,5},{5,6},{6,7},{8,9},{9,10},{10,11},{11... | collective-permute-start | bytes 811016 | tf_op jit(solution)/shard_map/ppermute | solution.py:20
  38.0 7.8 %collective-permute-start.3 = (f32[33,8,2,128]{3,1,2,0:T(8,128)S(1)}, f32[33,8,2,128]{3,1,2,0:T(8,128)S(1)}, u32[]{:S(2)}, u32[]{:S(2)}) collective-permute-start(f32[33,8,2,128]{3,1,2,0:T(8,128)S(1)} %get-tuple-element.30), channel_id=1, source_target_pairs={{1,0},{2,1},{3,2},{4,3},{5,4},{6,5},{7,6},{9,8},{10,9},{11,10},{12... | collective-permute-start | bytes 811016 | tf_op jit(solution)/shard_map/ppermute | solution.py:22
  51.4 0.9 %copy-start = (f32[5,3,6,10,128]{4,3,2,0,1:T(8,128)}, f32[5,3,6,10,128]{4,3,2,0,1:T(8,128)S(1)}, u32[]{:S(2)}) copy-start(f32[5,3,6,10,128]{4,3,2,0,1:T(8,128)S(1)} %fusion.7) | copy-start | bytes 1382404
  52.3 1.1 %slice-start = ((f32[5,3,6,10,128]{4,3,2,0,1:T(8,128)}), f32[4,3,6,10,128]{4,3,2,0,1:T(8,128)S(1)}, s32[]{:S(2)}) async-start(f32[5,3,6,10,128]{4,3,2,0,1:T(8,128)} %copy-done), calls=%async_computation.1 | async-start | bytes 1179648 | tf_op jit(solution)/shard_map/slice | solution.py:179
  55.9 0.7 copy-start.7
  56.2 6.3 %copy-start.1 = (f32[5,3,6,10,128]{4,3,2,0,1:T(8,128)S(1)}, f32[5,3,6,10,128]{4,3,2,0,1:T(8,128)}, u32[]{:S(2)}) copy-start(f32[5,3,6,10,128]{4,3,2,0,1:T(8,128)} %copy-done) | copy-start | bytes 1382404
  58.2 8.3 %all-to-all-start = ((f32[4,1,2048]{2,1,0:T(1,128)}), f32[4,1,2048]{2,1,0:T(1,128)S(1)}, u32[]{:S(2)}, u32[]{:S(2)}) async-start(f32[4,1,2048]{2,1,0:T(1,128)} %reshape.441), calls=%async_computation | async-start | bytes 65536 | tf_op jit(solution)/shard_map/all_to_all | solution.py:201

commit v5 on v2

--- a/solution.py
+++ b/solution.py
@@ -113,34 +113,20 @@
     return 2.0 * current - earlier + time_step_sq * buoyancy * (force + source)
 
 
-def shifted(value, by_x, by_y):
-    count_x = lax.axis_size("gx")
-    count_y = lax.axis_size("gy")
-    pairs = [
-        (i * count_y + j, (i + by_x) * count_y + j + by_y)
-        for i in range(count_x)
-        for j in range(count_y)
-        if 0 <= i + by_x < count_x and 0 <= j + by_y < count_y
-    ]
-    return lax.ppermute(value, ("gx", "gy"), pairs)
-
-
-def exchange(stacked, pairs_lo, pairs_hi):
+def exchange_x(stacked, pairs_lo, pairs_hi):
     channels, cells_x, cells_y, depth = stacked.shape
     plane = (cells_y, depth)
+    count = lax.axis_size("gx")
     wide_lo = stacked[:pairs_lo, cells_x - 2 :].reshape((-1,) + plane)
     thin_lo = stacked[pairs_lo:, cells_x - 1 :].reshape((-1,) + plane)
     wide_hi = stacked[:pairs_hi, :2].reshape((-1,) + plane)
     thin_hi = stacked[pairs_hi:, :1].reshape((-1,) + plane)
-    from_lo = shifted(jnp.concatenate([wide_lo, thin_lo]), 1, 0)
-    from_hi = shifted(jnp.concatenate([wide_hi, thin_hi]), -1, 0)
-    from_y_lo = shifted(stacked[:, :, cells_y - 2 :], 0, 1)
-    from_y_hi = shifted(stacked[:, :, :2], 0, -1)
-    corner_ll = shifted(stacked[:, cells_x - 2 :, cells_y - 2 :], 1, 1)
-    corner_lh = shifted(stacked[:, cells_x - 2 :, :2], 1, -1)
-    corner_hl = shifted(stacked[:, :2, cells_y - 2 :], -1, 1)
-    corner_hh = shifted(stacked[:, :2, :2], -1, -1)
-
+    from_lo = lax.ppermute(
+        jnp.concatenate([wide_lo, thin_lo]), "gx", [(i, i + 1) for i in range(count - 1)]
+    )
+    from_hi = lax.ppermute(
+        jnp.concatenate([wide_hi, thin_hi]), "gx", [(i + 1, i) for i in range(count - 1)]
+    )
     blank = jnp.zeros((channels - pairs_lo, 1) + plane, jnp.float32)
     rows_lo = jnp.concatenate(
         [
@@ -155,10 +141,7 @@
             jnp.concatenate([from_hi[pairs_hi * 2 :].reshape((-1, 1) + plane), blank], axis=1),
         ]
     )
-    band_lo = jnp.concatenate([corner_ll, rows_lo, corner_lh], axis=2)
-    band_mid = jnp.concatenate([from_y_lo, stacked, from_y_hi], axis=2)
-    band_hi = jnp.concatenate([corner_hl, rows_hi, corner_hh], axis=2)
-    return jnp.concatenate([band_lo, band_mid, band_hi], axis=1)
+    return jnp.concatenate([rows_lo, stacked, rows_hi], axis=1)
 
 
 def local(
@@ -184,12 +167,12 @@
     start_x = lax.axis_index("gx") * cells_x
     start_y = lax.axis_index("gy") * cells_y
     grid = (cells_x, cells_y, depth)
+
+    now = jnp.concatenate([fwd_now[None], adj_now]).reshape((fields * 3,) + grid)
+    prev = jnp.concatenate([fwd_prev[None], adj_prev]).reshape((fields * 3,) + grid)
     comps = fields * 3
-
-    now = jnp.concatenate([fwd_now[None], adj_now]).reshape((comps,) + grid)
-    prev = jnp.concatenate([fwd_prev[None], adj_prev]).reshape((comps,) + grid)
     stacked = jnp.concatenate([now, lame_first[None], shear_mod[None], prev, buoyancy[None]])
-    grown = exchange(stacked, comps + 2, comps)
+    grown = with_halo(exchange_x(stacked, comps + 2, comps), (("gy", 2),), 2)
     now_grown = grown[:comps].reshape((fields, 3) + grown.shape[1:])
     lame_grown = zpad(grown[comps])
     shear_grown = zpad(grown[comps + 1])
@@ -246,8 +229,8 @@
     totals = totals * (1.0 / (STEPS * receivers * groups))
 
     share = depth // groups
-    parts = jnp.moveaxis(totals.reshape((2, cells_x, cells_y, groups, share)), 3, 0)
-    kernels = jnp.sum(lax.all_to_all(parts, "grp", 0, 0, tiled=False), axis=0)
+    gathered = lax.all_to_all(totals, "grp", 3, 0, tiled=True)
+    kernels = jnp.sum(gathered.reshape((groups, 2, cells_x, cells_y, share)), axis=0)
     return (final, kernels)
 
 

time: 88.2 us -> 60 us (0.68)
  the two profiles are of different devices: /device:TPU:448 before, /device:TPU:321 now
where the time goes in v5:
time: 60 us; the launch traced here: 59.6 us
  starting transfers between devices  20.2 us (34%)
  waiting for transfers between devices  16.9 us (28%)
  other arithmetic  13 us (22%)
  local copies, waits for them, and re-layouts  6.74 us (11%)
  between operations  2.74 us (5%)
    ppermute x1, starting transfers between devices, with_halo(): lax.ppermute(tail, axis, [(i, i + 1) for i in range(ends)])  9 us
    ppermute x1, waiting for transfers between devices, exchange_x(): lax.ppermute(jnp.concatenate([wide_lo, thin_lo]), 'gx', [(i, i + 1) for i...  8 us
    ppermute x1, waiting for transfers between devices, with_halo(): lax.ppermute(head, axis, [(i + 1, i) for i in range(ends)])  4.4 us
    all_to_all x1, starting transfers between devices, local(): gathered = lax.all_to_all(totals, 'grp', 3, 0, tiled=True)  4.01 us
    sub x3, other arithmetic, strains_of(): grad_y = padded[:, :, :span_x + 1, 1:, :span_z + 1] - anchor  3.66 us
    unnamed x36, local copies, waits for them, and re-layouts  3.59 us
    all_to_all x1, waiting for transfers between devices, local(): gathered = lax.all_to_all(totals, 'grp', 3, 0, tiled=True)  3.23 us
    ppermute x1, starting transfers between devices, exchange_x(): lax.ppermute(jnp.concatenate([wide_lo, thin_lo]), 'gx', [(i, i + 1) for i...  2.92 us
  transfers between devices with their start and end apart: 5, of which 4 were waited for; matrix products, arithmetic and copies ran while one was open for 4% of the time, Pallas kernels for 0%

profile of v5, /device:TPU:321, one launch (start us, length us, event | category | flops | bytes accessed | tf_op | source)
XLA Modules:
  0.0 59.6 jit_solution(2697047225841265076)
XLA Ops:
  0.7 1.0 %pad_maximum_fusion.4 = f32[5,3,4,8,128]{4,3,2,1,0:T(8,128)S(1)} fusion(f32[4,3,4,8,128]{4,3,2,1,0:T(8,128)} %param.16, f32[1,3,4,8,128]{4,3,2,1,0:T(8,128)} %bitcast.221), kind=kLoop, calls=%fused_computation.96 | loop fusion | flops 61440 | bytes 491520 | tf_op jit(solution)/shard_map/concatenate | solution.py:171
  1.7 0.9 %pad_maximum_fusion.5 = f32[5,3,4,8,128]{4,3,2,1,0:T(8,128)S(1)} fusion(f32[4,3,4,8,128]{4,3,2,1,0:T(8,128)} %param.17, f32[1,3,4,8,128]{4,3,2,1,0:T(8,128)} %bitcast.222), kind=kLoop, calls=%fused_computation.97 | loop fusion | flops 61440 | bytes 491520 | tf_op jit(solution)/shard_map/concatenate | solution.py:172
  2.8 2.4 %collective-permute-start.1 = (f32[48,8,128]{2,1,0:T(8,128)S(1)}, f32[48,8,128]{2,1,0:T(8,128)S(1)}, u32[]{:S(2)}, u32[]{:S(2)}) collective-permute-start(f32[48,8,128]{2,1,0:T(8,128)S(1)} %pad_maximum_fusion.7), channel_id=1, source_target_pairs={{8,0},{16,8},{24,16},{32,24},{40,32},{48,40},{56,48},{64,56},{72,6... | collective-permute-start | bytes 589832 | tf_op jit(solution)/shard_map/ppermute | solution.py:127
  5.2 2.9 %collective-permute-start = (f32[50,8,128]{2,1,0:T(8,128)S(1)}, f32[50,8,128]{2,1,0:T(8,128)S(1)}, u32[]{:S(2)}, u32[]{:S(2)}) collective-permute-start(f32[50,8,128]{2,1,0:T(8,128)S(1)} %pad_maximum_fusion.6), channel_id=1, source_target_pairs={{0,8},{8,16},{16,24},{24,32},{32,40},{40,48},{48,56},{56,64},{64,7... | collective-permute-start | bytes 614408 | tf_op jit(solution)/shard_map/ppermute | solution.py:124
  10.8 8.0 %collective-permute-done = f32[50,8,128]{2,1,0:T(8,128)S(1)} collective-permute-done((f32[50,8,128]{2,1,0:T(8,128)S(1)}, f32[50,8,128]{2,1,0:T(8,128)S(1)}, u32[]{:S(2)}, u32[]{:S(2)}) %collective-permute-start) | collective-permute-done | bytes 204832 | tf_op jit(solution)/shard_map/ppermute | solution.py:124
  18.9 0.2 maximum_maximum_fusion
  19.1 9.0 %collective-permute-start.2 = (f32[33,8,2,128]{3,1,2,0:T(8,128)S(1)}, f32[33,8,2,128]{3,1,2,0:T(8,128)S(1)}, u32[]{:S(2)}, u32[]{:S(2)}) collective-permute-start(f32[33,8,2,128]{3,1,2,0:T(8,128)S(1)} %get-tuple-element.30), channel_id=1, source_target_pairs={{0,1},{1,2},{2,3},{3,4},{4,5},{5,6},{6,7},{8,9},{9,10},{10,11},{11... | collective-permute-start | bytes 811016 | tf_op jit(solution)/shard_map/ppermute | solution.py:20
  28.1 1.9 %collective-permute-start.3 = (f32[33,8,2,128]{3,1,2,0:T(8,128)S(1)}, f32[33,8,2,128]{3,1,2,0:T(8,128)S(1)}, u32[]{:S(2)}, u32[]{:S(2)}) collective-permute-start(f32[33,8,2,128]{3,1,2,0:T(8,128)S(1)} %get-tuple-element.31), channel_id=1, source_target_pairs={{1,0},{2,1},{3,2},{4,3},{5,4},{6,5},{7,6},{9,8},{10,9},{11,10},{12... | collective-permute-start | bytes 811016 | tf_op jit(solution)/shard_map/ppermute | solution.py:22
  30.3 1.2 %collective-permute-done.2 = f32[33,8,2,128]{3,1,2,0:T(8,128)S(1)} collective-permute-done((f32[33,8,2,128]{3,1,2,0:T(8,128)S(1)}, f32[33,8,2,128]{3,1,2,0:T(8,128)S(1)}, u32[]{:S(2)}, u32[]{:S(2)}) %collective-permute-start.2) | collective-permute-done | bytes 270368 | tf_op jit(solution)/shard_map/ppermute | solution.py:20
  31.5 4.4 %collective-permute-done.3 = f32[33,8,2,128]{3,1,2,0:T(8,128)S(1)} collective-permute-done((f32[33,8,2,128]{3,1,2,0:T(8,128)S(1)}, f32[33,8,2,128]{3,1,2,0:T(8,128)S(1)}, u32[]{:S(2)}, u32[]{:S(2)}) %collective-permute-start.3) | collective-permute-done | bytes 270368 | tf_op jit(solution)/shard_map/ppermute | solution.py:22
  36.4 0.4 pad_maximum_fusion
  37.3 2.3 %fusion.1 = (f32[5,3,7,11,129]{4,3,2,0,1:T(8,128)S(1)}, f32[5,3,7,11,129]{4,3,2,0,1:T(8,128)S(1)}, f32[5,3,7,11,129]{4,3,2,0,1:T(8,128)S(1)}) fusion(f32[5,3,8,12,128]{4,3,2,0,1:T(8,128)S(1)} %copy.224), kind=kLoop, calls=%fused_computation.9 | loop fusion | flops 446985 | bytes 2525220 | tf_op jit(solution)/shard_map/sub | solution.py:46
  39.6 0.7 %fusion.14 = (f32[5,7,11,129]{3,2,1,0:T(8,128)S(1)}, f32[5,7,11,129]{3,2,1,0:T(8,128)S(1)}, f32[5,7,11,129]{3,2,1,0:T(8,128)S(1)}, f32[5,7,11,129]{3,2,1,0:T(8,128)S(1)}, f32[5,7,11,129]{3,2,1,0:T(8,128)S(1)}) fusion(f32[5,3,7,11,129]{4,3,2,0,1:T(8,128)S(1)} %get-tuple-element.34, f32[7,11,129]{2,1,0:T(8,128)S(1)} %copy.229, ...), kind=kLoop, calls=%fused_computation.43 | loop fusion | flops 546315 | bytes 2900436 | tf_op jit(solution)/shard_map/add | solution.py:65
  40.3 0.2 fusion.13
  40.5 0.9 %fusion.28 = (f32[5,1,6,10,128]{4,3,2,0,1:T(8,128)S(1)}, f32[5,1,6,10,128]{4,3,2,0,1:T(8,128)S(1)}, f32[5,1,6,10,128]{4,3,2,0,1:T(8,128)S(1)}) fusion(f32[5,7,11,129]{3,2,1,0:T(8,128)S(1)} %get-tuple-element.21, f32[5,7,11,129]{3,2,1,0:T(8,128)S(1)} %get-tuple-element.20, f32[5,7,11,129]{3,2,1,0:T(8,128)S(1)} %get-tuple-element.18, ...), kind=kLoop, calls=%fused_computation.92 | loop fusion | flops 576000 | bytes 2764800 | tf_op jit(solution)/shard_map/stack | solution.py:80
  41.4 0.3 fusion.7
  42.0 0.6 %copy-done = f32[5,3,6,10,128]{4,3,2,0,1:T(8,128)} copy-done((f32[5,3,6,10,128]{4,3,2,0,1:T(8,128)}, f32[5,3,6,10,128]{4,3,2,0,1:T(8,128)S(1)}, u32[]{:S(2)}) %copy-start) | copy-done | bytes 460824
  42.8 0.8 %slice-done = f32[4,3,6,10,128]{4,3,2,0,1:T(8,128)S(1)} async-done(((f32[5,3,6,10,128]{4,3,2,0,1:T(8,128)}), f32[4,3,6,10,128]{4,3,2,0,1:T(8,128)S(1)}, s32[]{:S(2)}) %slice-start) | async-done | bytes 368664 | tf_op jit(solution)/shard_map/slice | solution.py:210
  43.7 1.3 %fusion.4 = (f32[4,3,5,9,129]{4,3,2,0,1:T(8,128)S(1)}, f32[4,3,5,9,129]{4,3,2,0,1:T(8,128)S(1)}, f32[4,3,5,9,129]{4,3,2,0,1:T(8,128)S(1)}) fusion(f32[4,3,6,10,128]{4,3,2,0,1:T(8,128)S(1)} %slice-done), kind=kLoop, calls=%fused_computation.13 | loop fusion | flops 208980 | bytes 1204560 | tf_op jit(solution)/shard_map/sub | solution.py:46
  45.1 0.4 fusion.18
  45.8 0.2 slice_reduce_fusion
  46.5 0.2 slice_reduce_fusion.1
  47.1 0.3 copy.261
  47.4 1.2 %reshape.473 = f32[4,1,2048]{2,1,0:T(1,128)} reshape(f32[128,2,4,8]{3,2,1,0:T(4,128)S(1)} %bitcast.206) | data formatting | bytes 65536
  48.5 4.0 %all-to-all-start = ((f32[4,1,2048]{2,1,0:T(1,128)}), f32[4,1,2048]{2,1,0:T(1,128)S(1)}, u32[]{:S(2)}, u32[]{:S(2)}) async-start(f32[4,1,2048]{2,1,0:T(1,128)} %reshape.473), calls=%async_computation | async-start | bytes 65536 | tf_op jit(solution)/shard_map/all_to_all | solution.py:232
  52.5 0.3 fusion.57
  52.8 0.8 %fusion.31 = f32[4,3,4,8,128]{4,3,2,1,0:T(8,128)} fusion(f32[4,1,4,8,128]{4,3,2,1,0:T(8,128)S(1)} %get-tuple-element.47, f32[4,1,4,8,128]{4,3,2,1,0:T(8,128)S(1)} %get-tuple-element.46, f32[4,1,4,8,128]{4,3,2,1,0:T(8,128)S(1)} %get-tuple-element.45, f32[4,3,4,8,128]{4,2,3,1,0:T(4,128)S(1)} %slice.532, f32[4,4,8,128]{3,2,1,0:T(8,128)S(1)} %slice.559, ...), kind=kLoop, calls=%fused_computation.103 | loop fusion | flops 393216 | bytes 870400 | tf_op jit(solution)/shard_map/add | solution.py:113
  53.6 3.2 %all-to-all-done = f32[4,1,2048]{2,1,0:T(1,128)S(1)} async-done(((f32[4,1,2048]{2,1,0:T(1,128)}), f32[4,1,2048]{2,1,0:T(1,128)S(1)}, u32[]{:S(2)}, u32[]{:S(2)}) %all-to-all-start) | async-done | bytes 32800 | tf_op jit(solution)/shard_map/all_to_all | solution.py:232
  56.8 0.5 broadcast.369
  57.3 0.7 %reduce.4 = f32[4,2048]{1,0:T(4,128)S(1)} reduce(f32[4,1,2048]{2,1,0:T(1,128)S(1)} %all-to-all-done, f32[]{:T(128)} %broadcast.369), dimensions={1}, to_apply=%all_to_all.4.reduce_sub_computation | reduce | bytes 65540 | tf_op jit(solution)/shard_map/all_to_all | solution.py:232
  58.1 0.6 %reshape.474 = f32[128,2,4,8]{3,2,1,0:T(4,128)S(1)} reshape(f32[4,2048]{1,0:T(4,128)S(1)} %reduce.4) | data formatting | bytes 65536
  58.9 0.7 %copy.263 = f32[2,4,8,32]{3,2,1,0:T(8,128)} copy(f32[2,4,8,32]{2,1,0,3:T(4,128)S(1)} %reduce_sum.82) | data formatting | bytes 16384
  (110 shorter events, 4.4 us)
Async XLA Ops:
  0.6 2.1 %copy-start.4 = (f32[4,8,128]{2,1,0:T(8,128)S(1)}, f32[4,8,128]{2,1,0:T(8,128)}, u32[]{:S(2)}) copy-start(f32[4,8,128]{2,1,0:T(8,128)} %param.20) | copy-start | bytes 49156
  0.6 2.1 %copy-start.3 = (f32[4,8,128]{2,1,0:T(8,128)S(1)}, f32[4,8,128]{2,1,0:T(8,128)}, u32[]{:S(2)}) copy-start(f32[4,8,128]{2,1,0:T(8,128)} %param.19) | copy-start | bytes 49156
  0.7 2.1 %copy-start.2 = (f32[4,8,128]{2,1,0:T(8,128)S(1)}, f32[4,8,128]{2,1,0:T(8,128)}, u32[]{:S(2)}) copy-start(f32[4,8,128]{2,1,0:T(8,128)} %param.18) | copy-start | bytes 49156
  2.6 6.9 %copy-start.8 = (s32[4]{0:T(128)S(1)}, s32[4]{0:T(128)}, u32[]{:S(2)}) copy-start(s32[4]{0:T(128)} %param.24) | copy-start | bytes 52
  2.7 7.0 %copy-start.9 = (s32[4]{0:T(128)S(1)}, s32[4]{0:T(128)}, u32[]{:S(2)}) copy-start(s32[4]{0:T(128)} %param.25) | copy-start | bytes 52
  2.7 7.1 %copy-start.6 = (f32[256,3]{0,1:T(4,128)S(1)}, f32[256,3]{0,1:T(4,128)}, u32[]{:S(2)}) copy-start(f32[256,3]{0,1:T(4,128)} %param.23) | copy-start | bytes 9220
  2.7 7.4 %copy-start.5 = (f32[4,256,3]{1,0,2:T(4,128)S(1)}, f32[4,256,3]{1,0,2:T(4,128)}, u32[]{:S(2)}) copy-start(f32[4,256,3]{1,0,2:T(4,128)} %param.26) | copy-start | bytes 36868
  2.8 7.8 %collective-permute-start.1 = (f32[48,8,128]{2,1,0:T(8,128)S(1)}, f32[48,8,128]{2,1,0:T(8,128)S(1)}, u32[]{:S(2)}, u32[]{:S(2)}) collective-permute-start(f32[48,8,128]{2,1,0:T(8,128)S(1)} %pad_maximum_fusion.7), channel_id=1, source_target_pairs={{8,0},{16,8},{24,16},{32,24},{40,32},{48,40},{56,48},{64,56},{72,6... | collective-permute-start | bytes 589832 | tf_op jit(solution)/shard_map/ppermute | solution.py:127
  5.2 13.5 %collective-permute-start = (f32[50,8,128]{2,1,0:T(8,128)S(1)}, f32[50,8,128]{2,1,0:T(8,128)S(1)}, u32[]{:S(2)}, u32[]{:S(2)}) collective-permute-start(f32[50,8,128]{2,1,0:T(8,128)S(1)} %pad_maximum_fusion.6), channel_id=1, source_target_pairs={{0,8},{8,16},{16,24},{24,32},{32,40},{40,48},{48,56},{56,64},{64,7... | collective-permute-start | bytes 614408 | tf_op jit(solution)/shard_map/ppermute | solution.py:124
  19.1 12.4 %collective-permute-start.2 = (f32[33,8,2,128]{3,1,2,0:T(8,128)S(1)}, f32[33,8,2,128]{3,1,2,0:T(8,128)S(1)}, u32[]{:S(2)}, u32[]{:S(2)}) collective-permute-start(f32[33,8,2,128]{3,1,2,0:T(8,128)S(1)} %get-tuple-element.30), channel_id=1, source_target_pairs={{0,1},{1,2},{2,3},{3,4},{4,5},{5,6},{6,7},{8,9},{9,10},{10,11},{11... | collective-permute-start | bytes 811016 | tf_op jit(solution)/shard_map/ppermute | solution.py:20
  28.1 7.8 %collective-permute-start.3 = (f32[33,8,2,128]{3,1,2,0:T(8,128)S(1)}, f32[33,8,2,128]{3,1,2,0:T(8,128)S(1)}, u32[]{:S(2)}, u32[]{:S(2)}) collective-permute-start(f32[33,8,2,128]{3,1,2,0:T(8,128)S(1)} %get-tuple-element.31), channel_id=1, source_target_pairs={{1,0},{2,1},{3,2},{4,3},{5,4},{6,5},{7,6},{9,8},{10,9},{11,10},{12... | collective-permute-start | bytes 811016 | tf_op jit(solution)/shard_map/ppermute | solution.py:22
  41.7 0.9 %copy-start = (f32[5,3,6,10,128]{4,3,2,0,1:T(8,128)}, f32[5,3,6,10,128]{4,3,2,0,1:T(8,128)S(1)}, u32[]{:S(2)}) copy-start(f32[5,3,6,10,128]{4,3,2,0,1:T(8,128)S(1)} %fusion.7) | copy-start | bytes 1382404
  42.6 1.1 %slice-start = ((f32[5,3,6,10,128]{4,3,2,0,1:T(8,128)}), f32[4,3,6,10,128]{4,3,2,0,1:T(8,128)S(1)}, s32[]{:S(2)}) async-start(f32[5,3,6,10,128]{4,3,2,0,1:T(8,128)} %copy-done), calls=%async_computation.1 | async-start | bytes 1179648 | tf_op jit(solution)/shard_map/slice | solution.py:210
  46.3 0.7 %copy-start.7 = (f32[6]{0:T(128)S(1)}, f32[6]{0:T(128)}, u32[]{:S(2)}) copy-start(f32[6]{0:T(128)} %constant.97.clone) | copy-start | bytes 76
  46.5 6.3 %copy-start.1 = (f32[5,3,6,10,128]{4,3,2,0,1:T(8,128)S(1)}, f32[5,3,6,10,128]{4,3,2,0,1:T(8,128)}, u32[]{:S(2)}) copy-start(f32[5,3,6,10,128]{4,3,2,0,1:T(8,128)} %copy-done) | copy-start | bytes 1382404
  48.5 8.3 %all-to-all-start = ((f32[4,1,2048]{2,1,0:T(1,128)}), f32[4,1,2048]{2,1,0:T(1,128)S(1)}, u32[]{:S(2)}, u32[]{:S(2)}) async-start(f32[4,1,2048]{2,1,0:T(1,128)} %reshape.473), calls=%async_computation | async-start | bytes 65536 | tf_op jit(solution)/shard_map/all_to_all | solution.py:232

commit v6 on v5

--- a/solution.py
+++ b/solution.py
@@ -142,6 +142,54 @@
         ]
     )
     return jnp.concatenate([rows_lo, stacked, rows_hi], axis=1)
+
+
+def up_z(cells):
+    top = lax.broadcasted_iota(jnp.int32, cells.shape, cells.ndim - 1) == cells.shape[-1] - 1
+    return jnp.where(top, 0.0, jnp.roll(cells, -1, axis=-1))
+
+
+def down_z(cells):
+    bottom = lax.broadcasted_iota(jnp.int32, cells.shape, cells.ndim - 1) == 0
+    return jnp.where(bottom, 0.0, jnp.roll(cells, 1, axis=-1))
+
+
+def dense_stencil(cells, lame, shear):
+    lower = cells[:, :, :-1]
+    grad_x = cells[:, :, 1:] - lower
+    grad_y = jnp.roll(lower, -1, axis=3) - lower
+    grad_z = up_z(lower) - lower
+    strain_xx = grad_x[:, 0]
+    strain_yy = grad_y[:, 1]
+    strain_zz = grad_z[:, 2]
+    strain_xy = 0.5 * (grad_y[:, 0] + grad_x[:, 1])
+    strain_xz = 0.5 * (grad_z[:, 0] + grad_x[:, 2])
+    strain_yz = 0.5 * (grad_z[:, 1] + grad_y[:, 2])
+    lame = lame[:-1]
+    shear = shear[:-1]
+    dilation = strain_xx + strain_yy + strain_zz
+    stress_xx = lame * dilation + 2.0 * shear * strain_xx
+    stress_yy = lame * dilation + 2.0 * shear * strain_yy
+    stress_zz = lame * dilation + 2.0 * shear * strain_zz
+    stress_xy = 2.0 * shear * strain_xy
+    stress_xz = 2.0 * shear * strain_xz
+    stress_yz = 2.0 * shear * strain_yz
+
+    def diff_x(stress):
+        return stress[:, 1:] - stress[:, :-1]
+
+    def diff_y(stress):
+        return (stress - jnp.roll(stress, 1, axis=2))[:, 1:]
+
+    def diff_z(stress):
+        return (stress - down_z(stress))[:, 1:]
+
+    force_x = diff_x(stress_xx) + diff_y(stress_xy) + diff_z(stress_xz)
+    force_y = diff_x(stress_xy) + diff_y(stress_yy) + diff_z(stress_yz)
+    force_z = diff_x(stress_xz) + diff_y(stress_yz) + diff_z(stress_zz)
+    force = jnp.stack([force_x, force_y, force_z], axis=1)
+    strain = jnp.stack([strain_xx, strain_yy, strain_zz, strain_xy, strain_xz, strain_yz], axis=1)
+    return (force, strain)
 
 
 def local(
@@ -173,9 +221,11 @@
     comps = fields * 3
     stacked = jnp.concatenate([now, lame_first[None], shear_mod[None], prev, buoyancy[None]])
     grown = with_halo(exchange_x(stacked, comps + 2, comps), (("gy", 2),), 2)
+    span_y = 16 * ((cells_y + 4 + 15) // 16)
+    grown = jnp.pad(grown, ((0, 0), (0, 0), (0, span_y - cells_y - 4), (0, 0)))
     now_grown = grown[:comps].reshape((fields, 3) + grown.shape[1:])
-    lame_grown = zpad(grown[comps])
-    shear_grown = zpad(grown[comps + 1])
+    lame_grown = grown[comps]
+    shear_grown = grown[comps + 1]
     prev_grown = grown[comps + 2 : 2 * comps + 2].reshape((fields, 3) + grown.shape[1:])
     buoy_grown = grown[2 * comps + 2]
 
@@ -189,35 +239,33 @@
         )
         for instant in range(STEPS)
     ]
-    masks_wide = locate(
-        cells, start_x - 1, start_y - 1, width_y, depth, cells_x + 2, cells_y + 2
-    )
-    masks = masks_wide[:, 1:-1, 1:-1]
-
-    force0, strain0 = stencil(zpad(now_grown), lame_grown, shear_grown)
-    now_wide = now_grown[:, :, 1:-1, 1:-1]
+    masks_wide = locate(cells, start_x - 1, start_y - 2, width_y, depth, cells_x + 2, span_y)
+    inner = (slice(None), slice(1, 1 + cells_x), slice(2, 2 + cells_y))
+
+    force0, strain0 = dense_stencil(now_grown, lame_grown, shear_grown)
+    now_wide = now_grown[:, :, 1:-1]
     next_wide = advance(
         now_wide,
-        prev_grown[:, :, 1:-1, 1:-1],
+        prev_grown[:, :, 1:-1],
         force0,
         amps[0],
         masks_wide,
-        buoy_grown[1:-1, 1:-1],
-    )
-    strain0 = strain0[:, :, 1:-1, 1:-1]
-
-    force1, strain1 = stencil(
-        zpad(next_wide[1:]), lame_grown[1:-1, 1:-1], shear_grown[1:-1, 1:-1]
-    )
-    master1 = stencil(zpad(next_wide[:1]), lame_grown[1:-1, 1:-1], shear_grown[1:-1, 1:-1])[1]
+        buoy_grown[1:-1],
+    )
+    strain0 = strain0[:, :, 2 : 2 + cells_x, 2 : 2 + cells_y]
+
+    force1, strain1 = dense_stencil(next_wide[1:], lame_grown[1:-1], shear_grown[1:-1])
+    master1 = dense_stencil(next_wide[:1], lame_grown[1:-1], shear_grown[1:-1])[1]
+    strain1 = strain1[:, :, 1 : 1 + cells_x, 2 : 2 + cells_y]
+    master1 = master1[:, :, 1 : 1 + cells_x, 2 : 2 + cells_y]
     final = advance(
-        next_wide[1:, :, 1:-1, 1:-1],
-        now_wide[1:, :, 1:-1, 1:-1],
+        next_wide[1:, :, 1 : 1 + cells_x],
+        now_wide[1:, :, 1 : 1 + cells_x],
         force1,
         amps[1][1:],
-        masks[1:],
-        buoy_grown[2:-2, 2:-2],
-    )
+        masks_wide[1:, 1 : 1 + cells_x],
+        buoy_grown[2 : 2 + cells_x],
+    )[:, :, :, 2 : 2 + cells_y]
 
     weights = jnp.array([1.0, 1.0, 1.0, 2.0, 2.0, 2.0], jnp.float32)[:, None, None, None]
     totals = jnp.zeros((2,) + grid, jnp.float32)

time: 60 us -> 55.1 us (0.918)
  other arithmetic: 13 us -> 8.36 us
    sub x4, other arithmetic: 3.68 us -> 0.71 us  [the longest x3 0.6 us: dense_stencil(): grad_y = jnp.roll(lower, -1, axis=3) - lower]
    add x4, other arithmetic: 1.35 us -> 0.48 us  [the longest x2 0.37 us: dense_stencil(): stress_xx = lame * dilation + 2.0 * shear * strain_xx]
    slice x14 -> x27, local copies, waits for them, and re-layouts: 1.26 us -> 1.88 us  [the longest x6 0.69 us: down_z(): return jnp.where(bottom, 0.0, jnp.roll(cells, 1, axis=-1))]
    unnamed x36 -> x34, local copies, waits for them, and re-layouts: 3.59 us -> 3.11 us
    another operation x5 -> x7, other arithmetic: 1.31 us -> 0.86 us  [the longest x4 0.77 us: dense_stencil(): force = jnp.stack([force_x, force_y, force_z], axis=1)]
where the time goes in v6:
time: 55.1 us; the launch traced here: 54.8 us
  starting transfers between devices  20.2 us (37%)
  waiting for transfers between devices  17.1 us (31%)
  other arithmetic  8.36 us (15%)
  local copies, waits for them, and re-layouts  6.23 us (11%)
  between operations  2.81 us (5%)
    ppermute x1, starting transfers between devices, with_halo(): lax.ppermute(tail, axis, [(i, i + 1) for i in range(ends)])  9.03 us
    ppermute x1, waiting for transfers between devices, exchange_x(): lax.ppermute(jnp.concatenate([wide_lo, thin_lo]), 'gx', [(i, i + 1) for i...  8.28 us
    ppermute x1, waiting for transfers between devices, with_halo(): lax.ppermute(head, axis, [(i + 1, i) for i in range(ends)])  4.4 us
    all_to_all x1, starting transfers between devices, local(): gathered = lax.all_to_all(totals, 'grp', 3, 0, tiled=True)  4.01 us
    all_to_all x1, waiting for transfers between devices, local(): gathered = lax.all_to_all(totals, 'grp', 3, 0, tiled=True)  3.24 us
    unnamed x34, local copies, waits for them, and re-layouts  3.11 us
    ppermute x1, starting transfers between devices, exchange_x(): lax.ppermute(jnp.concatenate([wide_lo, thin_lo]), 'gx', [(i, i + 1) for i...  2.92 us
    ppermute x1, starting transfers between devices, exchange_x(): lax.ppermute(jnp.concatenate([wide_hi, thin_hi]), 'gx', [(i + 1, i) for i...  2.36 us
  transfers between devices with their start and end apart: 5, of which 4 were waited for; matrix products, arithmetic and copies ran while one was open for 4% of the time, Pallas kernels for 0%

profile of v6, /device:TPU:321, one launch (start us, length us, event | category | flops | bytes accessed | tf_op | source)
XLA Modules:
  0.0 54.8 jit_solution(2218213634002831637)
XLA Ops:
  0.7 1.0 %pad_maximum_fusion.11 = f32[5,3,4,8,128]{4,3,2,1,0:T(8,128)S(1)} fusion(f32[4,3,4,8,128]{4,3,2,1,0:T(8,128)} %param.16, f32[1,3,4,8,128]{4,3,2,1,0:T(8,128)} %bitcast.272), kind=kLoop, calls=%fused_computation.87 | loop fusion | flops 61440 | bytes 491520 | tf_op jit(solution)/shard_map/concatenate | solution.py:219
  1.7 1.0 %pad_maximum_fusion.12 = f32[5,3,4,8,128]{4,3,2,1,0:T(8,128)S(1)} fusion(f32[4,3,4,8,128]{4,3,2,1,0:T(8,128)} %param.17, f32[1,3,4,8,128]{4,3,2,1,0:T(8,128)} %bitcast.273), kind=kLoop, calls=%fused_computation.88 | loop fusion | flops 61440 | bytes 491520 | tf_op jit(solution)/shard_map/concatenate | solution.py:220
  2.8 2.4 %collective-permute-start.1 = (f32[48,8,128]{2,1,0:T(8,128)S(1)}, f32[48,8,128]{2,1,0:T(8,128)S(1)}, u32[]{:S(2)}, u32[]{:S(2)}) collective-permute-start(f32[48,8,128]{2,1,0:T(8,128)S(1)} %pad_maximum_fusion.16), channel_id=1, source_target_pairs={{8,0},{16,8},{24,16},{32,24},{40,32},{48,40},{56,48},{64,56},{72,6... | collective-permute-start | bytes 589832 | tf_op jit(solution)/shard_map/ppermute | solution.py:127
  5.2 2.9 %collective-permute-start = (f32[50,8,128]{2,1,0:T(8,128)S(1)}, f32[50,8,128]{2,1,0:T(8,128)S(1)}, u32[]{:S(2)}, u32[]{:S(2)}) collective-permute-start(f32[50,8,128]{2,1,0:T(8,128)S(1)} %pad_maximum_fusion.13), channel_id=1, source_target_pairs={{0,8},{8,16},{16,24},{24,32},{32,40},{40,48},{48,56},{56,64},{64,7... | collective-permute-start | bytes 614408 | tf_op jit(solution)/shard_map/ppermute | solution.py:124
  10.5 8.3 %collective-permute-done = f32[50,8,128]{2,1,0:T(8,128)S(1)} collective-permute-done((f32[50,8,128]{2,1,0:T(8,128)S(1)}, f32[50,8,128]{2,1,0:T(8,128)S(1)}, u32[]{:S(2)}, u32[]{:S(2)}) %collective-permute-start) | collective-permute-done | bytes 204832 | tf_op jit(solution)/shard_map/ppermute | solution.py:124
  18.8 0.2 maximum_maximum_fusion
  19.0 9.0 %collective-permute-start.2 = (f32[33,8,2,128]{3,2,0,1:T(2,128)S(1)}, f32[33,8,2,128]{3,2,0,1:T(2,128)S(1)}, u32[]{:S(2)}, u32[]{:S(2)}) collective-permute-start(f32[33,8,2,128]{3,2,0,1:T(2,128)S(1)} %get-tuple-element.21), channel_id=1, source_target_pairs={{0,1},{1,2},{2,3},{3,4},{4,5},{5,6},{6,7},{8,9},{9,10},{10,11},{11... | collective-permute-start | bytes 811016 | tf_op jit(solution)/shard_map/ppermute | solution.py:20
  28.0 1.9 %collective-permute-start.3 = (f32[33,8,2,128]{3,2,0,1:T(2,128)S(1)}, f32[33,8,2,128]{3,2,0,1:T(2,128)S(1)}, u32[]{:S(2)}, u32[]{:S(2)}) collective-permute-start(f32[33,8,2,128]{3,2,0,1:T(2,128)S(1)} %get-tuple-element.22), channel_id=1, source_target_pairs={{1,0},{2,1},{3,2},{4,3},{5,4},{6,5},{7,6},{9,8},{10,9},{11,10},{12... | collective-permute-start | bytes 811016 | tf_op jit(solution)/shard_map/ppermute | solution.py:22
  30.2 1.2 %collective-permute-done.2 = f32[33,8,2,128]{3,2,0,1:T(2,128)S(1)} collective-permute-done((f32[33,8,2,128]{3,2,0,1:T(2,128)S(1)}, f32[33,8,2,128]{3,2,0,1:T(2,128)S(1)}, u32[]{:S(2)}, u32[]{:S(2)}) %collective-permute-start.2) | collective-permute-done | bytes 270368 | tf_op jit(solution)/shard_map/ppermute | solution.py:20
  31.4 4.4 %collective-permute-done.3 = f32[33,8,2,128]{3,2,0,1:T(2,128)S(1)} collective-permute-done((f32[33,8,2,128]{3,2,0,1:T(2,128)S(1)}, f32[33,8,2,128]{3,2,0,1:T(2,128)S(1)}, u32[]{:S(2)}, u32[]{:S(2)}) %collective-permute-start.3) | collective-permute-done | bytes 270368 | tf_op jit(solution)/shard_map/ppermute | solution.py:22
  35.8 0.6 %select_maximum_fusion = f32[33,8,16,128]{3,2,0,1:T(8,128)S(1)} fusion(f32[33,8,2,128]{3,2,0,1:T(2,128)S(1)} %collective-permute-done.3, f32[33,8,2,128]{3,2,0,1:T(2,128)S(1)} %collective-permute-done.2, f32[18,2,8,128]{3,2,0,1:T(8,128)S(1)} %concatenate.162, f32[33,4,8,128]{3,2,0,1:T(8,128)S(1)} %constant_dynamic-update-slice_fusion, ...), kind=kLoop, calls=%fused_computation | loop fusion | flops 7569408 | bytes 3784704 | tf_op jit(solution)/shard_map/concatenate | solution.py:18
  36.5 0.2 fusion.89
  36.8 0.3 slice.639
  37.4 0.3 pad_maximum_fusion
  37.7 0.3 copy_subtract_fusion
  38.0 0.3 fusion.18
  38.9 0.2 fusion.21
  39.1 0.3 fusion.33
  39.4 0.3 fusion.11
  39.9 0.2 slice.683
  40.1 0.2 maximum_subtract_fusion
  41.8 0.4 copy-done.5
  42.3 0.3 copy.207
  42.5 1.2 %reshape.519 = f32[4,1,2048]{2,1,0:T(1,128)} reshape(f32[128,2,4,8]{3,2,1,0:T(4,128)S(1)} %bitcast.255) | data formatting | bytes 65536
  43.7 4.0 %all-to-all-start = ((f32[4,1,2048]{2,1,0:T(1,128)}), f32[4,1,2048]{2,1,0:T(1,128)S(1)}, u32[]{:S(2)}, u32[]{:S(2)}) async-start(f32[4,1,2048]{2,1,0:T(1,128)} %reshape.519), calls=%async_computation | async-start | bytes 65536 | tf_op jit(solution)/shard_map/all_to_all | solution.py:280
  47.8 0.2 fusion.56
  48.0 0.8 %fusion.36 = f32[4,3,4,8,128]{4,3,2,1,0:T(8,128)} fusion(f32[4,3,4,16,128]{4,3,2,1,0:T(8,128)S(1)} %slice.674, f32[4,1,4,16,128]{4,3,2,1,0:T(8,128)S(1)} %fusion.44, f32[4,1,4,16,128]{4,3,2,1,0:T(8,128)S(1)} %get-tuple-element.43, f32[4,1,4,16,128]{4,3,2,1,0:T(8,128)S(1)} %get-tuple-element.42, f32[4,8,128]{2,1,0:T(8,128)S(1)} %slice.721, ...), kind=kLoop, calls=%fused_computation.92 | loop fusion | flops 344064 | bytes 1067008 | tf_op jit(solution)/shard_map/add | solution.py:113
  48.7 3.2 %all-to-all-done = f32[4,1,2048]{2,1,0:T(1,128)S(1)} async-done(((f32[4,1,2048]{2,1,0:T(1,128)}), f32[4,1,2048]{2,1,0:T(1,128)S(1)}, u32[]{:S(2)}, u32[]{:S(2)}) %all-to-all-start) | async-done | bytes 32800 | tf_op jit(solution)/shard_map/all_to_all | solution.py:280
  52.0 0.5 broadcast.415
  52.5 0.7 %reduce.4 = f32[4,2048]{1,0:T(4,128)S(1)} reduce(f32[4,1,2048]{2,1,0:T(1,128)S(1)} %all-to-all-done, f32[]{:T(128)} %broadcast.415), dimensions={1}, to_apply=%all_to_all.4.reduce_sub_computation | reduce | bytes 65540 | tf_op jit(solution)/shard_map/all_to_all | solution.py:280
  53.2 0.6 %reshape.520 = f32[128,2,4,8]{3,2,1,0:T(4,128)S(1)} reshape(f32[4,2048]{1,0:T(4,128)S(1)} %reduce.4) | data formatting | bytes 65536
  54.0 0.7 %copy.208 = f32[2,4,8,32]{3,2,1,0:T(8,128)} copy(f32[2,4,8,32]{2,1,0,3:T(4,128)S(1)} %reduce_sum.82) | data formatting | bytes 16384
  (120 shorter events, 4.1 us)
Async XLA Ops:
  0.6 2.1 %copy-start.2 = (f32[4,8,128]{2,1,0:T(8,128)S(1)}, f32[4,8,128]{2,1,0:T(8,128)}, u32[]{:S(2)}) copy-start(f32[4,8,128]{2,1,0:T(8,128)} %param.20) | copy-start | bytes 49156
  0.6 2.1 %copy-start.1 = (f32[4,8,128]{2,1,0:T(8,128)S(1)}, f32[4,8,128]{2,1,0:T(8,128)}, u32[]{:S(2)}) copy-start(f32[4,8,128]{2,1,0:T(8,128)} %param.19) | copy-start | bytes 49156
  0.7 2.1 %copy-start = (f32[4,8,128]{2,1,0:T(8,128)S(1)}, f32[4,8,128]{2,1,0:T(8,128)}, u32[]{:S(2)}) copy-start(f32[4,8,128]{2,1,0:T(8,128)} %param.18) | copy-start | bytes 49156
  1.7 7.9 %copy-start.6 = (s32[4]{0:T(128)S(1)}, s32[4]{0:T(128)}, u32[]{:S(2)}) copy-start(s32[4]{0:T(128)} %param.24) | copy-start | bytes 52
  1.7 8.0 %copy-start.7 = (s32[4]{0:T(128)S(1)}, s32[4]{0:T(128)}, u32[]{:S(2)}) copy-start(s32[4]{0:T(128)} %param.25) | copy-start | bytes 52
  1.7 8.2 %copy-start.4 = (f32[256,3]{0,1:T(4,128)S(1)}, f32[256,3]{0,1:T(4,128)}, u32[]{:S(2)}) copy-start(f32[256,3]{0,1:T(4,128)} %param.23) | copy-start | bytes 9220
  1.7 8.6 %copy-start.3 = (f32[4,256,3]{1,0,2:T(4,128)S(1)}, f32[4,256,3]{1,0,2:T(4,128)}, u32[]{:S(2)}) copy-start(f32[4,256,3]{1,0,2:T(4,128)} %param.26) | copy-start | bytes 36868
  2.8 7.7 %collective-permute-start.1 = (f32[48,8,128]{2,1,0:T(8,128)S(1)}, f32[48,8,128]{2,1,0:T(8,128)S(1)}, u32[]{:S(2)}, u32[]{:S(2)}) collective-permute-start(f32[48,8,128]{2,1,0:T(8,128)S(1)} %pad_maximum_fusion.16), channel_id=1, source_target_pairs={{8,0},{16,8},{24,16},{32,24},{40,32},{48,40},{56,48},{64,56},{72,6... | collective-permute-start | bytes 589832 | tf_op jit(solution)/shard_map/ppermute | solution.py:127
  5.2 13.5 %collective-permute-start = (f32[50,8,128]{2,1,0:T(8,128)S(1)}, f32[50,8,128]{2,1,0:T(8,128)S(1)}, u32[]{:S(2)}, u32[]{:S(2)}) collective-permute-start(f32[50,8,128]{2,1,0:T(8,128)S(1)} %pad_maximum_fusion.13), channel_id=1, source_target_pairs={{0,8},{8,16},{16,24},{24,32},{32,40},{40,48},{48,56},{56,64},{64,7... | collective-permute-start | bytes 614408 | tf_op jit(solution)/shard_map/ppermute | solution.py:124
  19.0 12.4 %collective-permute-start.2 = (f32[33,8,2,128]{3,2,0,1:T(2,128)S(1)}, f32[33,8,2,128]{3,2,0,1:T(2,128)S(1)}, u32[]{:S(2)}, u32[]{:S(2)}) collective-permute-start(f32[33,8,2,128]{3,2,0,1:T(2,128)S(1)} %get-tuple-element.21), channel_id=1, source_target_pairs={{0,1},{1,2},{2,3},{3,4},{4,5},{5,6},{6,7},{8,9},{9,10},{10,11},{11... | collective-permute-start | bytes 811016 | tf_op jit(solution)/shard_map/ppermute | solution.py:20
  28.0 7.8 %collective-permute-start.3 = (f32[33,8,2,128]{3,2,0,1:T(2,128)S(1)}, f32[33,8,2,128]{3,2,0,1:T(2,128)S(1)}, u32[]{:S(2)}, u32[]{:S(2)}) collective-permute-start(f32[33,8,2,128]{3,2,0,1:T(2,128)S(1)} %get-tuple-element.22), channel_id=1, source_target_pairs={{1,0},{2,1},{3,2},{4,3},{5,4},{6,5},{7,6},{9,8},{10,9},{11,10},{12... | collective-permute-start | bytes 811016 | tf_op jit(solution)/shard_map/ppermute | solution.py:22
  41.5 0.7 %copy-start.5 = (f32[6]{0:T(128)S(1)}, f32[6]{0:T(128)}, u32[]{:S(2)}) copy-start(f32[6]{0:T(128)} %constant.98.clone) | copy-start | bytes 76
  43.7 8.3 %all-to-all-start = ((f32[4,1,2048]{2,1,0:T(1,128)}), f32[4,1,2048]{2,1,0:T(1,128)S(1)}, u32[]{:S(2)}, u32[]{:S(2)}) async-start(f32[4,1,2048]{2,1,0:T(1,128)} %reshape.519), calls=%async_computation | async-start | bytes 65536 | tf_op jit(solution)/shard_map/all_to_all | solution.py:280

commit v7 on v6

--- a/solution.py
+++ b/solution.py
@@ -113,20 +113,12 @@
     return 2.0 * current - earlier + time_step_sq * buoyancy * (force + source)
 
 
-def exchange_x(stacked, pairs_lo, pairs_hi):
+def exchange_x(stacked, send_lo, send_hi, pairs_lo, pairs_hi):
     channels, cells_x, cells_y, depth = stacked.shape
     plane = (cells_y, depth)
     count = lax.axis_size("gx")
-    wide_lo = stacked[:pairs_lo, cells_x - 2 :].reshape((-1,) + plane)
-    thin_lo = stacked[pairs_lo:, cells_x - 1 :].reshape((-1,) + plane)
-    wide_hi = stacked[:pairs_hi, :2].reshape((-1,) + plane)
-    thin_hi = stacked[pairs_hi:, :1].reshape((-1,) + plane)
-    from_lo = lax.ppermute(
-        jnp.concatenate([wide_lo, thin_lo]), "gx", [(i, i + 1) for i in range(count - 1)]
-    )
-    from_hi = lax.ppermute(
-        jnp.concatenate([wide_hi, thin_hi]), "gx", [(i + 1, i) for i in range(count - 1)]
-    )
+    from_lo = lax.ppermute(send_lo, "gx", [(i, i + 1) for i in range(count - 1)])
+    from_hi = lax.ppermute(send_hi, "gx", [(i + 1, i) for i in range(count - 1)])
     blank = jnp.zeros((channels - pairs_lo, 1) + plane, jnp.float32)
     rows_lo = jnp.concatenate(
         [
@@ -220,7 +212,28 @@
     prev = jnp.concatenate([fwd_prev[None], adj_prev]).reshape((fields * 3,) + grid)
     comps = fields * 3
     stacked = jnp.concatenate([now, lame_first[None], shear_mod[None], prev, buoyancy[None]])
-    grown = with_halo(exchange_x(stacked, comps + 2, comps), (("gy", 2),), 2)
+    plane = (cells_y, depth)
+
+    def rows(first, last):
+        parts = [
+            fwd_now[:, first:last],
+            adj_now[:, :, first:last].reshape((receivers * 3, last - first) + plane),
+            lame_first[None, first:last],
+            shear_mod[None, first:last],
+            fwd_prev[:, first:last],
+            adj_prev[:, :, first:last].reshape((receivers * 3, last - first) + plane),
+            buoyancy[None, first:last],
+        ]
+        return [part.reshape((-1,) + plane) for part in parts]
+
+    last_two = rows(cells_x - 2, cells_x)
+    last_one = rows(cells_x - 1, cells_x)
+    first_two = rows(0, 2)
+    first_one = rows(0, 1)
+    send_lo = jnp.concatenate(last_two[:4] + last_one[4:])
+    send_hi = jnp.concatenate(first_two[:2] + first_one[2:])
+    grown = exchange_x(stacked, send_lo, send_hi, comps + 2, comps)
+    grown = with_halo(grown, (("gy", 2),), 2)
     span_y = 16 * ((cells_y + 4 + 15) // 16)
     grown = jnp.pad(grown, ((0, 0), (0, 0), (0, span_y - cells_y - 4), (0, 0)))
     now_grown = grown[:comps].reshape((fields, 3) + grown.shape[1:])

time: 55.1 us -> 59.9 us (1.087)
  local copies, waits for them, and re-layouts: 6.23 us -> 13 us
  waiting for transfers between devices: 17.1 us -> 13.3 us
  other arithmetic: 8.36 us -> 10 us
    ppermute x2, waiting for transfers between devices: 8.33 us -> 4.53 us  [the longest x1 4.53 us: exchange_x(): lax.ppermute(send_lo, 'gx', [(i, i + 1) for i in range(count - 1)])]
    unnamed x34 -> x42, local copies, waits for them, and re-layouts: 3.11 us -> 6.65 us
    slice x4 -> x3, local copies, waits for them, and re-layouts: 0.13 us -> 2.66 us  [the longest x1 0.96 us: rows(): adj_now[:, :, first:last].reshape((receivers * 3, last - first) + plane)]
    concatenate x2 -> x1, local copies, waits for them, and re-layouts: 0.04 us -> 0.71 us  [local(): send_lo = jnp.concatenate(last_two[:4] + last_one[4:])]
    sub x1, other arithmetic: 0.09 us -> 0.75 us  [locate(): coord_x = cells // (width_y * depth) - start_x]
    add x1, other arithmetic: 0.01 us -> 0.66 us  [local(): receiver_lag + instant]
    eq x2, other arithmetic: 0.08 us -> 0.73 us  [pick(): chosen = positions == lags[:, None]]
  transfers between devices with their start and end apart: 5 -> 5, of which waited for: 4 -> 4; matrix products, arithmetic and copies ran while one was open for 4% -> 10% of each run, Pallas kernels for 0% -> 0%
where the time goes in v7:
time: 59.9 us; the launch traced here: 59.1 us
  starting transfers between devices  20.1 us (34%)
  waiting for transfers between devices  13.3 us (22%)
  local copies, waits for them, and re-layouts  13 us (22%)
  other arithmetic  10 us (17%)
  between operations  2.76 us (5%)
    ppermute x1, starting transfers between devices, with_halo(): lax.ppermute(tail, axis, [(i, i + 1) for i in range(ends)])  8.89 us
    unnamed x42, local copies, waits for them, and re-layouts  6.65 us
    ppermute x1, waiting for transfers between devices, exchange_x(): lax.ppermute(send_lo, 'gx', [(i, i + 1) for i in range(count - 1)])  4.53 us
    ppermute x1, waiting for transfers between devices, with_halo(): lax.ppermute(head, axis, [(i + 1, i) for i in range(ends)])  4.4 us
    all_to_all x1, starting transfers between devices, local(): gathered = lax.all_to_all(totals, 'grp', 3, 0, tiled=True)  4.01 us
    all_to_all x1, waiting for transfers between devices, local(): gathered = lax.all_to_all(totals, 'grp', 3, 0, tiled=True)  3.24 us
    ppermute x1, starting transfers between devices, exchange_x(): lax.ppermute(send_lo, 'gx', [(i, i + 1) for i in range(count - 1)])  2.92 us
    ppermute x1, starting transfers between devices, exchange_x(): lax.ppermute(send_hi, 'gx', [(i + 1, i) for i in range(count - 1)])  2.35 us
  transfers between devices with their start and end apart: 5, of which 4 were waited for; matrix products, arithmetic and copies ran while one was open for 10% of the time, Pallas kernels for 0%

profile of v7, /device:TPU:321, one launch (start us, length us, event | category | flops | bytes accessed | tf_op | source)
XLA Modules:
  0.0 59.1 jit_solution(5024781566722300427)
XLA Ops:
  0.7 0.9 %fusion.91 = (f32[3,2,8,128]{3,2,1,0:T(8,128)S(1)}, f32[3,2,8,128]{3,2,1,0:T(8,128)S(1)}) fusion(f32[3,4,8,128]{3,2,1,0:T(8,128)} %param.14), kind=kLoop, calls=%fused_computation.259 | loop fusion | bytes 98304 | tf_op jit(solution)/shard_map/slice | solution.py:219
  1.6 0.8 %fusion.89 = (f32[4,3,1,8,128]{4,3,2,1,0:T(8,128)S(1)}, f32[4,3,1,8,128]{4,3,2,1,0:T(8,128)S(1)}) fusion(f32[4,3,4,8,128]{4,3,2,1,0:T(8,128)} %param.17), kind=kLoop, calls=%fused_computation.257 | loop fusion | bytes 196608 | tf_op jit(solution)/shard_map/slice | solution.py:224
  2.4 1.0 %fusion.90 = (f32[4,3,2,8,128]{4,3,2,1,0:T(8,128)S(1)}, f32[4,3,2,8,128]{4,3,2,1,0:T(8,128)S(1)}) fusion(f32[4,3,4,8,128]{4,3,2,1,0:T(8,128)} %param.16), kind=kLoop, calls=%fused_computation.258 | loop fusion | bytes 393216 | tf_op jit(solution)/shard_map/slice | solution.py:220
  3.4 0.7 %constant_dynamic-update-slice_fusion.4 = f32[50,8,128]{2,1,0:T(8,128)S(1)} fusion(f32[50,8,128]{2,1,0:T(8,128)S(1)} %constant_dynamic-update-slice_fusion.5, f32[4,8,128]{2,1,0:T(8,128)} %param.18), kind=kLoop, calls=%fused_computation.162 | loop fusion | bytes 16384
  4.1 0.7 %constant_dynamic-update-slice_fusion.16 = f32[48,8,128]{2,1,0:T(8,128)S(1)} fusion(f32[48,8,128]{2,1,0:T(8,128)S(1)} %constant_dynamic-update-slice_fusion.17, f32[4,8,128]{2,1,0:T(8,128)} %param.18), kind=kLoop, calls=%fused_computation.174 | loop fusion | bytes 8192
  4.8 0.7 %constant_dynamic-update-slice_fusion.3 = f32[50,8,128]{2,1,0:T(8,128)S(1)} fusion(f32[50,8,128]{2,1,0:T(8,128)S(1)} %constant_dynamic-update-slice_fusion.4, f32[4,8,128]{2,1,0:T(8,128)} %param.19), kind=kLoop, calls=%fused_computation.161 | loop fusion | bytes 16384
  5.5 0.7 %constant_dynamic-update-slice_fusion.15 = f32[48,8,128]{2,1,0:T(8,128)S(1)} fusion(f32[48,8,128]{2,1,0:T(8,128)S(1)} %constant_dynamic-update-slice_fusion.16, f32[4,8,128]{2,1,0:T(8,128)} %param.19), kind=kLoop, calls=%fused_computation.173 | loop fusion | bytes 8192
  6.2 0.7 %constant_dynamic-update-slice_fusion.2 = (f32[50,8,128]{2,1,0:T(8,128)S(1)}, f32[48,8,128]{2,1,0:T(8,128)S(1)}) fusion(f32[50,8,128]{2,1,0:T(8,128)S(1)} %constant_dynamic-update-slice_fusion.3, f32[3,4,8,128]{3,2,1,0:T(8,128)} %param.15, f32[48,8,128]{2,1,0:T(8,128)S(1)} %constant_dynamic-update-slice_fusion.15), kind=kLoop, calls=%fused_computation.160 | loop fusion | bytes 49152
  6.9 0.7 %constant_dynamic-update-slice_fusion = (f32[50,8,128]{2,1,0:T(8,128)S(1)}, f32[48,8,128]{2,1,0:T(8,128)S(1)}) fusion(f32[50,8,128]{2,1,0:T(8,128)S(1)} %get-tuple-element.57, f32[4,8,128]{2,1,0:T(8,128)} %param.20, f32[48,8,128]{2,1,0:T(8,128)S(1)} %get-tuple-element.58), kind=kLoop, calls=%fused_computation.158 | loop fusion | bytes 16384 | tf_op jit(solution)/shard_map/concatenate | solution.py:233
  7.6 2.3 %collective-permute-start.1 = (f32[48,8,128]{2,1,0:T(8,128)S(1)}, f32[48,8,128]{2,1,0:T(8,128)S(1)}, u32[]{:S(2)}, u32[]{:S(2)}) collective-permute-start(f32[48,8,128]{2,1,0:T(8,128)S(1)} %get-tuple-element.53), channel_id=1, source_target_pairs={{8,0},{16,8},{24,16},{32,24},{40,32},{48,40},{56,48},{64,56},{72,6... | collective-permute-start | bytes 589832 | tf_op jit(solution)/shard_map/ppermute | solution.py:121
  10.0 2.9 %collective-permute-start = (f32[50,8,128]{2,1,0:T(8,128)S(1)}, f32[50,8,128]{2,1,0:T(8,128)S(1)}, u32[]{:S(2)}, u32[]{:S(2)}) collective-permute-start(f32[50,8,128]{2,1,0:T(8,128)S(1)} %get-tuple-element.52), channel_id=1, source_target_pairs={{0,8},{8,16},{16,24},{24,32},{32,40},{40,48},{48,56},{56,64},{64,7... | collective-permute-start | bytes 614408 | tf_op jit(solution)/shard_map/ppermute | solution.py:120
  14.2 0.7 %fusion.84 = (s32[5]{0:T(128)S(1)}, s32[5]{0:T(128)S(1)}, s32[5]{0:T(128)S(1)}) fusion(s32[]{:T(128)S(6)} %sub.134, s32[4]{0:T(128)} %param.24, s32[1]{0:T(128)S(6)} %copy.216, s32[]{:T(128)S(6)} %sub.138), kind=kLoop, calls=%fused_computation.252 | loop fusion | flops 215 | bytes 88 | tf_op jit(solution)/shard_map/sub | solution.py:91
  15.1 0.7 %broadcast_add_fusion = s32[4]{0:T(128)S(1)} fusion(s32[4]{0:T(128)} %param.25), kind=kLoop, calls=%fused_computation.253 | loop fusion | flops 4 | bytes 32 | tf_op jit(solution)/shard_map/add | solution.py:250
  15.9 0.7 %iota_compare_fusion.1 = (pred[4,256]{1,0:T(4,128)(4,1)S(1)}, pred[4,256]{1,0:T(4,128)(4,1)S(1)}) fusion(s32[4]{0:T(128)S(1)} %broadcast_add_fusion, s32[4]{0:T(128)} %param.25), kind=kLoop, calls=%fused_computation.228 | loop fusion | flops 2048 | bytes 2080 | tf_op jit(solution)/shard_map/eq | solution.py:107
  16.6 0.9 %pad_maximum_fusion.12 = f32[5,3,4,8,128]{4,3,2,1,0:T(8,128)S(1)} fusion(f32[4,3,4,8,128]{4,3,2,1,0:T(8,128)} %param.17, f32[1,3,4,8,128]{4,3,2,1,0:T(8,128)} %bitcast.272), kind=kLoop, calls=%fused_computation.88 | loop fusion | flops 61440 | bytes 491520 | tf_op jit(solution)/shard_map/concatenate | solution.py:212
  17.6 0.8 %pad_maximum_fusion.11 = f32[5,3,4,8,128]{4,3,2,1,0:T(8,128)S(1)} fusion(f32[4,3,4,8,128]{4,3,2,1,0:T(8,128)S(1)} %copy-done, f32[1,3,4,8,128]{4,3,2,1,0:T(8,128)} %bitcast.271), kind=kLoop, calls=%fused_computation.87 | loop fusion | flops 61440 | bytes 491520 | tf_op jit(solution)/shard_map/concatenate | solution.py:211
  19.0 4.5 %collective-permute-done = f32[50,8,128]{2,1,0:T(8,128)S(1)} collective-permute-done((f32[50,8,128]{2,1,0:T(8,128)S(1)}, f32[50,8,128]{2,1,0:T(8,128)S(1)}, u32[]{:S(2)}, u32[]{:S(2)}) %collective-permute-start) | collective-permute-done | bytes 204832 | tf_op jit(solution)/shard_map/ppermute | solution.py:120
  23.7 8.9 %collective-permute-start.2 = (f32[33,8,2,128]{3,2,1,0:T(2,128)S(1)}, f32[33,8,2,128]{3,2,1,0:T(2,128)S(1)}, u32[]{:S(2)}, u32[]{:S(2)}) collective-permute-start(f32[33,8,2,128]{3,2,1,0:T(2,128)S(1)} %get-tuple-element.21), channel_id=1, source_target_pairs={{0,1},{1,2},{2,3},{3,4},{4,5},{5,6},{6,7},{8,9},{9,10},{10,11},{11... | collective-permute-start | bytes 811016 | tf_op jit(solution)/shard_map/ppermute | solution.py:20
  32.6 1.9 %collective-permute-start.3 = (f32[33,8,2,128]{3,2,1,0:T(2,128)S(1)}, f32[33,8,2,128]{3,2,1,0:T(2,128)S(1)}, u32[]{:S(2)}, u32[]{:S(2)}) collective-permute-start(f32[33,8,2,128]{3,2,1,0:T(2,128)S(1)} %get-tuple-element.22), channel_id=1, source_target_pairs={{1,0},{2,1},{3,2},{4,3},{5,4},{6,5},{7,6},{9,8},{10,9},{11,10},{12... | collective-permute-start | bytes 811016 | tf_op jit(solution)/shard_map/ppermute | solution.py:22
  34.9 1.2 %collective-permute-done.2 = f32[33,8,2,128]{3,2,1,0:T(2,128)S(1)} collective-permute-done((f32[33,8,2,128]{3,2,1,0:T(2,128)S(1)}, f32[33,8,2,128]{3,2,1,0:T(2,128)S(1)}, u32[]{:S(2)}, u32[]{:S(2)}) %collective-permute-start.2) | collective-permute-done | bytes 270368 | tf_op jit(solution)/shard_map/ppermute | solution.py:20
  36.0 4.4 %collective-permute-done.3 = f32[33,8,2,128]{3,2,1,0:T(2,128)S(1)} collective-permute-done((f32[33,8,2,128]{3,2,1,0:T(2,128)S(1)}, f32[33,8,2,128]{3,2,1,0:T(2,128)S(1)}, u32[]{:S(2)}, u32[]{:S(2)}) %collective-permute-start.3) | collective-permute-done | bytes 270368 | tf_op jit(solution)/shard_map/ppermute | solution.py:22
  40.4 0.6 %select_maximum_fusion = f32[33,8,16,128]{3,2,1,0:T(8,128)S(1)} fusion(f32[33,8,2,128]{3,2,1,0:T(2,128)S(1)} %collective-permute-done.3, f32[33,8,2,128]{3,2,1,0:T(2,128)S(1)} %collective-permute-done.2, f32[18,2,8,128]{3,2,1,0:T(8,128)S(1)} %concatenate.150, f32[15,2,8,128]{3,2,1,0:T(8,128)S(1)} %bitcast.262, ...), kind=kLoop, calls=%fused_computation | loop fusion | flops 7569408 | bytes 3784704 | tf_op jit(solution)/shard_map/concatenate | solution.py:18
  41.9 0.5 copy_subtract_fusion
  46.1 0.4 copy-done.6
  46.9 1.2 %reshape.519 = f32[4,1,2048]{2,1,0:T(1,128)} reshape(f32[128,2,4,8]{3,2,1,0:T(4,128)S(1)} %bitcast.257) | data formatting | bytes 65536
  48.1 4.0 %all-to-all-start = ((f32[4,1,2048]{2,1,0:T(1,128)}), f32[4,1,2048]{2,1,0:T(1,128)S(1)}, u32[]{:S(2)}, u32[]{:S(2)}) async-start(f32[4,1,2048]{2,1,0:T(1,128)} %reshape.519), calls=%async_computation | async-start | bytes 65536 | tf_op jit(solution)/shard_map/all_to_all | solution.py:293
  52.3 0.8 %fusion.36 = f32[4,3,4,8,128]{4,3,2,1,0:T(8,128)} fusion(f32[4,3,4,16,128]{4,3,2,1,0:T(8,128)S(1)} %slice.710, f32[4,1,4,16,128]{4,3,2,1,0:T(8,128)S(1)} %fusion.44, f32[4,1,4,16,128]{4,3,2,1,0:T(8,128)S(1)} %get-tuple-element.47, f32[4,1,4,16,128]{4,3,2,1,0:T(8,128)S(1)} %get-tuple-element.46, f32[4,8,128]{2,1,0:T(8,128)S(1)} %slice.757, ...), kind=kLoop, calls=%fused_computation.91 | loop fusion | flops 344064 | bytes 1067008 | tf_op jit(solution)/shard_map/add | solution.py:113
  53.1 3.2 %all-to-all-done = f32[4,1,2048]{2,1,0:T(1,128)S(1)} async-done(((f32[4,1,2048]{2,1,0:T(1,128)}), f32[4,1,2048]{2,1,0:T(1,128)S(1)}, u32[]{:S(2)}, u32[]{:S(2)}) %all-to-all-start) | async-done | bytes 32800 | tf_op jit(solution)/shard_map/all_to_all | solution.py:293
  56.4 0.5 broadcast.415
  56.9 0.7 %reduce.4 = f32[4,2048]{1,0:T(4,128)S(1)} reduce(f32[4,1,2048]{2,1,0:T(1,128)S(1)} %all-to-all-done, f32[]{:T(128)} %broadcast.415), dimensions={1}, to_apply=%all_to_all.4.reduce_sub_computation | reduce | bytes 65540 | tf_op jit(solution)/shard_map/all_to_all | solution.py:293
  57.6 0.6 %reshape.520 = f32[128,2,4,8]{3,2,1,0:T(4,128)S(1)} reshape(f32[4,2048]{1,0:T(4,128)S(1)} %reduce.4) | data formatting | bytes 65536
  58.4 0.7 %copy.150 = f32[2,4,8,32]{3,2,1,0:T(8,128)} copy(f32[2,4,8,32]{2,1,0,3:T(4,128)S(1)} %reduce_sum.82) | data formatting | bytes 16384
  (120 shorter events, 6.2 us)
Async XLA Ops:
  0.6 16.9 %copy-start = (f32[4,3,4,8,128]{4,3,2,1,0:T(8,128)S(1)}, f32[4,3,4,8,128]{4,3,2,1,0:T(8,128)}, u32[]{:S(2)}) copy-start(f32[4,3,4,8,128]{4,3,2,1,0:T(8,128)} %param.16) | copy-start | bytes 589828
  0.6 17.8 %copy-start.1 = (f32[4,8,128]{2,1,0:T(8,128)S(1)}, f32[4,8,128]{2,1,0:T(8,128)}, u32[]{:S(2)}) copy-start(f32[4,8,128]{2,1,0:T(8,128)} %param.18) | copy-start | bytes 49156
  0.7 17.8 %copy-start.2 = (f32[4,8,128]{2,1,0:T(8,128)S(1)}, f32[4,8,128]{2,1,0:T(8,128)}, u32[]{:S(2)}) copy-start(f32[4,8,128]{2,1,0:T(8,128)} %param.19) | copy-start | bytes 49156
  0.7 18.3 %copy-start.3 = (f32[4,8,128]{2,1,0:T(8,128)S(1)}, f32[4,8,128]{2,1,0:T(8,128)}, u32[]{:S(2)}) copy-start(f32[4,8,128]{2,1,0:T(8,128)} %param.20) | copy-start | bytes 49156
  0.7 17.8 %copy-start.5 = (f32[256,3]{0,1:T(4,128)S(1)}, f32[256,3]{0,1:T(4,128)}, u32[]{:S(2)}) copy-start(f32[256,3]{0,1:T(4,128)} %param.23) | copy-start | bytes 9220
  0.7 18.1 %copy-start.4 = (f32[4,256,3]{1,0,2:T(4,128)S(1)}, f32[4,256,3]{1,0,2:T(4,128)}, u32[]{:S(2)}) copy-start(f32[4,256,3]{1,0,2:T(4,128)} %param.26) | copy-start | bytes 36868
  7.6 11.3 %collective-permute-start.1 = (f32[48,8,128]{2,1,0:T(8,128)S(1)}, f32[48,8,128]{2,1,0:T(8,128)S(1)}, u32[]{:S(2)}, u32[]{:S(2)}) collective-permute-start(f32[48,8,128]{2,1,0:T(8,128)S(1)} %get-tuple-element.53), channel_id=1, source_target_pairs={{8,0},{16,8},{24,16},{32,24},{40,32},{48,40},{56,48},{64,56},{72,6... | collective-permute-start | bytes 589832 | tf_op jit(solution)/shard_map/ppermute | solution.py:121
  10.0 13.5 %collective-permute-start = (f32[50,8,128]{2,1,0:T(8,128)S(1)}, f32[50,8,128]{2,1,0:T(8,128)S(1)}, u32[]{:S(2)}, u32[]{:S(2)}) collective-permute-start(f32[50,8,128]{2,1,0:T(8,128)S(1)} %get-tuple-element.52), channel_id=1, source_target_pairs={{0,8},{8,16},{16,24},{24,32},{32,40},{40,48},{48,56},{56,64},{64,7... | collective-permute-start | bytes 614408 | tf_op jit(solution)/shard_map/ppermute | solution.py:120
  23.7 12.3 %collective-permute-start.2 = (f32[33,8,2,128]{3,2,1,0:T(2,128)S(1)}, f32[33,8,2,128]{3,2,1,0:T(2,128)S(1)}, u32[]{:S(2)}, u32[]{:S(2)}) collective-permute-start(f32[33,8,2,128]{3,2,1,0:T(2,128)S(1)} %get-tuple-element.21), channel_id=1, source_target_pairs={{0,1},{1,2},{2,3},{3,4},{4,5},{5,6},{6,7},{8,9},{9,10},{10,11},{11... | collective-permute-start | bytes 811016 | tf_op jit(solution)/shard_map/ppermute | solution.py:20
  32.6 7.8 %collective-permute-start.3 = (f32[33,8,2,128]{3,2,1,0:T(2,128)S(1)}, f32[33,8,2,128]{3,2,1,0:T(2,128)S(1)}, u32[]{:S(2)}, u32[]{:S(2)}) collective-permute-start(f32[33,8,2,128]{3,2,1,0:T(2,128)S(1)} %get-tuple-element.22), channel_id=1, source_target_pairs={{1,0},{2,1},{3,2},{4,3},{5,4},{6,5},{7,6},{9,8},{10,9},{11,10},{12... | collective-permute-start | bytes 811016 | tf_op jit(solution)/shard_map/ppermute | solution.py:22
  45.8 0.7 %copy-start.6 = (f32[6]{0:T(128)S(1)}, f32[6]{0:T(128)}, u32[]{:S(2)}) copy-start(f32[6]{0:T(128)} %constant.98.clone) | copy-start | bytes 76
  48.1 8.3 %all-to-all-start = ((f32[4,1,2048]{2,1,0:T(1,128)}), f32[4,1,2048]{2,1,0:T(1,128)S(1)}, u32[]{:S(2)}, u32[]{:S(2)}) async-start(f32[4,1,2048]{2,1,0:T(1,128)} %reshape.519), calls=%async_computation | async-start | bytes 65536 | tf_op jit(solution)/shard_map/all_to_all | solution.py:293

commit v8 on v6

--- a/solution.py
+++ b/solution.py
@@ -190,6 +190,43 @@
     force = jnp.stack([force_x, force_y, force_z], axis=1)
     strain = jnp.stack([strain_xx, strain_yy, strain_zz, strain_xy, strain_xz, strain_yz], axis=1)
     return (force, strain)
+
+
+def exchange_y(grown, pairs_lo, pairs_hi, span_y):
+    channels, cells_x, cells_y, depth = grown.shape
+    count = lax.axis_size("gy")
+    wide_lo = grown[:pairs_lo, :, cells_y - 2 :].reshape((-1, depth))
+    thin_lo = grown[pairs_lo:, :, cells_y - 1 :].reshape((-1, depth))
+    wide_hi = grown[:pairs_hi, :, :2].reshape((-1, depth))
+    thin_hi = grown[pairs_hi:, :, :1].reshape((-1, depth))
+    from_lo = lax.ppermute(
+        jnp.concatenate([wide_lo, thin_lo]), "gy", [(i, i + 1) for i in range(count - 1)]
+    )
+    from_hi = lax.ppermute(
+        jnp.concatenate([wide_hi, thin_hi]), "gy", [(i + 1, i) for i in range(count - 1)]
+    )
+    split_lo = pairs_lo * cells_x * 2
+    blank = jnp.zeros((channels - pairs_lo, cells_x, 1, depth), jnp.float32)
+    cols_lo = jnp.concatenate(
+        [
+            from_lo[:split_lo].reshape((pairs_lo, cells_x, 2, depth)),
+            jnp.concatenate(
+                [blank, from_lo[split_lo:].reshape((-1, cells_x, 1, depth))], axis=2
+            ),
+        ]
+    )
+    split_hi = pairs_hi * cells_x * 2
+    blank = jnp.zeros((channels - pairs_hi, cells_x, 1, depth), jnp.float32)
+    cols_hi = jnp.concatenate(
+        [
+            from_hi[:split_hi].reshape((pairs_hi, cells_x, 2, depth)),
+            jnp.concatenate(
+                [from_hi[split_hi:].reshape((-1, cells_x, 1, depth)), blank], axis=2
+            ),
+        ]
+    )
+    tail = jnp.zeros((channels, cells_x, span_y - cells_y - 4, depth), jnp.float32)
+    return jnp.concatenate([cols_lo, grown, cols_hi, tail], axis=2)
 
 
 def local(
@@ -220,9 +257,8 @@
     prev = jnp.concatenate([fwd_prev[None], adj_prev]).reshape((fields * 3,) + grid)
     comps = fields * 3
     stacked = jnp.concatenate([now, lame_first[None], shear_mod[None], prev, buoyancy[None]])
-    grown = with_halo(exchange_x(stacked, comps + 2, comps), (("gy", 2),), 2)
     span_y = 16 * ((cells_y + 4 + 15) // 16)
-    grown = jnp.pad(grown, ((0, 0), (0, 0), (0, span_y - cells_y - 4), (0, 0)))
+    grown = exchange_y(exchange_x(stacked, comps + 2, comps), comps + 2, comps, span_y)
     now_grown = grown[:comps].reshape((fields, 3) + grown.shape[1:])
     lame_grown = grown[comps]
     shear_grown = grown[comps + 1]

time: 55.1 us -> 55 us (level)
  the two profiles are of different devices: /device:TPU:321 before, /device:TPU:384 now
where the time goes in v8:
time: 55 us; the launch traced here: 54.6 us
  waiting for transfers between devices  21.5 us (39%)
  starting transfers between devices  14.5 us (26%)
  other arithmetic  9.14 us (17%)
  local copies, waits for them, and re-layouts  6.58 us (12%)
  between operations  2.91 us (5%)
    ppermute x1, waiting for transfers between devices, exchange_x(): lax.ppermute(jnp.concatenate([wide_lo, thin_lo]), 'gx', [(i, i + 1) for i...  11.8 us
    all_to_all x1, waiting for transfers between devices, local(): gathered = lax.all_to_all(totals, 'grp', 3, 0, tiled=True)  4.39 us
    all_to_all x1, starting transfers between devices, local(): gathered = lax.all_to_all(totals, 'grp', 3, 0, tiled=True)  4.29 us
    ppermute x1, waiting for transfers between devices, exchange_y(): lax.ppermute(jnp.concatenate([wide_lo, thin_lo]), 'gy', [(i, i + 1) for i...  3.99 us
    ppermute x1, starting transfers between devices, exchange_x(): lax.ppermute(jnp.concatenate([wide_hi, thin_hi]), 'gx', [(i + 1, i) for i...  3.54 us
    unnamed x34, local copies, waits for them, and re-layouts  3.12 us
    ppermute x1, starting transfers between devices, exchange_y(): lax.ppermute(jnp.concatenate([wide_lo, thin_lo]), 'gy', [(i, i + 1) for i...  2.41 us
    ppermute x1, starting transfers between devices, exchange_x(): lax.ppermute(jnp.concatenate([wide_lo, thin_lo]), 'gx', [(i, i + 1) for i...  2.31 us
  transfers between devices with their start and end apart: 5, of which 5 were waited for; matrix products, arithmetic and copies ran while one was open for 5% of the time, Pallas kernels for 0%

profile of v8, /device:TPU:384, one launch (start us, length us, event | category | flops | bytes accessed | tf_op | source)
XLA Modules:
  0.0 54.6 jit_solution(3235935731451480081)
XLA Ops:
  0.7 1.0 %pad_maximum_fusion.8 = f32[5,3,4,8,128]{4,3,2,1,0:T(8,128)S(1)} fusion(f32[4,3,4,8,128]{4,3,2,1,0:T(8,128)} %param.16, f32[1,3,4,8,128]{4,3,2,1,0:T(8,128)} %bitcast.298), kind=kLoop, calls=%fused_computation.83 | loop fusion | flops 61440 | bytes 491520 | tf_op jit(solution)/shard_map/concatenate | solution.py:256
  1.7 0.9 %pad_maximum_fusion.9 = f32[5,3,4,8,128]{4,3,2,1,0:T(8,128)S(1)} fusion(f32[4,3,4,8,128]{4,3,2,1,0:T(8,128)} %param.17, f32[1,3,4,8,128]{4,3,2,1,0:T(8,128)} %bitcast.299), kind=kLoop, calls=%fused_computation.84 | loop fusion | flops 61440 | bytes 491520 | tf_op jit(solution)/shard_map/concatenate | solution.py:257
  2.8 3.5 %collective-permute-start.1 = (f32[48,8,128]{2,1,0:T(8,128)S(1)}, f32[48,8,128]{2,1,0:T(8,128)S(1)}, u32[]{:S(2)}, u32[]{:S(2)}) collective-permute-start(f32[48,8,128]{2,1,0:T(8,128)S(1)} %pad_maximum_fusion.14), channel_id=1, source_target_pairs={{8,0},{16,8},{24,16},{32,24},{40,32},{48,40},{56,48},{64,56},{72,6... | collective-permute-start | bytes 589832 | tf_op jit(solution)/shard_map/ppermute | solution.py:127
  6.4 2.3 %collective-permute-start = (f32[50,8,128]{2,1,0:T(8,128)S(1)}, f32[50,8,128]{2,1,0:T(8,128)S(1)}, u32[]{:S(2)}, u32[]{:S(2)}) collective-permute-start(f32[50,8,128]{2,1,0:T(8,128)S(1)} %pad_maximum_fusion.10), channel_id=1, source_target_pairs={{0,8},{8,16},{16,24},{24,32},{32,40},{40,48},{48,56},{56,64},{64,7... | collective-permute-start | bytes 614408 | tf_op jit(solution)/shard_map/ppermute | solution.py:124
  11.4 0.8 %collective-permute-done.1 = f32[48,8,128]{2,1,0:T(8,128)S(1)} collective-permute-done((f32[48,8,128]{2,1,0:T(8,128)S(1)}, f32[48,8,128]{2,1,0:T(8,128)S(1)}, u32[]{:S(2)}, u32[]{:S(2)}) %collective-permute-start.1) | collective-permute-done | bytes 196640 | tf_op jit(solution)/shard_map/ppermute | solution.py:127
  12.2 11.8 %collective-permute-done = f32[50,8,128]{2,1,0:T(8,128)S(1)} collective-permute-done((f32[50,8,128]{2,1,0:T(8,128)S(1)}, f32[50,8,128]{2,1,0:T(8,128)S(1)}, u32[]{:S(2)}, u32[]{:S(2)}) %collective-permute-start) | collective-permute-done | bytes 204832 | tf_op jit(solution)/shard_map/ppermute | solution.py:124
  24.3 1.9 %collective-permute-start.3 = (f32[384,128]{1,0:T(8,128)S(1)}, f32[384,128]{1,0:T(8,128)S(1)}, u32[]{:S(2)}, u32[]{:S(2)}) collective-permute-start(f32[384,128]{1,0:T(8,128)S(1)} %pad_maximum_fusion.15), channel_id=1, source_target_pairs={{1,0},{2,1},{3,2},{4,3},{5,4},{6,5},{7,6},{9,8},{10,9},{11,10},{12... | collective-permute-start | bytes 589832 | tf_op jit(solution)/shard_map/ppermute | solution.py:205
  26.4 2.4 %collective-permute-start.2 = (f32[400,128]{1,0:T(8,128)S(1)}, f32[400,128]{1,0:T(8,128)S(1)}, u32[]{:S(2)}, u32[]{:S(2)}) collective-permute-start(f32[400,128]{1,0:T(8,128)S(1)} %pad_maximum_fusion.11), channel_id=1, source_target_pairs={{0,1},{1,2},{2,3},{3,4},{4,5},{5,6},{6,7},{8,9},{9,10},{10,11},{11... | collective-permute-start | bytes 614408 | tf_op jit(solution)/shard_map/ppermute | solution.py:202
  28.8 0.6 %collective-permute-done.3 = f32[384,128]{1,0:T(8,128)S(1)} collective-permute-done((f32[384,128]{1,0:T(8,128)S(1)}, f32[384,128]{1,0:T(8,128)S(1)}, u32[]{:S(2)}, u32[]{:S(2)}) %collective-permute-start.3) | collective-permute-done | bytes 196640 | tf_op jit(solution)/shard_map/ppermute | solution.py:205
  29.5 4.0 %collective-permute-done.2 = f32[400,128]{1,0:T(8,128)S(1)} collective-permute-done((f32[400,128]{1,0:T(8,128)S(1)}, f32[400,128]{1,0:T(8,128)S(1)}, u32[]{:S(2)}, u32[]{:S(2)}) %collective-permute-start.2) | collective-permute-done | bytes 204832 | tf_op jit(solution)/shard_map/ppermute | solution.py:202
  33.6 1.3 %fusion.1 = f32[33,8,16,128]{3,2,0,1:T(8,128)S(1)} fusion(f32[18,8,1,128]{3,2,0,1:T(1,128)S(1)} %copy.234, f32[16,8,1,128]{3,2,0,1:T(1,128)S(1)} %copy.230, f32[18,2,8,128]{3,2,0,1:T(8,128)S(1)} %concatenate.180, f32[33,4,8,128]{3,2,0,1:T(8,128)S(1)} %constant_dynamic-update-slice_fusion, f32[16,2,8,128]{3,2,0,1:T(8,128)S(1)} %concatenate.175, ...), kind=kLoop, calls=%fused_computation.4 | loop fusion | flops 11354112 | bytes 3645504 | tf_op jit(solution)/shard_map/concatenate | solution.py:229
  35.2 0.3 slice.667
  35.8 0.3 pad_maximum_fusion
  36.2 0.3 copy_subtract_fusion
  36.5 0.3 fusion.15
  37.3 0.2 fusion.17
  37.5 0.3 fusion.29
  37.8 0.3 fusion.8
  38.3 0.2 slice.711
  38.6 0.2 maximum_subtract_fusion
  40.2 0.4 copy-done.5
  40.7 0.3 copy.272
  41.0 1.2 %reshape.551 = f32[4,1,2048]{2,1,0:T(1,128)} reshape(f32[128,2,4,8]{3,2,1,0:T(4,128)S(1)} %bitcast.279) | data formatting | bytes 65536
  42.1 4.3 %all-to-all-start = ((f32[4,1,2048]{2,1,0:T(1,128)}), f32[4,1,2048]{2,1,0:T(1,128)S(1)}, u32[]{:S(2)}, u32[]{:S(2)}) async-start(f32[4,1,2048]{2,1,0:T(1,128)} %reshape.551), calls=%async_computation | async-start | bytes 65536 | tf_op jit(solution)/shard_map/all_to_all | solution.py:316
  46.5 0.2 fusion.52
  46.7 0.8 %fusion.32 = f32[4,3,4,8,128]{4,3,2,1,0:T(8,128)} fusion(f32[4,3,4,16,128]{4,3,2,1,0:T(8,128)S(1)} %slice.702, f32[4,1,4,16,128]{4,3,2,1,0:T(8,128)S(1)} %fusion.40, f32[4,1,4,16,128]{4,3,2,1,0:T(8,128)S(1)} %get-tuple-element.41, f32[4,1,4,16,128]{4,3,2,1,0:T(8,128)S(1)} %get-tuple-element.40, f32[4,8,128]{2,1,0:T(8,128)S(1)} %slice.749, ...), kind=kLoop, calls=%fused_computation.89 | loop fusion | flops 344064 | bytes 1067008 | tf_op jit(solution)/shard_map/add | solution.py:113
  47.5 4.4 %all-to-all-done = f32[4,1,2048]{2,1,0:T(1,128)S(1)} async-done(((f32[4,1,2048]{2,1,0:T(1,128)}), f32[4,1,2048]{2,1,0:T(1,128)S(1)}, u32[]{:S(2)}, u32[]{:S(2)}) %all-to-all-start) | async-done | bytes 32800 | tf_op jit(solution)/shard_map/all_to_all | solution.py:316
  51.9 0.5 broadcast.418
  52.4 0.7 %reduce.4 = f32[4,2048]{1,0:T(4,128)S(1)} reduce(f32[4,1,2048]{2,1,0:T(1,128)S(1)} %all-to-all-done, f32[]{:T(128)} %broadcast.418), dimensions={1}, to_apply=%all_to_all.4.reduce_sub_computation | reduce | bytes 65540 | tf_op jit(solution)/shard_map/all_to_all | solution.py:316
  53.1 0.6 %reshape.552 = f32[128,2,4,8]{3,2,1,0:T(4,128)S(1)} reshape(f32[4,2048]{1,0:T(4,128)S(1)} %reduce.4) | data formatting | bytes 65536
  53.8 0.1 reduce_sum.82
  53.9 0.7 %copy.273 = f32[2,4,8,32]{3,2,1,0:T(8,128)} copy(f32[2,4,8,32]{2,1,0,3:T(4,128)S(1)} %reduce_sum.82) | data formatting | bytes 16384
  (137 shorter events, 4.6 us)
Async XLA Ops:
  0.6 2.1 %copy-start.2 = (f32[4,8,128]{2,1,0:T(8,128)S(1)}, f32[4,8,128]{2,1,0:T(8,128)}, u32[]{:S(2)}) copy-start(f32[4,8,128]{2,1,0:T(8,128)} %param.20) | copy-start | bytes 49156
  0.6 2.1 %copy-start.1 = (f32[4,8,128]{2,1,0:T(8,128)S(1)}, f32[4,8,128]{2,1,0:T(8,128)}, u32[]{:S(2)}) copy-start(f32[4,8,128]{2,1,0:T(8,128)} %param.19) | copy-start | bytes 49156
  0.7 2.1 %copy-start = (f32[4,8,128]{2,1,0:T(8,128)S(1)}, f32[4,8,128]{2,1,0:T(8,128)}, u32[]{:S(2)}) copy-start(f32[4,8,128]{2,1,0:T(8,128)} %param.18) | copy-start | bytes 49156
  1.7 8.4 %copy-start.6 = (s32[4]{0:T(128)S(1)}, s32[4]{0:T(128)}, u32[]{:S(2)}) copy-start(s32[4]{0:T(128)} %param.24) | copy-start | bytes 52
  1.7 8.6 %copy-start.7 = (s32[4]{0:T(128)S(1)}, s32[4]{0:T(128)}, u32[]{:S(2)}) copy-start(s32[4]{0:T(128)} %param.25) | copy-start | bytes 52
  1.7 8.7 %copy-start.4 = (f32[256,3]{0,1:T(4,128)S(1)}, f32[256,3]{0,1:T(4,128)}, u32[]{:S(2)}) copy-start(f32[256,3]{0,1:T(4,128)} %param.23) | copy-start | bytes 9220
  1.7 9.0 %copy-start.3 = (f32[4,256,3]{1,0,2:T(4,128)S(1)}, f32[4,256,3]{1,0,2:T(4,128)}, u32[]{:S(2)}) copy-start(f32[4,256,3]{1,0,2:T(4,128)} %param.26) | copy-start | bytes 36868
  2.8 9.3 %collective-permute-start.1 = (f32[48,8,128]{2,1,0:T(8,128)S(1)}, f32[48,8,128]{2,1,0:T(8,128)S(1)}, u32[]{:S(2)}, u32[]{:S(2)}) collective-permute-start(f32[48,8,128]{2,1,0:T(8,128)S(1)} %pad_maximum_fusion.14), channel_id=1, source_target_pairs={{8,0},{16,8},{24,16},{32,24},{40,32},{48,40},{56,48},{64,56},{72,6... | collective-permute-start | bytes 589832 | tf_op jit(solution)/shard_map/ppermute | solution.py:127
  6.4 17.6 %collective-permute-start = (f32[50,8,128]{2,1,0:T(8,128)S(1)}, f32[50,8,128]{2,1,0:T(8,128)S(1)}, u32[]{:S(2)}, u32[]{:S(2)}) collective-permute-start(f32[50,8,128]{2,1,0:T(8,128)S(1)} %pad_maximum_fusion.10), channel_id=1, source_target_pairs={{0,8},{8,16},{16,24},{24,32},{32,40},{40,48},{48,56},{56,64},{64,7... | collective-permute-start | bytes 614408 | tf_op jit(solution)/shard_map/ppermute | solution.py:124
  24.3 5.1 %collective-permute-start.3 = (f32[384,128]{1,0:T(8,128)S(1)}, f32[384,128]{1,0:T(8,128)S(1)}, u32[]{:S(2)}, u32[]{:S(2)}) collective-permute-start(f32[384,128]{1,0:T(8,128)S(1)} %pad_maximum_fusion.15), channel_id=1, source_target_pairs={{1,0},{2,1},{3,2},{4,3},{5,4},{6,5},{7,6},{9,8},{10,9},{11,10},{12... | collective-permute-start | bytes 589832 | tf_op jit(solution)/shard_map/ppermute | solution.py:205
  26.4 7.1 %collective-permute-start.2 = (f32[400,128]{1,0:T(8,128)S(1)}, f32[400,128]{1,0:T(8,128)S(1)}, u32[]{:S(2)}, u32[]{:S(2)}) collective-permute-start(f32[400,128]{1,0:T(8,128)S(1)} %pad_maximum_fusion.11), channel_id=1, source_target_pairs={{0,1},{1,2},{2,3},{3,4},{4,5},{5,6},{6,7},{8,9},{9,10},{10,11},{11... | collective-permute-start | bytes 614408 | tf_op jit(solution)/shard_map/ppermute | solution.py:202
  39.9 0.7 %copy-start.5 = (f32[6]{0:T(128)S(1)}, f32[6]{0:T(128)}, u32[]{:S(2)}) copy-start(f32[6]{0:T(128)} %constant.99.clone) | copy-start | bytes 76
  42.1 9.7 %all-to-all-start = ((f32[4,1,2048]{2,1,0:T(1,128)}), f32[4,1,2048]{2,1,0:T(1,128)S(1)}, u32[]{:S(2)}, u32[]{:S(2)}) async-start(f32[4,1,2048]{2,1,0:T(1,128)} %reshape.551), calls=%async_computation | async-start | bytes 65536 | tf_op jit(solution)/shard_map/all_to_all | solution.py:316

commit v9 on v6

--- a/solution.py
+++ b/solution.py
@@ -144,20 +144,30 @@
     return jnp.concatenate([rows_lo, stacked, rows_hi], axis=1)
 
 
+def ahead(cells, axis):
+    widths = [(0, 0)] * cells.ndim
+    widths[axis] = (0, 1)
+    return jnp.pad(lax.slice_in_dim(cells, 1, cells.shape[axis], axis=axis), widths)
+
+
+def behind(cells, axis):
+    widths = [(0, 0)] * cells.ndim
+    widths[axis] = (1, 0)
+    return jnp.pad(lax.slice_in_dim(cells, 0, cells.shape[axis] - 1, axis=axis), widths)
+
+
 def up_z(cells):
-    top = lax.broadcasted_iota(jnp.int32, cells.shape, cells.ndim - 1) == cells.shape[-1] - 1
-    return jnp.where(top, 0.0, jnp.roll(cells, -1, axis=-1))
+    return ahead(cells, cells.ndim - 1)
 
 
 def down_z(cells):
-    bottom = lax.broadcasted_iota(jnp.int32, cells.shape, cells.ndim - 1) == 0
-    return jnp.where(bottom, 0.0, jnp.roll(cells, 1, axis=-1))
+    return behind(cells, cells.ndim - 1)
 
 
 def dense_stencil(cells, lame, shear):
     lower = cells[:, :, :-1]
     grad_x = cells[:, :, 1:] - lower
-    grad_y = jnp.roll(lower, -1, axis=3) - lower
+    grad_y = ahead(lower, 3) - lower
     grad_z = up_z(lower) - lower
     strain_xx = grad_x[:, 0]
     strain_yy = grad_y[:, 1]
@@ -179,7 +189,7 @@
         return stress[:, 1:] - stress[:, :-1]
 
     def diff_y(stress):
-        return (stress - jnp.roll(stress, 1, axis=2))[:, 1:]
+        return (stress - behind(stress, 2))[:, 1:]
 
     def diff_z(stress):
         return (stress - down_z(stress))[:, 1:]

time: 55.1 us -> 53.1 us (0.964)
  local copies, waits for them, and re-layouts: 6.23 us -> 4.93 us
  other arithmetic: 8.36 us -> 7.76 us
    slice x22 -> x3, local copies, waits for them, and re-layouts: 1.62 us -> 0.32 us  [ahead(): lax.slice_in_dim(cells, 1, cells.shape[axis], axis=axis)]
    unnamed x34 -> x33, local copies, waits for them, and re-layouts: 3.11 us -> 3.11 us
where the time goes in v9:
time: 53.1 us; the launch traced here: 52.8 us
  starting transfers between devices  20.2 us (38%)
  waiting for transfers between devices  17.2 us (32%)
  other arithmetic  7.76 us (15%)
  local copies, waits for them, and re-layouts  4.93 us (9%)
  between operations  2.62 us (5%)
    ppermute x1, starting transfers between devices, with_halo(): lax.ppermute(tail, axis, [(i, i + 1) for i in range(ends)])  9.03 us
    ppermute x1, waiting for transfers between devices, exchange_x(): lax.ppermute(jnp.concatenate([wide_lo, thin_lo]), 'gx', [(i, i + 1) for i...  8.27 us
    ppermute x1, waiting for transfers between devices, with_halo(): lax.ppermute(head, axis, [(i + 1, i) for i in range(ends)])  4.4 us
    all_to_all x1, starting transfers between devices, local(): gathered = lax.all_to_all(totals, 'grp', 3, 0, tiled=True)  4.01 us
    all_to_all x1, waiting for transfers between devices, local(): gathered = lax.all_to_all(totals, 'grp', 3, 0, tiled=True)  3.32 us
    unnamed x33, local copies, waits for them, and re-layouts  3.11 us
    ppermute x1, starting transfers between devices, exchange_x(): lax.ppermute(jnp.concatenate([wide_lo, thin_lo]), 'gx', [(i, i + 1) for i...  2.92 us
    ppermute x1, starting transfers between devices, exchange_x(): lax.ppermute(jnp.concatenate([wide_hi, thin_hi]), 'gx', [(i + 1, i) for i...  2.36 us
  transfers between devices with their start and end apart: 5, of which 4 were waited for; matrix products, arithmetic and copies ran while one was open for 4% of the time, Pallas kernels for 0%

profile of v9, /device:TPU:321, one launch (start us, length us, event | category | flops | bytes accessed | tf_op | source)
XLA Modules:
  0.0 52.8 jit_solution(6813790610355456608)
XLA Ops:
  0.7 1.0 %pad_maximum_fusion.3 = f32[5,3,4,8,128]{4,3,2,1,0:T(8,128)S(1)} fusion(f32[4,3,4,8,128]{4,3,2,1,0:T(8,128)} %param.16, f32[1,3,4,8,128]{4,3,2,1,0:T(8,128)} %bitcast.267), kind=kLoop, calls=%fused_computation.74 | loop fusion | flops 61440 | bytes 491520 | tf_op jit(solution)/shard_map/concatenate | solution.py:229
  1.7 0.9 %pad_maximum_fusion.4 = f32[5,3,4,8,128]{4,3,2,1,0:T(8,128)S(1)} fusion(f32[4,3,4,8,128]{4,3,2,1,0:T(8,128)} %param.17, f32[1,3,4,8,128]{4,3,2,1,0:T(8,128)} %bitcast.268), kind=kLoop, calls=%fused_computation.75 | loop fusion | flops 61440 | bytes 491520 | tf_op jit(solution)/shard_map/concatenate | solution.py:230
  2.8 2.4 %collective-permute-start.1 = (f32[48,8,128]{2,1,0:T(8,128)S(1)}, f32[48,8,128]{2,1,0:T(8,128)S(1)}, u32[]{:S(2)}, u32[]{:S(2)}) collective-permute-start(f32[48,8,128]{2,1,0:T(8,128)S(1)} %pad_maximum_fusion.8), channel_id=1, source_target_pairs={{8,0},{16,8},{24,16},{32,24},{40,32},{48,40},{56,48},{64,56},{72,6... | collective-permute-start | bytes 589832 | tf_op jit(solution)/shard_map/ppermute | solution.py:127
  5.2 2.9 %collective-permute-start = (f32[50,8,128]{2,1,0:T(8,128)S(1)}, f32[50,8,128]{2,1,0:T(8,128)S(1)}, u32[]{:S(2)}, u32[]{:S(2)}) collective-permute-start(f32[50,8,128]{2,1,0:T(8,128)S(1)} %pad_maximum_fusion.5), channel_id=1, source_target_pairs={{0,8},{8,16},{16,24},{24,32},{32,40},{40,48},{48,56},{56,64},{64,7... | collective-permute-start | bytes 614408 | tf_op jit(solution)/shard_map/ppermute | solution.py:124
  10.5 8.3 %collective-permute-done = f32[50,8,128]{2,1,0:T(8,128)S(1)} collective-permute-done((f32[50,8,128]{2,1,0:T(8,128)S(1)}, f32[50,8,128]{2,1,0:T(8,128)S(1)}, u32[]{:S(2)}, u32[]{:S(2)}) %collective-permute-start) | collective-permute-done | bytes 204832 | tf_op jit(solution)/shard_map/ppermute | solution.py:124
  18.8 0.2 maximum_maximum_fusion
  19.0 9.0 %collective-permute-start.2 = (f32[33,8,2,128]{3,2,0,1:T(2,128)S(1)}, f32[33,8,2,128]{3,2,0,1:T(2,128)S(1)}, u32[]{:S(2)}, u32[]{:S(2)}) collective-permute-start(f32[33,8,2,128]{3,2,0,1:T(2,128)S(1)} %get-tuple-element.21), channel_id=1, source_target_pairs={{0,1},{1,2},{2,3},{3,4},{4,5},{5,6},{6,7},{8,9},{9,10},{10,11},{11... | collective-permute-start | bytes 811016 | tf_op jit(solution)/shard_map/ppermute | solution.py:20
  28.0 1.9 %collective-permute-start.3 = (f32[33,8,2,128]{3,2,0,1:T(2,128)S(1)}, f32[33,8,2,128]{3,2,0,1:T(2,128)S(1)}, u32[]{:S(2)}, u32[]{:S(2)}) collective-permute-start(f32[33,8,2,128]{3,2,0,1:T(2,128)S(1)} %get-tuple-element.22), channel_id=1, source_target_pairs={{1,0},{2,1},{3,2},{4,3},{5,4},{6,5},{7,6},{9,8},{10,9},{11,10},{12... | collective-permute-start | bytes 811016 | tf_op jit(solution)/shard_map/ppermute | solution.py:22
  29.9 0.1 and_convert_fusion
  30.2 1.2 %collective-permute-done.2 = f32[33,8,2,128]{3,2,0,1:T(2,128)S(1)} collective-permute-done((f32[33,8,2,128]{3,2,0,1:T(2,128)S(1)}, f32[33,8,2,128]{3,2,0,1:T(2,128)S(1)}, u32[]{:S(2)}, u32[]{:S(2)}) %collective-permute-start.2) | collective-permute-done | bytes 270368 | tf_op jit(solution)/shard_map/ppermute | solution.py:20
  31.4 4.4 %collective-permute-done.3 = f32[33,8,2,128]{3,2,0,1:T(2,128)S(1)} collective-permute-done((f32[33,8,2,128]{3,2,0,1:T(2,128)S(1)}, f32[33,8,2,128]{3,2,0,1:T(2,128)S(1)}, u32[]{:S(2)}, u32[]{:S(2)}) %collective-permute-start.3) | collective-permute-done | bytes 270368 | tf_op jit(solution)/shard_map/ppermute | solution.py:22
  35.8 0.6 %select_maximum_fusion = f32[33,8,16,128]{3,2,0,1:T(8,128)S(1)} fusion(f32[33,8,2,128]{3,2,0,1:T(2,128)S(1)} %collective-permute-done.3, f32[33,8,2,128]{3,2,0,1:T(2,128)S(1)} %collective-permute-done.2, f32[18,2,8,128]{3,2,0,1:T(8,128)S(1)} %concatenate.90, f32[33,4,8,128]{3,2,0,1:T(8,128)S(1)} %constant_dynamic-update-slice_fusion, ...), kind=kLoop, calls=%fused_computation | loop fusion | flops 7569408 | bytes 3784704 | tf_op jit(solution)/shard_map/concatenate | solution.py:18
  36.5 0.2 fusion.72
  36.7 0.1 fusion.73
  36.9 0.4 pad_subtract_fusion.1
  37.3 0.3 fusion.16
  37.7 0.4 fusion.25
  38.0 0.3 fusion.10
  38.5 0.2 slice.576
  38.9 0.1 pad_subtract_fusion.3
  39.8 0.4 copy-done.5
  40.3 0.3 copy.194
  40.5 1.2 %reshape.491 = f32[4,1,2048]{2,1,0:T(1,128)} reshape(f32[128,2,4,8]{3,2,1,0:T(4,128)S(1)} %bitcast.249) | data formatting | bytes 65536
  41.7 4.0 %all-to-all-start = ((f32[4,1,2048]{2,1,0:T(1,128)}), f32[4,1,2048]{2,1,0:T(1,128)S(1)}, u32[]{:S(2)}, u32[]{:S(2)}) async-start(f32[4,1,2048]{2,1,0:T(1,128)} %reshape.491), calls=%async_computation | async-start | bytes 65536 | tf_op jit(solution)/shard_map/all_to_all | solution.py:290
  45.7 0.2 fusion.41
  45.9 0.8 %fusion.27 = f32[4,3,4,8,128]{4,3,2,1,0:T(8,128)} fusion(f32[4,3,4,16,128]{4,3,2,1,0:T(8,128)S(1)} %slice.568, f32[4,1,4,16,128]{4,3,2,1,0:T(8,128)S(1)} %get-tuple-element.45, f32[4,1,4,16,128]{4,3,2,1,0:T(8,128)S(1)} %get-tuple-element.44, f32[4,1,4,16,128]{4,3,2,1,0:T(8,128)S(1)} %get-tuple-element.43, f32[4,8,128]{2,1,0:T(8,128)S(1)} %slice.607, ...), kind=kLoop, calls=%fused_computation.79 | loop fusion | flops 344064 | bytes 1067008 | tf_op jit(solution)/shard_map/add | solution.py:113
  46.7 3.3 %all-to-all-done = f32[4,1,2048]{2,1,0:T(1,128)S(1)} async-done(((f32[4,1,2048]{2,1,0:T(1,128)}), f32[4,1,2048]{2,1,0:T(1,128)S(1)}, u32[]{:S(2)}, u32[]{:S(2)}) %all-to-all-start) | async-done | bytes 32800 | tf_op jit(solution)/shard_map/all_to_all | solution.py:290
  50.0 0.5 broadcast.419
  50.5 0.7 %reduce.4 = f32[4,2048]{1,0:T(4,128)S(1)} reduce(f32[4,1,2048]{2,1,0:T(1,128)S(1)} %all-to-all-done, f32[]{:T(128)} %broadcast.419), dimensions={1}, to_apply=%all_to_all.4.reduce_sub_computation | reduce | bytes 65540 | tf_op jit(solution)/shard_map/all_to_all | solution.py:290
  51.3 0.6 %reshape.492 = f32[128,2,4,8]{3,2,1,0:T(4,128)S(1)} reshape(f32[4,2048]{1,0:T(4,128)S(1)} %reduce.4) | data formatting | bytes 65536
  51.9 0.1 reduce_sum.82
  52.1 0.7 %copy.195 = f32[2,4,8,32]{3,2,1,0:T(8,128)} copy(f32[2,4,8,32]{2,1,0,3:T(4,128)S(1)} %reduce_sum.82) | data formatting | bytes 16384
  (95 shorter events, 2.4 us)
Async XLA Ops:
  0.6 2.1 %copy-start.2 = (f32[4,8,128]{2,1,0:T(8,128)S(1)}, f32[4,8,128]{2,1,0:T(8,128)}, u32[]{:S(2)}) copy-start(f32[4,8,128]{2,1,0:T(8,128)} %param.20) | copy-start | bytes 49156
  0.6 2.1 %copy-start.1 = (f32[4,8,128]{2,1,0:T(8,128)S(1)}, f32[4,8,128]{2,1,0:T(8,128)}, u32[]{:S(2)}) copy-start(f32[4,8,128]{2,1,0:T(8,128)} %param.19) | copy-start | bytes 49156
  0.7 2.1 %copy-start = (f32[4,8,128]{2,1,0:T(8,128)S(1)}, f32[4,8,128]{2,1,0:T(8,128)}, u32[]{:S(2)}) copy-start(f32[4,8,128]{2,1,0:T(8,128)} %param.18) | copy-start | bytes 49156
  1.7 7.9 %copy-start.6 = (s32[4]{0:T(128)S(1)}, s32[4]{0:T(128)}, u32[]{:S(2)}) copy-start(s32[4]{0:T(128)} %param.24) | copy-start | bytes 52
  1.7 8.0 %copy-start.7 = (s32[4]{0:T(128)S(1)}, s32[4]{0:T(128)}, u32[]{:S(2)}) copy-start(s32[4]{0:T(128)} %param.25) | copy-start | bytes 52
  1.7 8.1 %copy-start.4 = (f32[256,3]{0,1:T(4,128)S(1)}, f32[256,3]{0,1:T(4,128)}, u32[]{:S(2)}) copy-start(f32[256,3]{0,1:T(4,128)} %param.23) | copy-start | bytes 9220
  1.7 8.4 %copy-start.3 = (f32[4,256,3]{1,0,2:T(4,128)S(1)}, f32[4,256,3]{1,0,2:T(4,128)}, u32[]{:S(2)}) copy-start(f32[4,256,3]{1,0,2:T(4,128)} %param.26) | copy-start | bytes 36868
  2.8 7.7 %collective-permute-start.1 = (f32[48,8,128]{2,1,0:T(8,128)S(1)}, f32[48,8,128]{2,1,0:T(8,128)S(1)}, u32[]{:S(2)}, u32[]{:S(2)}) collective-permute-start(f32[48,8,128]{2,1,0:T(8,128)S(1)} %pad_maximum_fusion.8), channel_id=1, source_target_pairs={{8,0},{16,8},{24,16},{32,24},{40,32},{48,40},{56,48},{64,56},{72,6... | collective-permute-start | bytes 589832 | tf_op jit(solution)/shard_map/ppermute | solution.py:127
  5.2 13.5 %collective-permute-start = (f32[50,8,128]{2,1,0:T(8,128)S(1)}, f32[50,8,128]{2,1,0:T(8,128)S(1)}, u32[]{:S(2)}, u32[]{:S(2)}) collective-permute-start(f32[50,8,128]{2,1,0:T(8,128)S(1)} %pad_maximum_fusion.5), channel_id=1, source_target_pairs={{0,8},{8,16},{16,24},{24,32},{32,40},{40,48},{48,56},{56,64},{64,7... | collective-permute-start | bytes 614408 | tf_op jit(solution)/shard_map/ppermute | solution.py:124
  19.0 12.4 %collective-permute-start.2 = (f32[33,8,2,128]{3,2,0,1:T(2,128)S(1)}, f32[33,8,2,128]{3,2,0,1:T(2,128)S(1)}, u32[]{:S(2)}, u32[]{:S(2)}) collective-permute-start(f32[33,8,2,128]{3,2,0,1:T(2,128)S(1)} %get-tuple-element.21), channel_id=1, source_target_pairs={{0,1},{1,2},{2,3},{3,4},{4,5},{5,6},{6,7},{8,9},{9,10},{10,11},{11... | collective-permute-start | bytes 811016 | tf_op jit(solution)/shard_map/ppermute | solution.py:20
  28.0 7.8 %collective-permute-start.3 = (f32[33,8,2,128]{3,2,0,1:T(2,128)S(1)}, f32[33,8,2,128]{3,2,0,1:T(2,128)S(1)}, u32[]{:S(2)}, u32[]{:S(2)}) collective-permute-start(f32[33,8,2,128]{3,2,0,1:T(2,128)S(1)} %get-tuple-element.22), channel_id=1, source_target_pairs={{1,0},{2,1},{3,2},{4,3},{5,4},{6,5},{7,6},{9,8},{10,9},{11,10},{12... | collective-permute-start | bytes 811016 | tf_op jit(solution)/shard_map/ppermute | solution.py:22
  39.5 0.7 %copy-start.5 = (f32[6]{0:T(128)S(1)}, f32[6]{0:T(128)}, u32[]{:S(2)}) copy-start(f32[6]{0:T(128)} %constant.93.clone) | copy-start | bytes 76
  41.7 8.3 %all-to-all-start = ((f32[4,1,2048]{2,1,0:T(1,128)}), f32[4,1,2048]{2,1,0:T(1,128)S(1)}, u32[]{:S(2)}, u32[]{:S(2)}) async-start(f32[4,1,2048]{2,1,0:T(1,128)} %reshape.491), calls=%async_computation | async-start | bytes 65536 | tf_op jit(solution)/shard_map/all_to_all | solution.py:290

commit v10 on v9

--- a/solution.py
+++ b/solution.py
@@ -226,10 +226,18 @@
     start_y = lax.axis_index("gy") * cells_y
     grid = (cells_x, cells_y, depth)
 
-    now = jnp.concatenate([fwd_now[None], adj_now]).reshape((fields * 3,) + grid)
-    prev = jnp.concatenate([fwd_prev[None], adj_prev]).reshape((fields * 3,) + grid)
     comps = fields * 3
-    stacked = jnp.concatenate([now, lame_first[None], shear_mod[None], prev, buoyancy[None]])
+    stacked = jnp.concatenate(
+        [
+            fwd_now,
+            adj_now.reshape((receivers * 3,) + grid),
+            lame_first[None],
+            shear_mod[None],
+            fwd_prev,
+            adj_prev.reshape((receivers * 3,) + grid),
+            buoyancy[None],
+        ]
+    )
     grown = with_halo(exchange_x(stacked, comps + 2, comps), (("gy", 2),), 2)
     span_y = 16 * ((cells_y + 4 + 15) // 16)
     grown = jnp.pad(grown, ((0, 0), (0, 0), (0, span_y - cells_y - 4), (0, 0)))

time: 53.1 us -> 56.4 us (1.062)
  local copies, waits for them, and re-layouts: 4.93 us -> 9.87 us
  other arithmetic: 7.76 us -> 5.86 us
    unnamed x33 -> x37, local copies, waits for them, and re-layouts: 3.11 us -> 8.08 us
    concatenate x3 -> x2, other arithmetic: 1.92 us -> 0.02 us  [local(): jnp.concatenate([fwd_now, adj_now.reshape((receivers * 3,) + grid), lame_...]
  transfers between devices with their start and end apart: 5 -> 5, of which waited for: 4 -> 5; matrix products, arithmetic and copies ran while one was open for 4% -> 4% of each run, Pallas kernels for 0% -> 0%
where the time goes in v10:
time: 56.4 us; the launch traced here: 55.9 us
  starting transfers between devices  20.2 us (36%)
  waiting for transfers between devices  17.3 us (31%)
  local copies, waits for them, and re-layouts  9.87 us (18%)
  other arithmetic  5.86 us (10%)
  between operations  2.59 us (5%)
    ppermute x1, starting transfers between devices, with_halo(): lax.ppermute(tail, axis, [(i, i + 1) for i in range(ends)])  9.03 us
    ppermute x1, waiting for transfers between devices, exchange_x(): lax.ppermute(jnp.concatenate([wide_lo, thin_lo]), 'gx', [(i, i + 1) for i...  8.3 us
    unnamed x37, local copies, waits for them, and re-layouts  8.08 us
    ppermute x1, waiting for transfers between devices, with_halo(): lax.ppermute(head, axis, [(i + 1, i) for i in range(ends)])  4.4 us
    all_to_all x1, starting transfers between devices, local(): gathered = lax.all_to_all(totals, 'grp', 3, 0, tiled=True)  4.01 us
    all_to_all x1, waiting for transfers between devices, local(): gathered = lax.all_to_all(totals, 'grp', 3, 0, tiled=True)  3.32 us
    ppermute x1, starting transfers between devices, exchange_x(): lax.ppermute(jnp.concatenate([wide_lo, thin_lo]), 'gx', [(i, i + 1) for i...  2.92 us
    ppermute x1, starting transfers between devices, exchange_x(): lax.ppermute(jnp.concatenate([wide_hi, thin_hi]), 'gx', [(i + 1, i) for i...  2.36 us
  transfers between devices with their start and end apart: 5, of which 5 were waited for; matrix products, arithmetic and copies ran while one was open for 4% of the time, Pallas kernels for 0%

profile of v10, /device:TPU:321, one launch (start us, length us, event | category | flops | bytes accessed | tf_op | source)
XLA Modules:
  0.0 55.9 jit_solution(3584192498840154887)
XLA Ops:
  0.7 1.0 %copy.174 = f32[4,3,4,8,128]{4,3,1,0,2:T(8,128)S(1)} copy(f32[4,3,4,8,128]{4,3,2,1,0:T(8,128)} %param.16) | data formatting | bytes 393216 | tf_op args[2]
  1.6 0.9 %copy.177 = f32[4,3,4,8,128]{4,3,1,0,2:T(8,128)S(1)} copy(f32[4,3,4,8,128]{4,3,2,1,0:T(8,128)} %param.17) | data formatting | bytes 393216 | tf_op args[3]
  2.6 0.8 %constant_dynamic-update-slice_fusion.6 = (f32[33,4,8,128]{3,2,0,1:T(8,128)S(1)}, f32[3,4,8,128]{3,2,0,1:T(8,128)S(1)}) fusion(f32[3,4,8,128]{3,2,1,0:T(8,128)} %param.14), kind=kLoop, calls=%fused_computation.151 | loop fusion | bytes 147456
  3.5 0.7 %constant_dynamic-update-slice_fusion.4 = (f32[33,4,8,128]{3,2,0,1:T(8,128)S(1)}, f32[18,4,8,128]{3,2,0,1:T(8,128)S(1)}) fusion(f32[33,4,8,128]{3,2,0,1:T(8,128)S(1)} %constant_dynamic-update-slice_fusion.5, f32[4,8,128]{2,1,0:T(8,128)} %param.18), kind=kLoop, calls=%fused_computation.149 | loop fusion | bytes 49152
  4.2 0.7 %constant_dynamic-update-slice_fusion.3 = (f32[33,4,8,128]{3,2,0,1:T(8,128)S(1)}, f32[18,4,8,128]{3,2,0,1:T(8,128)S(1)}) fusion(f32[33,4,8,128]{3,2,0,1:T(8,128)S(1)} %get-tuple-element.57, f32[4,8,128]{2,1,0:T(8,128)} %param.19, f32[18,4,8,128]{3,2,0,1:T(8,128)S(1)} %get-tuple-element.58), kind=kLoop, calls=%fused_computation.148 | loop fusion | bytes 49152
  4.9 0.8 %fusion.73 = (f32[3,4,8,128]{3,2,0,1:T(8,128)S(1)}, f32[33,4,8,128]{3,2,0,1:T(8,128)S(1)}, f32[18,4,8,128]{3,2,0,1:T(8,128)S(1)}) fusion(f32[3,4,8,128]{3,2,1,0:T(8,128)} %param.15, f32[33,4,8,128]{3,2,0,1:T(8,128)S(1)} %get-tuple-element.55, f32[18,4,8,128]{3,2,0,1:T(8,128)S(1)} %get-tuple-element.56), kind=kLoop, calls=%fused_computation.232 | loop fusion | bytes 196608 | tf_op args[1]
  5.8 2.4 %collective-permute-start.1 = (f32[48,8,128]{2,1,0:T(8,128)S(1)}, f32[48,8,128]{2,1,0:T(8,128)S(1)}, u32[]{:S(2)}, u32[]{:S(2)}) collective-permute-start(f32[48,8,128]{2,1,0:T(8,128)S(1)} %pad_maximum_fusion.6), channel_id=1, source_target_pairs={{8,0},{16,8},{24,16},{32,24},{40,32},{48,40},{56,48},{64,56},{72,6... | collective-permute-start | bytes 589832 | tf_op jit(solution)/shard_map/ppermute | solution.py:127
  8.3 2.9 %collective-permute-start = (f32[50,8,128]{2,1,0:T(8,128)S(1)}, f32[50,8,128]{2,1,0:T(8,128)S(1)}, u32[]{:S(2)}, u32[]{:S(2)}) collective-permute-start(f32[50,8,128]{2,1,0:T(8,128)S(1)} %pad_maximum_fusion.3), channel_id=1, source_target_pairs={{0,8},{8,16},{16,24},{24,32},{32,40},{40,48},{48,56},{56,64},{64,7... | collective-permute-start | bytes 614408 | tf_op jit(solution)/shard_map/ppermute | solution.py:124
  13.5 8.3 %collective-permute-done = f32[50,8,128]{2,1,0:T(8,128)S(1)} collective-permute-done((f32[50,8,128]{2,1,0:T(8,128)S(1)}, f32[50,8,128]{2,1,0:T(8,128)S(1)}, u32[]{:S(2)}, u32[]{:S(2)}) %collective-permute-start) | collective-permute-done | bytes 204832 | tf_op jit(solution)/shard_map/ppermute | solution.py:124
  21.9 0.2 maximum_maximum_fusion
  22.1 9.0 %collective-permute-start.2 = (f32[33,8,2,128]{3,2,0,1:T(2,128)S(1)}, f32[33,8,2,128]{3,2,0,1:T(2,128)S(1)}, u32[]{:S(2)}, u32[]{:S(2)}) collective-permute-start(f32[33,8,2,128]{3,2,0,1:T(2,128)S(1)} %get-tuple-element.21), channel_id=1, source_target_pairs={{0,1},{1,2},{2,3},{3,4},{4,5},{5,6},{6,7},{8,9},{9,10},{10,11},{11... | collective-permute-start | bytes 811016 | tf_op jit(solution)/shard_map/ppermute | solution.py:20
  31.1 1.9 %collective-permute-start.3 = (f32[33,8,2,128]{3,2,0,1:T(2,128)S(1)}, f32[33,8,2,128]{3,2,0,1:T(2,128)S(1)}, u32[]{:S(2)}, u32[]{:S(2)}) collective-permute-start(f32[33,8,2,128]{3,2,0,1:T(2,128)S(1)} %get-tuple-element.22), channel_id=1, source_target_pairs={{1,0},{2,1},{3,2},{4,3},{5,4},{6,5},{7,6},{9,8},{10,9},{11,10},{12... | collective-permute-start | bytes 811016 | tf_op jit(solution)/shard_map/ppermute | solution.py:22
  33.3 1.2 %collective-permute-done.2 = f32[33,8,2,128]{3,2,0,1:T(2,128)S(1)} collective-permute-done((f32[33,8,2,128]{3,2,0,1:T(2,128)S(1)}, f32[33,8,2,128]{3,2,0,1:T(2,128)S(1)}, u32[]{:S(2)}, u32[]{:S(2)}) %collective-permute-start.2) | collective-permute-done | bytes 270368 | tf_op jit(solution)/shard_map/ppermute | solution.py:20
  34.5 4.4 %collective-permute-done.3 = f32[33,8,2,128]{3,2,0,1:T(2,128)S(1)} collective-permute-done((f32[33,8,2,128]{3,2,0,1:T(2,128)S(1)}, f32[33,8,2,128]{3,2,0,1:T(2,128)S(1)}, u32[]{:S(2)}, u32[]{:S(2)}) %collective-permute-start.3) | collective-permute-done | bytes 270368 | tf_op jit(solution)/shard_map/ppermute | solution.py:22
  38.9 0.6 %select_maximum_fusion = f32[33,8,16,128]{3,2,0,1:T(8,128)S(1)} fusion(f32[33,8,2,128]{3,2,0,1:T(2,128)S(1)} %collective-permute-done.3, f32[33,8,2,128]{3,2,0,1:T(2,128)S(1)} %collective-permute-done.2, f32[18,2,8,128]{3,2,0,1:T(8,128)S(1)} %concatenate.86, f32[33,4,8,128]{3,2,0,1:T(8,128)S(1)} %get-tuple-element.53, f32[16,2,8,128]{3,2,0,1:T(8,128)S(1)} %concatenate.80, ...), kind=kLoop, calls=%fused_computation | loop fusion | flops 7569408 | bytes 3784704 | tf_op jit(solution)/shard_map/concatenate | solution.py:18
  39.6 0.2 fusion.71
  40.0 0.4 pad_subtract_fusion.1
  40.4 0.3 fusion.16
  40.7 0.4 fusion.25
  41.1 0.3 fusion.10
  41.6 0.2 slice.577
  42.9 0.4 copy-done.5
  43.4 0.3 copy.219
  43.6 1.2 %reshape.491 = f32[4,1,2048]{2,1,0:T(1,128)} reshape(f32[128,2,4,8]{3,2,1,0:T(4,128)S(1)} %bitcast.247) | data formatting | bytes 65536
  44.8 4.0 %all-to-all-start = ((f32[4,1,2048]{2,1,0:T(1,128)}), f32[4,1,2048]{2,1,0:T(1,128)S(1)}, u32[]{:S(2)}, u32[]{:S(2)}) async-start(f32[4,1,2048]{2,1,0:T(1,128)} %reshape.491), calls=%async_computation | async-start | bytes 65536 | tf_op jit(solution)/shard_map/all_to_all | solution.py:298
  48.8 0.2 fusion.41
  49.0 0.8 %fusion.27 = f32[4,3,4,8,128]{4,3,2,1,0:T(8,128)} fusion(f32[4,3,4,16,128]{4,3,2,1,0:T(8,128)S(1)} %slice.569, f32[4,1,4,16,128]{4,3,2,1,0:T(8,128)S(1)} %get-tuple-element.47, f32[4,1,4,16,128]{4,3,2,1,0:T(8,128)S(1)} %get-tuple-element.46, f32[4,1,4,16,128]{4,3,2,1,0:T(8,128)S(1)} %get-tuple-element.45, f32[4,8,128]{2,1,0:T(8,128)S(1)} %slice.608, ...), kind=kLoop, calls=%fused_computation.77 | loop fusion | flops 344064 | bytes 1067008 | tf_op jit(solution)/shard_map/add | solution.py:113
  49.8 3.3 %all-to-all-done = f32[4,1,2048]{2,1,0:T(1,128)S(1)} async-done(((f32[4,1,2048]{2,1,0:T(1,128)}), f32[4,1,2048]{2,1,0:T(1,128)S(1)}, u32[]{:S(2)}, u32[]{:S(2)}) %all-to-all-start) | async-done | bytes 32800 | tf_op jit(solution)/shard_map/all_to_all | solution.py:298
  53.1 0.5 broadcast.419
  53.6 0.7 %reduce.4 = f32[4,2048]{1,0:T(4,128)S(1)} reduce(f32[4,1,2048]{2,1,0:T(1,128)S(1)} %all-to-all-done, f32[]{:T(128)} %broadcast.419), dimensions={1}, to_apply=%all_to_all.4.reduce_sub_computation | reduce | bytes 65540 | tf_op jit(solution)/shard_map/all_to_all | solution.py:298
  54.3 0.6 %reshape.492 = f32[128,2,4,8]{3,2,1,0:T(4,128)S(1)} reshape(f32[4,2048]{1,0:T(4,128)S(1)} %reduce.4) | data formatting | bytes 65536
  55.1 0.7 %copy.220 = f32[2,4,8,32]{3,2,1,0:T(8,128)} copy(f32[2,4,8,32]{2,1,0,3:T(4,128)S(1)} %reduce_sum.82) | data formatting | bytes 16384
  (95 shorter events, 3.0 us)
Async XLA Ops:
  0.6 7.6 %copy-start = (f32[4,8,128]{2,1,0:T(8,128)S(1)}, f32[4,8,128]{2,1,0:T(8,128)}, u32[]{:S(2)}) copy-start(f32[4,8,128]{2,1,0:T(8,128)} %param.18) | copy-start | bytes 49156
  0.6 7.6 %copy-start.1 = (f32[4,8,128]{2,1,0:T(8,128)S(1)}, f32[4,8,128]{2,1,0:T(8,128)}, u32[]{:S(2)}) copy-start(f32[4,8,128]{2,1,0:T(8,128)} %param.19) | copy-start | bytes 49156
  0.7 5.1 %copy-start.2 = (f32[4,8,128]{2,1,0:T(8,128)S(1)}, f32[4,8,128]{2,1,0:T(8,128)}, u32[]{:S(2)}) copy-start(f32[4,8,128]{2,1,0:T(8,128)} %param.20) | copy-start | bytes 49156
  1.6 10.9 %copy-start.6 = (s32[4]{0:T(128)S(1)}, s32[4]{0:T(128)}, u32[]{:S(2)}) copy-start(s32[4]{0:T(128)} %param.24) | copy-start | bytes 52
  2.6 10.2 %copy-start.7 = (s32[4]{0:T(128)S(1)}, s32[4]{0:T(128)}, u32[]{:S(2)}) copy-start(s32[4]{0:T(128)} %param.25) | copy-start | bytes 52
  2.6 10.2 %copy-start.4 = (f32[256,3]{0,1:T(4,128)S(1)}, f32[256,3]{0,1:T(4,128)}, u32[]{:S(2)}) copy-start(f32[256,3]{0,1:T(4,128)} %param.23) | copy-start | bytes 9220
  2.6 10.5 %copy-start.3 = (f32[4,256,3]{1,0,2:T(4,128)S(1)}, f32[4,256,3]{1,0,2:T(4,128)}, u32[]{:S(2)}) copy-start(f32[4,256,3]{1,0,2:T(4,128)} %param.26) | copy-start | bytes 36868
  5.8 7.7 %collective-permute-start.1 = (f32[48,8,128]{2,1,0:T(8,128)S(1)}, f32[48,8,128]{2,1,0:T(8,128)S(1)}, u32[]{:S(2)}, u32[]{:S(2)}) collective-permute-start(f32[48,8,128]{2,1,0:T(8,128)S(1)} %pad_maximum_fusion.6), channel_id=1, source_target_pairs={{8,0},{16,8},{24,16},{32,24},{40,32},{48,40},{56,48},{64,56},{72,6... | collective-permute-start | bytes 589832 | tf_op jit(solution)/shard_map/ppermute | solution.py:127
  8.3 13.5 %collective-permute-start = (f32[50,8,128]{2,1,0:T(8,128)S(1)}, f32[50,8,128]{2,1,0:T(8,128)S(1)}, u32[]{:S(2)}, u32[]{:S(2)}) collective-permute-start(f32[50,8,128]{2,1,0:T(8,128)S(1)} %pad_maximum_fusion.3), channel_id=1, source_target_pairs={{0,8},{8,16},{16,24},{24,32},{32,40},{40,48},{48,56},{56,64},{64,7... | collective-permute-start | bytes 614408 | tf_op jit(solution)/shard_map/ppermute | solution.py:124
  22.1 12.4 %collective-permute-start.2 = (f32[33,8,2,128]{3,2,0,1:T(2,128)S(1)}, f32[33,8,2,128]{3,2,0,1:T(2,128)S(1)}, u32[]{:S(2)}, u32[]{:S(2)}) collective-permute-start(f32[33,8,2,128]{3,2,0,1:T(2,128)S(1)} %get-tuple-element.21), channel_id=1, source_target_pairs={{0,1},{1,2},{2,3},{3,4},{4,5},{5,6},{6,7},{8,9},{9,10},{10,11},{11... | collective-permute-start | bytes 811016 | tf_op jit(solution)/shard_map/ppermute | solution.py:20
  31.1 7.8 %collective-permute-start.3 = (f32[33,8,2,128]{3,2,0,1:T(2,128)S(1)}, f32[33,8,2,128]{3,2,0,1:T(2,128)S(1)}, u32[]{:S(2)}, u32[]{:S(2)}) collective-permute-start(f32[33,8,2,128]{3,2,0,1:T(2,128)S(1)} %get-tuple-element.22), channel_id=1, source_target_pairs={{1,0},{2,1},{3,2},{4,3},{5,4},{6,5},{7,6},{9,8},{10,9},{11,10},{12... | collective-permute-start | bytes 811016 | tf_op jit(solution)/shard_map/ppermute | solution.py:22
  42.6 0.7 %copy-start.5 = (f32[6]{0:T(128)S(1)}, f32[6]{0:T(128)}, u32[]{:S(2)}) copy-start(f32[6]{0:T(128)} %constant.93.clone) | copy-start | bytes 76
  44.8 8.3 %all-to-all-start = ((f32[4,1,2048]{2,1,0:T(1,128)}), f32[4,1,2048]{2,1,0:T(1,128)S(1)}, u32[]{:S(2)}, u32[]{:S(2)}) async-start(f32[4,1,2048]{2,1,0:T(1,128)} %reshape.491), calls=%async_computation | async-start | bytes 65536 | tf_op jit(solution)/shard_map/all_to_all | solution.py:298

commit v11 on v9

--- a/solution.py
+++ b/solution.py
@@ -287,8 +287,12 @@
     totals = totals * (1.0 / (STEPS * receivers * groups))
 
     share = depth // groups
-    gathered = lax.all_to_all(totals, "grp", 3, 0, tiled=True)
-    kernels = jnp.sum(gathered.reshape((groups, 2, cells_x, cells_y, share)), axis=0)
+    chunk = 2 * cells_x * cells_y * share
+    parts = jnp.moveaxis(totals.reshape((2, cells_x, cells_y, groups, share)), 3, 0)
+    parts = parts.reshape((groups, chunk // 128, 128))
+    gathered = lax.all_to_all(parts, "grp", 0, 0, tiled=True)
+    kernels = jnp.sum(gathered.reshape((groups, chunk // 128, 128)), axis=0)
+    kernels = kernels.reshape((2, cells_x, cells_y, share))
     return (final, kernels)
 
 

time: 53.1 us -> 64.4 us (1.21)
  other arithmetic: 7.76 us -> 16.2 us
  local copies, waits for them, and re-layouts: 4.93 us -> 9.35 us
  waiting for transfers between devices: 17.2 us -> 15.6 us
    unnamed x6, other arithmetic: 0.15 us -> 2.85 us
    reshape x0 -> x2, local copies, waits for them, and re-layouts: none -> 1.4 us  [the longest x1 0.71 us: local(): parts = parts.reshape((groups, chunk // 128, 128))]
    another operation x3, other arithmetic: 0.09 us -> 1.4 us  [dense_stencil(): jnp.stack([strain_xx, strain_yy, strain_zz, strain_xy, strain_xz, strain_...]
    unnamed x33 -> x36, local copies, waits for them, and re-layouts: 3.11 us -> 4.26 us
    reduce_sum x2, other arithmetic: 0.08 us -> 1.23 us  [local(): summed = jnp.sum(strain, axis=0)]
    reduce_sum x1, other arithmetic: 0.09 us -> 1.19 us  [local(): shear_term = 2.0 * jnp.sum(weights * master * summed, axis=0)]
    all_to_all x1, waiting for transfers between devices: 3.32 us -> 2.32 us  [local(): gathered = lax.all_to_all(parts, 'grp', 0, 0, tiled=True)]
    another operation x2, other arithmetic: 0.59 us -> 1.56 us  [dense_stencil(): force = jnp.stack([force_x, force_y, force_z], axis=1)]
  transfers between devices with their start and end apart: 5 -> 5, of which waited for: 4 -> 4; matrix products, arithmetic and copies ran while one was open for 4% -> 6% of each run, Pallas kernels for 0% -> 0%
where the time goes in v11:
time: 64.4 us; the launch traced here: 64 us
  starting transfers between devices  20.2 us (31%)
  other arithmetic  16.2 us (25%)
  waiting for transfers between devices  15.6 us (24%)
  local copies, waits for them, and re-layouts  9.35 us (15%)
  between operations  2.57 us (4%)
    ppermute x1, starting transfers between devices, with_halo(): lax.ppermute(tail, axis, [(i, i + 1) for i in range(ends)])  9.03 us
    ppermute x1, waiting for transfers between devices, exchange_x(): lax.ppermute(jnp.concatenate([wide_lo, thin_lo]), 'gx', [(i, i + 1) for i...  8.27 us
    ppermute x1, waiting for transfers between devices, with_halo(): lax.ppermute(head, axis, [(i + 1, i) for i in range(ends)])  4.4 us
    unnamed x36, local copies, waits for them, and re-layouts  4.26 us
    all_to_all x1, starting transfers between devices, local(): gathered = lax.all_to_all(parts, 'grp', 0, 0, tiled=True)  4.01 us
    ppermute x1, starting transfers between devices, exchange_x(): lax.ppermute(jnp.concatenate([wide_lo, thin_lo]), 'gx', [(i, i + 1) for i...  2.92 us
    unnamed x6, other arithmetic  2.85 us
    ppermute x1, starting transfers between devices, exchange_x(): lax.ppermute(jnp.concatenate([wide_hi, thin_hi]), 'gx', [(i + 1, i) for i...  2.36 us
  transfers between devices with their start and end apart: 5, of which 4 were waited for; matrix products, arithmetic and copies ran while one was open for 6% of the time, Pallas kernels for 0%

profile of v11, /device:TPU:321, one launch (start us, length us, event | category | flops | bytes accessed | tf_op | source)
XLA Modules:
  0.0 64.0 jit_solution(8760778547366363028)
XLA Ops:
  0.7 1.0 %pad_maximum_fusion.3 = f32[5,3,4,8,128]{4,3,2,1,0:T(8,128)S(1)} fusion(f32[4,3,4,8,128]{4,3,2,1,0:T(8,128)} %param.16, f32[1,3,4,8,128]{4,3,2,1,0:T(8,128)} %bitcast.283), kind=kLoop, calls=%fused_computation.75 | loop fusion | flops 61440 | bytes 491520 | tf_op jit(solution)/shard_map/concatenate | solution.py:229
  1.7 0.9 %pad_maximum_fusion.4 = f32[5,3,4,8,128]{4,3,2,1,0:T(8,128)S(1)} fusion(f32[4,3,4,8,128]{4,3,2,1,0:T(8,128)} %param.17, f32[1,3,4,8,128]{4,3,2,1,0:T(8,128)} %bitcast.284), kind=kLoop, calls=%fused_computation.76 | loop fusion | flops 61440 | bytes 491520 | tf_op jit(solution)/shard_map/concatenate | solution.py:230
  2.8 2.4 %collective-permute-start.1 = (f32[48,8,128]{2,1,0:T(8,128)S(1)}, f32[48,8,128]{2,1,0:T(8,128)S(1)}, u32[]{:S(2)}, u32[]{:S(2)}) collective-permute-start(f32[48,8,128]{2,1,0:T(8,128)S(1)} %pad_maximum_fusion.8), channel_id=1, source_target_pairs={{8,0},{16,8},{24,16},{32,24},{40,32},{48,40},{56,48},{64,56},{72,6... | collective-permute-start | bytes 589832 | tf_op jit(solution)/shard_map/ppermute | solution.py:127
  5.2 2.9 %collective-permute-start = (f32[50,8,128]{2,1,0:T(8,128)S(1)}, f32[50,8,128]{2,1,0:T(8,128)S(1)}, u32[]{:S(2)}, u32[]{:S(2)}) collective-permute-start(f32[50,8,128]{2,1,0:T(8,128)S(1)} %pad_maximum_fusion.5), channel_id=1, source_target_pairs={{0,8},{8,16},{16,24},{24,32},{32,40},{40,48},{48,56},{56,64},{64,7... | collective-permute-start | bytes 614408 | tf_op jit(solution)/shard_map/ppermute | solution.py:124
  10.5 8.3 %collective-permute-done = f32[50,8,128]{2,1,0:T(8,128)S(1)} collective-permute-done((f32[50,8,128]{2,1,0:T(8,128)S(1)}, f32[50,8,128]{2,1,0:T(8,128)S(1)}, u32[]{:S(2)}, u32[]{:S(2)}) %collective-permute-start) | collective-permute-done | bytes 204832 | tf_op jit(solution)/shard_map/ppermute | solution.py:124
  19.0 9.0 %collective-permute-start.2 = (f32[33,8,2,128]{3,2,0,1:T(2,128)S(1)}, f32[33,8,2,128]{3,2,0,1:T(2,128)S(1)}, u32[]{:S(2)}, u32[]{:S(2)}) collective-permute-start(f32[33,8,2,128]{3,2,0,1:T(2,128)S(1)} %get-tuple-element.19), channel_id=1, source_target_pairs={{0,1},{1,2},{2,3},{3,4},{4,5},{5,6},{6,7},{8,9},{9,10},{10,11},{11... | collective-permute-start | bytes 811016 | tf_op jit(solution)/shard_map/ppermute | solution.py:20
  28.0 1.9 %collective-permute-start.3 = (f32[33,8,2,128]{3,2,0,1:T(2,128)S(1)}, f32[33,8,2,128]{3,2,0,1:T(2,128)S(1)}, u32[]{:S(2)}, u32[]{:S(2)}) collective-permute-start(f32[33,8,2,128]{3,2,0,1:T(2,128)S(1)} %get-tuple-element.20), channel_id=1, source_target_pairs={{1,0},{2,1},{3,2},{4,3},{5,4},{6,5},{7,6},{9,8},{10,9},{11,10},{12... | collective-permute-start | bytes 811016 | tf_op jit(solution)/shard_map/ppermute | solution.py:22
  30.1 0.6 slice.604
  30.8 0.6 collective-permute-done.2
  31.4 4.4 %collective-permute-done.3 = f32[33,8,2,128]{3,2,0,1:T(2,128)S(1)} collective-permute-done((f32[33,8,2,128]{3,2,0,1:T(2,128)S(1)}, f32[33,8,2,128]{3,2,0,1:T(2,128)S(1)}, u32[]{:S(2)}, u32[]{:S(2)}) %collective-permute-start.3) | collective-permute-done | bytes 270368 | tf_op jit(solution)/shard_map/ppermute | solution.py:22
  36.7 0.8 %slice.568 = f32[4,3,4,16,128]{4,3,2,1,0:T(8,128)} slice(f32[5,3,8,16,128]{4,3,2,1,0:T(8,128)S(1)} %bitcast.248), slice={[1:5], [0:3], [2:6], [0:16], [0:128]} | slice | bytes 786432 | tf_op jit(solution)/shard_map/slice | solution.py:273
  39.3 0.8 %slice_multiply_fusion = f32[4,3,4,16,128]{4,3,2,0,1:T(8,128)} fusion(f32[5,3,6,16,128]{4,3,2,0,1:T(8,128)S(1)} %fusion.10), kind=kLoop, calls=%fused_computation.25 | loop fusion | flops 98304 | bytes 786432 | tf_op jit(solution)/shard_map/mul | solution.py:113
  40.3 0.8 %bitcast_dynamic-update-slice_fusion.1 = f32[5,6,7,16,128]{4,3,2,1,0:T(8,128)} fusion(f32[5,3,7,16,128]{4,3,2,0,1:T(8,128)S(1)} %get-tuple-element.27), kind=kLoop, calls=%fused_computation.40 | loop fusion | bytes 573440
  42.4 0.6 constant_dynamic-update-slice_fusion.8
  43.0 0.6 %constant_dynamic-update-slice_fusion.7 = f32[1,6,5,16,128]{4,3,2,0,1:T(8,128)} fusion(f32[1,6,5,16,128]{4,3,2,0,1:T(8,128)} %constant_dynamic-update-slice_fusion.8, f32[1,3,5,16,128]{4,3,2,1,0:T(8,128)S(1)} %get-tuple-element.29, f32[1,3,5,16,128]{4,3,2,1,0:T(8,128)S(1)} %get-tuple-element.28), kind=kLoop, calls=%fused_computation.163 | loop fusion | flops 20480 | bytes 122880
  43.6 0.6 constant_dynamic-update-slice_fusion.6
  45.0 0.8 %fusion.34 = (f32[4,5,16,128]{3,2,1,0:T(8,128)}, f32[4,5,16,128]{3,2,1,0:T(8,128)S(1)}, f32[4,5,16,128]{3,2,1,0:T(8,128)S(1)}, f32[4,5,16,128]{3,2,1,0:T(8,128)S(1)}, f32[4,5,16,128]{3,2,1,0:T(8,128)S(1)}) fusion(f32[4,3,5,16,128]{4,3,2,0,1:T(8,128)S(1)} %get-tuple-element.32, f32[5,16,128]{2,1,0:T(8,128)S(1)} %get-tuple-element.11, ...), kind=kLoop, calls=%fused_computation.100 | loop fusion | flops 450560 | bytes 2416640 | tf_op jit(solution)/shard_map/add | solution.py:181
  46.0 0.7 %stack.68 = f32[1,4,8,4,32]{4,3,2,1,0:T(4,128)} reshape(f32[1,4,8,128]{3,2,1,0:T(8,128)S(1)} %fusion.65) | data formatting | bytes 32768 | tf_op jit(solution)/shard_map/stack | solution.py:286
  46.8 0.7 %bitcast_dynamic-update-slice_fusion = f32[5,6,7,16,128]{4,3,2,1,0:T(8,128)} fusion(f32[5,6,7,16,128]{4,3,2,1,0:T(8,128)} %bitcast_dynamic-update-slice_fusion.1, f32[5,3,7,16,128]{4,3,2,0,1:T(8,128)S(1)} %get-tuple-element.26), kind=kLoop, calls=%fused_computation.39 | loop fusion | bytes 573440
  47.5 0.7 %slice_dynamic-update-slice_fusion = f32[5,6,7,16,128]{4,3,2,1,0:T(8,128)} fusion(f32[5,6,7,16,128]{4,3,2,1,0:T(8,128)} %bitcast_dynamic-update-slice_fusion, f32[5,3,7,16,128]{4,3,2,1,0:T(8,128)S(1)} %copy_subtract_fusion), kind=kLoop, calls=%fused_computation.56 | loop fusion | bytes 573440
  48.2 0.8 %multiply_dynamic-update-slice_fusion.1 = f32[5,6,7,16,128]{4,3,2,1,0:T(8,128)} fusion(f32[5,6,7,16,128]{4,3,2,1,0:T(8,128)} %slice_dynamic-update-slice_fusion, f32[5,3,7,16,128]{4,3,2,0,1:T(8,128)S(1)} %get-tuple-element.27, f32[5,3,7,16,128]{4,3,2,0,1:T(8,128)S(1)} %get-tuple-element.26), kind=kLoop, calls=%fused_computation.50 | loop fusion | flops 143360 | bytes 860160
  49.0 0.8 %fusion.15 = f32[5,6,7,16,128]{4,3,2,1,0:T(8,128)} fusion(f32[5,6,7,16,128]{4,3,2,1,0:T(8,128)} %multiply_dynamic-update-slice_fusion.1, f32[5,3,7,16,128]{4,3,2,0,1:T(8,128)S(1)} %get-tuple-element.27, f32[5,3,7,16,128]{4,3,2,1,0:T(8,128)S(1)} %copy_subtract_fusion), kind=kLoop, calls=%fused_computation.38 | loop fusion | flops 143360 | bytes 860160
  49.8 0.8 %multiply_dynamic-update-slice_fusion = f32[5,6,7,16,128]{4,3,2,1,0:T(8,128)} fusion(f32[5,6,7,16,128]{4,3,2,1,0:T(8,128)} %fusion.15, f32[5,3,7,16,128]{4,3,2,0,1:T(8,128)S(1)} %get-tuple-element.26, f32[5,3,7,16,128]{4,3,2,1,0:T(8,128)S(1)} %copy_subtract_fusion), kind=kLoop, calls=%fused_computation.49 | loop fusion | flops 143360 | bytes 860160 | tf_op jit(solution)/shard_map/stack | solution.py:201
  50.5 1.2 %slice_reduce_fusion.1 = f32[6,4,8,128]{3,2,1,0:T(8,128)S(1)} fusion(f32[5,6,7,16,128]{4,3,2,1,0:T(8,128)} %multiply_dynamic-update-slice_fusion), kind=kLoop, calls=%fused_computation.24 | loop fusion | flops 73728 | bytes 491520 | tf_op jit(solution)/shard_map/reduce_sum | solution.py:283
  51.8 1.2 %fusion.49 = (f32[4,8,128]{2,1,0:T(8,128)S(1)}, f32[4,8,128]{2,1,0:T(8,128)S(1)}) fusion(f32[6,4,8,128]{3,2,1,0:T(8,128)S(1)} %slice_reduce_fusion, f32[1,6,5,16,128]{4,3,2,0,1:T(8,128)} %constant_dynamic-update-slice_fusion.5, f32[6]{0:T(128)S(1)} %copy-done.8, f32[6,4,8,128]{3,2,1,0:T(8,128)S(1)} %slice_reduce_fusion.1, ...), kind=kLoop, calls=%fused_computation.138 | loop fusion | flops 139264 | bytes 426008 | tf_op jit(solution)/shard_map/reduce_sum | solution.py:285
  53.3 0.9 %fusion.45 = f32[4,2,4,8,32]{4,0,3,2,1:T(4,128)S(1)} fusion(f32[1,4,8,4,32]{4,3,2,1,0:T(4,128)S(1)} %mul.397, f32[1,4,8,4,32]{4,3,2,1,0:T(4,128)S(1)} %stack.65, f32[1,4,8,4,32]{4,3,2,1,0:T(4,128)S(1)} %mul.408, f32[1,4,8,4,32]{4,3,2,1,0:T(4,128)} %stack.68), kind=kLoop, calls=%fused_computation.129 | loop fusion | flops 32768 | bytes 98304 | tf_op jit(solution)/shard_map/transpose | solution.py:291
  54.2 0.7 %reshape.506 = f32[4,16,128]{2,1,0:T(8,128)} reshape(f32[4,2,4,8,32]{4,3,2,1,0:T(8,128)S(1)} %copy.167) | data formatting | bytes 65536 | tf_op jit(solution)/shard_map/reshape | solution.py:292
  54.9 4.0 %all-to-all-start = ((f32[4,16,128]{2,1,0:T(8,128)}), f32[4,16,128]{2,1,0:T(8,128)S(1)}, u32[]{:S(2)}, u32[]{:S(2)}) async-start(f32[4,16,128]{2,1,0:T(8,128)} %reshape.506), calls=%async_computation | async-start | bytes 65536 | tf_op jit(solution)/shard_map/all_to_all | solution.py:293
  59.0 1.2 %fusion.42 = (f32[4,1,4,16,128]{4,3,2,1,0:T(8,128)S(1)}, f32[4,1,4,16,128]{4,3,2,1,0:T(8,128)S(1)}, f32[4,1,4,16,128]{4,3,2,1,0:T(8,128)S(1)}) fusion(f32[4,5,16,127]{3,2,1,0:T(8,128)S(1)} %bitcast.266, f32[4,5,15,128]{3,2,1,0:T(8,128)S(1)} %bitcast.265, f32[4,5,16,128]{3,2,1,0:T(8,128)} %get-tuple-element.6, f32[4,5,16,128]{3,2,1,0:T(8,128)S(1)} %get-tuple-element.22, ...), kind=kLoop, calls=%fused_computation.123 | loop fusion | flops 491520 | bytes 2521344 | tf_op jit(solution)/shard_map/stack | solution.py:200
  60.2 0.8 %fusion.28 = f32[4,3,4,8,128]{4,3,2,1,0:T(8,128)} fusion(f32[4,3,4,16,128]{4,3,2,1,0:T(8,128)S(1)} %copy-done, f32[4,1,4,16,128]{4,3,2,1,0:T(8,128)S(1)} %get-tuple-element.42, f32[4,1,4,16,128]{4,3,2,1,0:T(8,128)S(1)} %get-tuple-element.41, f32[4,1,4,16,128]{4,3,2,1,0:T(8,128)S(1)} %get-tuple-element.40, f32[4,8,128]{2,1,0:T(8,128)S(1)} %slice.607, ...), kind=kLoop, calls=%fused_computation.80 | loop fusion | flops 344064 | bytes 1067008 | tf_op jit(solution)/shard_map/add | solution.py:113
  60.9 2.3 %all-to-all-done = f32[4,16,128]{2,1,0:T(8,128)S(1)} async-done(((f32[4,16,128]{2,1,0:T(8,128)}), f32[4,16,128]{2,1,0:T(8,128)S(1)}, u32[]{:S(2)}, u32[]{:S(2)}) %all-to-all-start) | async-done | bytes 32800 | tf_op jit(solution)/shard_map/all_to_all | solution.py:293
  63.3 0.7 %reshape.507 = f32[2,4,8,32]{3,2,1,0:T(8,128)} reshape(f32[16,128]{1,0:T(8,128)S(1)} %reduce_sum.82) | data formatting | bytes 16384 | tf_op jit(solution)/shard_map/reshape | solution.py:295
  (104 shorter events, 6.9 us)
Async XLA Ops:
  0.6 2.1 %copy-start.5 = (f32[4,8,128]{2,1,0:T(8,128)S(1)}, f32[4,8,128]{2,1,0:T(8,128)}, u32[]{:S(2)}) copy-start(f32[4,8,128]{2,1,0:T(8,128)} %param.20) | copy-start | bytes 49156
  0.6 2.1 %copy-start.4 = (f32[4,8,128]{2,1,0:T(8,128)S(1)}, f32[4,8,128]{2,1,0:T(8,128)}, u32[]{:S(2)}) copy-start(f32[4,8,128]{2,1,0:T(8,128)} %param.19) | copy-start | bytes 49156
  0.7 2.1 %copy-start.3 = (f32[4,8,128]{2,1,0:T(8,128)S(1)}, f32[4,8,128]{2,1,0:T(8,128)}, u32[]{:S(2)}) copy-start(f32[4,8,128]{2,1,0:T(8,128)} %param.18) | copy-start | bytes 49156
  1.7 7.9 %copy-start.9 = (s32[4]{0:T(128)S(1)}, s32[4]{0:T(128)}, u32[]{:S(2)}) copy-start(s32[4]{0:T(128)} %param.24) | copy-start | bytes 52
  1.7 8.0 %copy-start.10 = (s32[4]{0:T(128)S(1)}, s32[4]{0:T(128)}, u32[]{:S(2)}) copy-start(s32[4]{0:T(128)} %param.25) | copy-start | bytes 52
  1.7 8.1 %copy-start.7 = (f32[256,3]{0,1:T(4,128)S(1)}, f32[256,3]{0,1:T(4,128)}, u32[]{:S(2)}) copy-start(f32[256,3]{0,1:T(4,128)} %param.23) | copy-start | bytes 9220
  1.7 8.4 %copy-start.6 = (f32[4,256,3]{1,0,2:T(4,128)S(1)}, f32[4,256,3]{1,0,2:T(4,128)}, u32[]{:S(2)}) copy-start(f32[4,256,3]{1,0,2:T(4,128)} %param.26) | copy-start | bytes 36868
  2.8 7.7 %collective-permute-start.1 = (f32[48,8,128]{2,1,0:T(8,128)S(1)}, f32[48,8,128]{2,1,0:T(8,128)S(1)}, u32[]{:S(2)}, u32[]{:S(2)}) collective-permute-start(f32[48,8,128]{2,1,0:T(8,128)S(1)} %pad_maximum_fusion.8), channel_id=1, source_target_pairs={{8,0},{16,8},{24,16},{32,24},{40,32},{48,40},{56,48},{64,56},{72,6... | collective-permute-start | bytes 589832 | tf_op jit(solution)/shard_map/ppermute | solution.py:127
  5.2 13.5 %collective-permute-start = (f32[50,8,128]{2,1,0:T(8,128)S(1)}, f32[50,8,128]{2,1,0:T(8,128)S(1)}, u32[]{:S(2)}, u32[]{:S(2)}) collective-permute-start(f32[50,8,128]{2,1,0:T(8,128)S(1)} %pad_maximum_fusion.5), channel_id=1, source_target_pairs={{0,8},{8,16},{16,24},{24,32},{32,40},{40,48},{48,56},{56,64},{64,7... | collective-permute-start | bytes 614408 | tf_op jit(solution)/shard_map/ppermute | solution.py:124
  19.0 12.4 %collective-permute-start.2 = (f32[33,8,2,128]{3,2,0,1:T(2,128)S(1)}, f32[33,8,2,128]{3,2,0,1:T(2,128)S(1)}, u32[]{:S(2)}, u32[]{:S(2)}) collective-permute-start(f32[33,8,2,128]{3,2,0,1:T(2,128)S(1)} %get-tuple-element.19), channel_id=1, source_target_pairs={{0,1},{1,2},{2,3},{3,4},{4,5},{5,6},{6,7},{8,9},{9,10},{10,11},{11... | collective-permute-start | bytes 811016 | tf_op jit(solution)/shard_map/ppermute | solution.py:20
  28.0 7.8 %collective-permute-start.3 = (f32[33,8,2,128]{3,2,0,1:T(2,128)S(1)}, f32[33,8,2,128]{3,2,0,1:T(2,128)S(1)}, u32[]{:S(2)}, u32[]{:S(2)}) collective-permute-start(f32[33,8,2,128]{3,2,0,1:T(2,128)S(1)} %get-tuple-element.20), channel_id=1, source_target_pairs={{1,0},{2,1},{3,2},{4,3},{5,4},{6,5},{7,6},{9,8},{10,9},{11,10},{12... | collective-permute-start | bytes 811016 | tf_op jit(solution)/shard_map/ppermute | solution.py:22
  46.8 5.0 %copy-start.8 = (f32[6]{0:T(128)S(1)}, f32[6]{0:T(128)}, u32[]{:S(2)}) copy-start(f32[6]{0:T(128)} %constant.93.clone) | copy-start | bytes 76
  51.8 8.4 %copy-start = (f32[4,3,4,16,128]{4,3,2,1,0:T(8,128)S(1)}, f32[4,3,4,16,128]{4,3,2,1,0:T(8,128)}, u32[]{:S(2)}) copy-start(f32[4,3,4,16,128]{4,3,2,1,0:T(8,128)} %slice.568) | copy-start | bytes 1179652
  51.8 8.4 %copy-start.1 = (f32[4,3,4,16,128]{4,3,2,0,1:T(8,128)S(1)}, f32[4,3,4,16,128]{4,3,2,0,1:T(8,128)}, u32[]{:S(2)}) copy-start(f32[4,3,4,16,128]{4,3,2,0,1:T(8,128)} %slice_multiply_fusion) | copy-start | bytes 1179652
  51.8 8.4 %copy-start.2 = (f32[4,4,8,128]{3,2,1,0:T(8,128)S(1)}, f32[4,4,8,128]{3,2,1,0:T(8,128)}, u32[]{:S(2)}) copy-start(f32[4,4,8,128]{3,2,1,0:T(8,128)} %slice.604) | copy-start | bytes 196612
  54.9 8.3 %all-to-all-start = ((f32[4,16,128]{2,1,0:T(8,128)}), f32[4,16,128]{2,1,0:T(8,128)S(1)}, u32[]{:S(2)}, u32[]{:S(2)}) async-start(f32[4,16,128]{2,1,0:T(8,128)} %reshape.506), calls=%async_computation | async-start | bytes 65536 | tf_op jit(solution)/shard_map/all_to_all | solution.py:293

commit v12 on v11

--- a/solution.py
+++ b/solution.py
@@ -288,6 +288,7 @@
 
     share = depth // groups
     chunk = 2 * cells_x * cells_y * share
+    totals = lax.optimization_barrier(totals)
     parts = jnp.moveaxis(totals.reshape((2, cells_x, cells_y, groups, share)), 3, 0)
     parts = parts.reshape((groups, chunk // 128, 128))
     gathered = lax.all_to_all(parts, "grp", 0, 0, tiled=True)

time: 64.4 us -> 50.5 us (0.78)
  other arithmetic: 16.2 us -> 6.89 us
  local copies, waits for them, and re-layouts: 9.35 us -> 3.16 us
  waiting for transfers between devices: 15.6 us -> 17.2 us
    unnamed x36 -> x30, local copies, waits for them, and re-layouts: 4.26 us -> 0.58 us
    unnamed x6, other arithmetic: 2.85 us -> 0.15 us
    another operation x3, other arithmetic: 1.4 us -> 0.09 us  [dense_stencil(): jnp.stack([strain_xx, strain_yy, strain_zz, strain_xy, strain_xz, strain_...]
    reduce_sum x2, other arithmetic: 1.23 us -> 0.08 us  [local(): summed = jnp.sum(strain, axis=0)]
    reduce_sum x1, other arithmetic: 1.19 us -> 0.09 us  [local(): shear_term = 2.0 * jnp.sum(weights * master * summed, axis=0)]
    all_to_all x1, waiting for transfers between devices: 2.32 us -> 3.32 us  [local(): gathered = lax.all_to_all(parts, 'grp', 0, 0, tiled=True)]
    another operation x2, other arithmetic: 1.56 us -> 0.59 us  [dense_stencil(): force = jnp.stack([force_x, force_y, force_z], axis=1)]
    transpose x1 -> x0, other arithmetic: 0.91 us -> none  [local(): jnp.moveaxis(totals.reshape((2, cells_x, cells_y, groups, share)), 3, 0)]
  transfers between devices with their start and end apart: 5 -> 5, of which waited for: 4 -> 4; matrix products, arithmetic and copies ran while one was open for 6% -> 4% of each run, Pallas kernels for 0% -> 0%
where the time goes in v12:
time: 50.5 us; the launch traced here: 50.1 us
  starting transfers between devices  20.2 us (40%)
  waiting for transfers between devices  17.2 us (34%)
  other arithmetic  6.89 us (14%)
  local copies, waits for them, and re-layouts  3.16 us (6%)
  between operations  2.62 us (5%)
    ppermute x1, starting transfers between devices, with_halo(): lax.ppermute(tail, axis, [(i, i + 1) for i in range(ends)])  9.03 us
    ppermute x1, waiting for transfers between devices, exchange_x(): lax.ppermute(jnp.concatenate([wide_lo, thin_lo]), 'gx', [(i, i + 1) for i...  8.27 us
    ppermute x1, waiting for transfers between devices, with_halo(): lax.ppermute(head, axis, [(i + 1, i) for i in range(ends)])  4.4 us
    all_to_all x1, starting transfers between devices, local(): gathered = lax.all_to_all(parts, 'grp', 0, 0, tiled=True)  4.01 us
    all_to_all x1, waiting for transfers between devices, local(): gathered = lax.all_to_all(parts, 'grp', 0, 0, tiled=True)  3.32 us
    ppermute x1, starting transfers between devices, exchange_x(): lax.ppermute(jnp.concatenate([wide_lo, thin_lo]), 'gx', [(i, i + 1) for i...  2.92 us
    ppermute x1, starting transfers between devices, exchange_x(): lax.ppermute(jnp.concatenate([wide_hi, thin_hi]), 'gx', [(i + 1, i) for i...  2.36 us
    ppermute x1, starting transfers between devices, with_halo(): lax.ppermute(head, axis, [(i + 1, i) for i in range(ends)])  1.92 us
  transfers between devices with their start and end apart: 5, of which 4 were waited for; matrix products, arithmetic and copies ran while one was open for 4% of the time, Pallas kernels for 0%

profile of v12, /device:TPU:321, one launch (start us, length us, event | category | flops | bytes accessed | tf_op | source)
XLA Modules:
  0.0 50.1 jit_solution(14264805630904953121)
XLA Ops:
  0.7 1.0 %pad_maximum_fusion.3 = f32[5,3,4,8,128]{4,3,2,1,0:T(8,128)S(1)} fusion(f32[4,3,4,8,128]{4,3,2,1,0:T(8,128)} %param.16, f32[1,3,4,8,128]{4,3,2,1,0:T(8,128)} %bitcast.270), kind=kLoop, calls=%fused_computation.74 | loop fusion | flops 61440 | bytes 491520 | tf_op jit(solution)/shard_map/concatenate | solution.py:229
  1.7 0.9 %pad_maximum_fusion.4 = f32[5,3,4,8,128]{4,3,2,1,0:T(8,128)S(1)} fusion(f32[4,3,4,8,128]{4,3,2,1,0:T(8,128)} %param.17, f32[1,3,4,8,128]{4,3,2,1,0:T(8,128)} %bitcast.271), kind=kLoop, calls=%fused_computation.75 | loop fusion | flops 61440 | bytes 491520 | tf_op jit(solution)/shard_map/concatenate | solution.py:230
  2.8 2.4 %collective-permute-start.1 = (f32[48,8,128]{2,1,0:T(8,128)S(1)}, f32[48,8,128]{2,1,0:T(8,128)S(1)}, u32[]{:S(2)}, u32[]{:S(2)}) collective-permute-start(f32[48,8,128]{2,1,0:T(8,128)S(1)} %pad_maximum_fusion.8), channel_id=1, source_target_pairs={{8,0},{16,8},{24,16},{32,24},{40,32},{48,40},{56,48},{64,56},{72,6... | collective-permute-start | bytes 589832 | tf_op jit(solution)/shard_map/ppermute | solution.py:127
  5.2 2.9 %collective-permute-start = (f32[50,8,128]{2,1,0:T(8,128)S(1)}, f32[50,8,128]{2,1,0:T(8,128)S(1)}, u32[]{:S(2)}, u32[]{:S(2)}) collective-permute-start(f32[50,8,128]{2,1,0:T(8,128)S(1)} %pad_maximum_fusion.5), channel_id=1, source_target_pairs={{0,8},{8,16},{16,24},{24,32},{32,40},{40,48},{48,56},{56,64},{64,7... | collective-permute-start | bytes 614408 | tf_op jit(solution)/shard_map/ppermute | solution.py:124
  9.8 0.1 select_reduce_fusion.2
  9.9 0.1 copy.133
  10.5 8.3 %collective-permute-done = f32[50,8,128]{2,1,0:T(8,128)S(1)} collective-permute-done((f32[50,8,128]{2,1,0:T(8,128)S(1)}, f32[50,8,128]{2,1,0:T(8,128)S(1)}, u32[]{:S(2)}, u32[]{:S(2)}) %collective-permute-start) | collective-permute-done | bytes 204832 | tf_op jit(solution)/shard_map/ppermute | solution.py:124
  18.8 0.2 maximum_maximum_fusion
  19.0 9.0 %collective-permute-start.2 = (f32[33,8,2,128]{3,2,0,1:T(2,128)S(1)}, f32[33,8,2,128]{3,2,0,1:T(2,128)S(1)}, u32[]{:S(2)}, u32[]{:S(2)}) collective-permute-start(f32[33,8,2,128]{3,2,0,1:T(2,128)S(1)} %get-tuple-element.19), channel_id=1, source_target_pairs={{0,1},{1,2},{2,3},{3,4},{4,5},{5,6},{6,7},{8,9},{9,10},{10,11},{11... | collective-permute-start | bytes 811016 | tf_op jit(solution)/shard_map/ppermute | solution.py:20
  28.0 1.9 %collective-permute-start.3 = (f32[33,8,2,128]{3,2,0,1:T(2,128)S(1)}, f32[33,8,2,128]{3,2,0,1:T(2,128)S(1)}, u32[]{:S(2)}, u32[]{:S(2)}) collective-permute-start(f32[33,8,2,128]{3,2,0,1:T(2,128)S(1)} %get-tuple-element.20), channel_id=1, source_target_pairs={{1,0},{2,1},{3,2},{4,3},{5,4},{6,5},{7,6},{9,8},{10,9},{11,10},{12... | collective-permute-start | bytes 811016 | tf_op jit(solution)/shard_map/ppermute | solution.py:22
  29.9 0.1 and_convert_fusion
  30.2 1.2 %collective-permute-done.2 = f32[33,8,2,128]{3,2,0,1:T(2,128)S(1)} collective-permute-done((f32[33,8,2,128]{3,2,0,1:T(2,128)S(1)}, f32[33,8,2,128]{3,2,0,1:T(2,128)S(1)}, u32[]{:S(2)}, u32[]{:S(2)}) %collective-permute-start.2) | collective-permute-done | bytes 270368 | tf_op jit(solution)/shard_map/ppermute | solution.py:20
  31.4 4.4 %collective-permute-done.3 = f32[33,8,2,128]{3,2,0,1:T(2,128)S(1)} collective-permute-done((f32[33,8,2,128]{3,2,0,1:T(2,128)S(1)}, f32[33,8,2,128]{3,2,0,1:T(2,128)S(1)}, u32[]{:S(2)}, u32[]{:S(2)}) %collective-permute-start.3) | collective-permute-done | bytes 270368 | tf_op jit(solution)/shard_map/ppermute | solution.py:22
  35.8 0.6 %select_maximum_fusion = f32[33,8,16,128]{3,2,0,1:T(8,128)S(1)} fusion(f32[33,8,2,128]{3,2,0,1:T(2,128)S(1)} %collective-permute-done.3, f32[33,8,2,128]{3,2,0,1:T(2,128)S(1)} %collective-permute-done.2, f32[18,2,8,128]{3,2,0,1:T(8,128)S(1)} %concatenate.90, f32[33,4,8,128]{3,2,0,1:T(8,128)S(1)} %constant_dynamic-update-slice_fusion, ...), kind=kLoop, calls=%fused_computation | loop fusion | flops 7569408 | bytes 3784704 | tf_op jit(solution)/shard_map/concatenate | solution.py:18
  36.5 0.2 fusion.72
  36.6 0.1 copy.123
  36.7 0.1 fusion.73
  36.9 0.4 pad_subtract_fusion.1
  37.3 0.3 fusion.16
  37.7 0.4 fusion.25
  38.0 0.3 fusion.10
  38.5 0.2 slice.576
  38.9 0.1 pad_subtract_fusion.3
  39.1 0.1 fusion.33
  39.8 0.4 copy-done.5
  40.3 0.1 reshape.498
  40.4 0.7 %reshape.499 = f32[4,16,128]{2,1,0:T(8,128)} reshape(f32[4,2,4,8,32]{4,3,2,1,0:T(8,128)S(1)} %bitcast.262) | data formatting | bytes 65536 | tf_op jit(solution)/shard_map/reshape | solution.py:293
  41.1 4.0 %all-to-all-start = ((f32[4,16,128]{2,1,0:T(8,128)}), f32[4,16,128]{2,1,0:T(8,128)S(1)}, u32[]{:S(2)}, u32[]{:S(2)}) async-start(f32[4,16,128]{2,1,0:T(8,128)} %reshape.499), calls=%async_computation | async-start | bytes 65536 | tf_op jit(solution)/shard_map/all_to_all | solution.py:294
  45.1 0.2 fusion.41
  45.3 0.8 %fusion.27 = f32[4,3,4,8,128]{4,3,2,1,0:T(8,128)} fusion(f32[4,3,4,16,128]{4,3,2,1,0:T(8,128)S(1)} %slice.568, f32[4,1,4,16,128]{4,3,2,1,0:T(8,128)S(1)} %get-tuple-element.43, f32[4,1,4,16,128]{4,3,2,1,0:T(8,128)S(1)} %get-tuple-element.42, f32[4,1,4,16,128]{4,3,2,1,0:T(8,128)S(1)} %get-tuple-element.41, f32[4,8,128]{2,1,0:T(8,128)S(1)} %slice.607, ...), kind=kLoop, calls=%fused_computation.79 | loop fusion | flops 344064 | bytes 1067008 | tf_op jit(solution)/shard_map/add | solution.py:113
  46.1 3.3 %all-to-all-done = f32[4,16,128]{2,1,0:T(8,128)S(1)} async-done(((f32[4,16,128]{2,1,0:T(8,128)}), f32[4,16,128]{2,1,0:T(8,128)S(1)}, u32[]{:S(2)}, u32[]{:S(2)}) %all-to-all-start) | async-done | bytes 32800 | tf_op jit(solution)/shard_map/all_to_all | solution.py:294
  49.4 0.7 %reshape.500 = f32[2,4,8,32]{3,2,1,0:T(8,128)} reshape(f32[16,128]{1,0:T(8,128)S(1)} %reduce_sum.82) | data formatting | bytes 16384 | tf_op jit(solution)/shard_map/reshape | solution.py:296
  (93 shorter events, 2.0 us)
Async XLA Ops:
  0.6 2.1 %copy-start.2 = (f32[4,8,128]{2,1,0:T(8,128)S(1)}, f32[4,8,128]{2,1,0:T(8,128)}, u32[]{:S(2)}) copy-start(f32[4,8,128]{2,1,0:T(8,128)} %param.20) | copy-start | bytes 49156
  0.6 2.1 %copy-start.1 = (f32[4,8,128]{2,1,0:T(8,128)S(1)}, f32[4,8,128]{2,1,0:T(8,128)}, u32[]{:S(2)}) copy-start(f32[4,8,128]{2,1,0:T(8,128)} %param.19) | copy-start | bytes 49156
  0.7 2.1 %copy-start = (f32[4,8,128]{2,1,0:T(8,128)S(1)}, f32[4,8,128]{2,1,0:T(8,128)}, u32[]{:S(2)}) copy-start(f32[4,8,128]{2,1,0:T(8,128)} %param.18) | copy-start | bytes 49156
  1.7 7.9 %copy-start.6 = (s32[4]{0:T(128)S(1)}, s32[4]{0:T(128)}, u32[]{:S(2)}) copy-start(s32[4]{0:T(128)} %param.24) | copy-start | bytes 52
  1.7 8.0 %copy-start.7 = (s32[4]{0:T(128)S(1)}, s32[4]{0:T(128)}, u32[]{:S(2)}) copy-start(s32[4]{0:T(128)} %param.25) | copy-start | bytes 52
  1.7 8.1 %copy-start.4 = (f32[256,3]{0,1:T(4,128)S(1)}, f32[256,3]{0,1:T(4,128)}, u32[]{:S(2)}) copy-start(f32[256,3]{0,1:T(4,128)} %param.23) | copy-start | bytes 9220
  1.7 8.4 %copy-start.3 = (f32[4,256,3]{1,0,2:T(4,128)S(1)}, f32[4,256,3]{1,0,2:T(4,128)}, u32[]{:S(2)}) copy-start(f32[4,256,3]{1,0,2:T(4,128)} %param.26) | copy-start | bytes 36868
  2.8 7.7 %collective-permute-start.1 = (f32[48,8,128]{2,1,0:T(8,128)S(1)}, f32[48,8,128]{2,1,0:T(8,128)S(1)}, u32[]{:S(2)}, u32[]{:S(2)}) collective-permute-start(f32[48,8,128]{2,1,0:T(8,128)S(1)} %pad_maximum_fusion.8), channel_id=1, source_target_pairs={{8,0},{16,8},{24,16},{32,24},{40,32},{48,40},{56,48},{64,56},{72,6... | collective-permute-start | bytes 589832 | tf_op jit(solution)/shard_map/ppermute | solution.py:127
  5.2 13.5 %collective-permute-start = (f32[50,8,128]{2,1,0:T(8,128)S(1)}, f32[50,8,128]{2,1,0:T(8,128)S(1)}, u32[]{:S(2)}, u32[]{:S(2)}) collective-permute-start(f32[50,8,128]{2,1,0:T(8,128)S(1)} %pad_maximum_fusion.5), channel_id=1, source_target_pairs={{0,8},{8,16},{16,24},{24,32},{32,40},{40,48},{48,56},{56,64},{64,7... | collective-permute-start | bytes 614408 | tf_op jit(solution)/shard_map/ppermute | solution.py:124
  19.0 12.4 %collective-permute-start.2 = (f32[33,8,2,128]{3,2,0,1:T(2,128)S(1)}, f32[33,8,2,128]{3,2,0,1:T(2,128)S(1)}, u32[]{:S(2)}, u32[]{:S(2)}) collective-permute-start(f32[33,8,2,128]{3,2,0,1:T(2,128)S(1)} %get-tuple-element.19), channel_id=1, source_target_pairs={{0,1},{1,2},{2,3},{3,4},{4,5},{5,6},{6,7},{8,9},{9,10},{10,11},{11... | collective-permute-start | bytes 811016 | tf_op jit(solution)/shard_map/ppermute | solution.py:20
  28.0 7.8 %collective-permute-start.3 = (f32[33,8,2,128]{3,2,0,1:T(2,128)S(1)}, f32[33,8,2,128]{3,2,0,1:T(2,128)S(1)}, u32[]{:S(2)}, u32[]{:S(2)}) collective-permute-start(f32[33,8,2,128]{3,2,0,1:T(2,128)S(1)} %get-tuple-element.20), channel_id=1, source_target_pairs={{1,0},{2,1},{3,2},{4,3},{5,4},{6,5},{7,6},{9,8},{10,9},{11,10},{12... | collective-permute-start | bytes 811016 | tf_op jit(solution)/shard_map/ppermute | solution.py:22
  39.5 0.7 %copy-start.5 = (f32[6]{0:T(128)S(1)}, f32[6]{0:T(128)}, u32[]{:S(2)}) copy-start(f32[6]{0:T(128)} %constant.93.clone) | copy-start | bytes 76
  41.1 8.3 %all-to-all-start = ((f32[4,16,128]{2,1,0:T(8,128)}), f32[4,16,128]{2,1,0:T(8,128)S(1)}, u32[]{:S(2)}, u32[]{:S(2)}) async-start(f32[4,16,128]{2,1,0:T(8,128)} %reshape.499), calls=%async_computation | async-start | bytes 65536 | tf_op jit(solution)/shard_map/all_to_all | solution.py:294
